TPU v7x, 32 devices: a whole 2x2x4 slice. The times are simulated.
32 devices in a mesh: cell: 16 (over z, y, core), bin: 2 (over x).
Axes of the slice: x: 2, y: 2, z: 4, core: 2. Of those that a mesh axis runs over, the one named last changes fastest.
Arguments:
- tensor: float32 [96, 4096, 1024], P('cell', None, 'bin'), may hold values from -6 to 6
- cell_factor: float32 [4096, 128], P('cell'), may hold values from -4 to 4
- bin_factor: float32 [1024, 128], P('bin'), may hold values from -4 to 4
Outputs:
- updated: float32 [96, 128], P('cell', 'bin')
All inputs are finite; a program needn't handle non-finite values.
Results may differ from a plain program's by a relative error of at most 0.000096.
Values sent between devices are 32-bit elements; how exact they have to be, the bound alone decides.
No kernel may reach another device: no remote copies, remote signals or barrier semaphores. Data moves between devices by JAX's collectives and lax.ppermute only.
A program may use at most 128 MiB of HBM per device.

v0:
```python
import jax
import jax.numpy as jnp
from jax import lax
from jax.sharding import PartitionSpec as P


def body(tensor, cell_factor, bin_factor):
    highest = lax.Precision.HIGHEST
    image_rows, cell_count, bin_count = tensor.shape
    rank_cols = bin_factor.shape[1]
    projected = jnp.dot(
        tensor.reshape(image_rows * cell_count, bin_count), bin_factor, precision=highest
    )
    projected = projected.reshape(image_rows, cell_count, rank_cols)
    bin_local = jnp.dot(bin_factor.T, bin_factor, precision=highest)
    gram_bin = lax.psum(bin_local, "bin")
    mttkrp = jnp.sum(
        projected * lax.all_gather(cell_factor, "cell", axis=0, tiled=True)[None, :, :], axis=1
    )
    cell_local = jnp.dot(cell_factor.T, cell_factor, precision=highest)
    gram_cell = lax.psum(cell_local, "cell")
    gram = gram_cell * gram_bin
    chol_lower = jnp.linalg.cholesky(gram)
    totals = lax.psum(mttkrp, "bin")
    solved = jax.scipy.linalg.cho_solve((chol_lower, True), totals.T).T
    own_cols = rank_cols // lax.axis_size("bin")
    updated = lax.dynamic_slice_in_dim(solved, lax.axis_index("bin") * own_cols, own_cols, 1)
    return updated


def solution(mesh):
    placed = (P("cell", None, "bin"), P("cell", None), P("bin", None))
    return jax.shard_map(
        body, mesh=mesh, in_specs=placed, out_specs=P("cell", "bin"), check_vma=False
    )
```

profile of v0, /device:TPU:0, one launch (start us, length us, event | category | flops | bytes accessed | tf_op | source)
XLA Modules:
  0.0 223.3 jit_solution(393272512199881900)
XLA Ops:
  6.5 0.0 copy-start
  6.5 0.0 all-reduce.3.cloned.1.call-start
  6.5 2.0 fusion.7
  8.6 0.0 all-reduce.3.cloned.1.call-update
  8.6 0.0 all-reduce.5.cloned.1.call-start
  8.6 0.0 copy-done
  8.6 1.2 fusion.8
  9.8 0.0 all-reduce.5.cloned.1.call-update
  9.9 0.0 all-gather.2.cloned.1.call-start
  9.9 0.7 all-gather.2.cloned.1.call-update
  10.6 87.4 %all-reduce.3.cloned.1.call-done = f32[128,128]{0,1:T(8,128)} async-done(((f32[128,128]{0,1:T(8,128)}), f32[128,128]{0,1:T(8,128)}) %all-reduce.3.cloned.1.call-update) | async-done | bytes 65552 | tf_op jit(solution)/shard_map/psum | solution.py:21
  98.0 24.7 %all-reduce.5.cloned.1.call-done = f32[128,128]{0,1:T(8,128)} async-done(((f32[128,128]{0,1:T(8,128)}), f32[128,128]{0,1:T(8,128)}) %all-reduce.5.cloned.1.call-update) | async-done | bytes 65552 | tf_op jit(solution)/shard_map/psum | solution.py:16
  122.7 0.9 mul.14
  123.6 0.1 copy.9
  123.7 11.7 %cholesky.16 = f32[128,128]{1,0:T(8,128)S(1)} custom-call(f32[128,128]{1,0:T(8,128)S(1)} %fusion.6), custom_call_target="Cholesky" | custom-call | tf_op jit(solution)/shard_map/jit(cholesky)/cholesky | solution.py:23
  135.5 0.6 compare_reduce_fusion
  136.1 0.7 fusion.1
  136.8 9.8 %custom-call.10 = f32[1,128,128]{1,2,0:T(8,128)S(1)} custom-call(f32[1,128,128]{2,1,0:T(8,128)S(1)} %fusion.1), custom_call_target="InvertDiagBlocksLowerTriangular" | custom-call | tf_op jit(solution)/shard_map/jit(_cho_solve)/triangular_solve | solution.py:25
  146.6 20.2 %all-gather.2.cloned.1.call-done = f32[4096,128]{1,0:T(8,128)} async-done(((f32[256,128]{1,0:T(8,128)}), f32[4096,128]{1,0:T(8,128)}) %all-gather.2.cloned.1.call-update) | async-done | bytes 2097168 | tf_op jit(solution)/shard_map/all_gather | solution.py:18
  166.8 43.8 %multiply_reduce_fusion = f32[6,128]{1,0:T(8,128)S(1)} fusion(f32[6,4096,512]{2,1,0:T(8,128)} %param.3, f32[4096,128]{1,0:T(8,128)} %all-gather.2.cloned.1.call-done, f32[512,128]{1,0:T(8,128)S(1)} %copy-done), kind=kOutput, calls=%fused_computation | convolution fusion | flops 19333644288 | bytes 52694016 | tf_op jit(solution)/shard_map/dot_general | solution.py:11
  210.7 4.9 %psum.23 = f32[6,128]{1,0:T(8,128)S(1)} all-reduce(f32[6,128]{1,0:T(8,128)S(1)} %multiply_reduce_fusion), channel_id=1, replica_groups=mesh['cell'=16,'bin'=2] {'bin'}, use_global_device_ids=true, to_apply=%region_5.6 | all-reduce | flops 768 | bytes 6144 | tf_op jit(solution)/shard_map/psum | solution.py:24
  215.6 0.3 fusion.4
  215.9 0.2 fusion.2
  216.1 0.7 constant_dynamic-slice_fusion
  (2 shorter events, 0.0 us)
Async XLA Ops:
  6.5 2.1 copy-start
  6.5 91.5 %all-reduce.3.cloned.1.call-start = ((), (), s32[]{:S(2)}) async-start(), calls=%async_computation | async-start | bytes 131072 | tf_op jit(solution)/shard_map/psum | solution.py:21
  8.6 114.1 %all-reduce.5.cloned.1.call-start = ((), (), s32[]{:S(2)}) async-start(), calls=%async_computation.1 | async-start | bytes 131072 | tf_op jit(solution)/shard_map/psum | solution.py:16
  9.9 156.9 %all-gather.2.cloned.1.call-start = ((), (), s32[]{:S(2)}) async-start(), calls=%async_computation.2 | async-start | bytes 2228224 | tf_op jit(solution)/shard_map/all_gather | solution.py:18
Sparse Core Ops, SparseCore 0:
  10.8 87.1 all-reduce.2
  100.3 22.3 all-reduce.4
  125.1 41.6 all-gather.1
where the time goes:
time: 224 us; the launch traced here: 223 us
  waiting for transfers between devices  133 us (59%)
  matrix products  47.5 us (21%)
  other arithmetic  23.8 us (11%)
  between operations  13.2 us (6%)
  blocking collectives  4.95 us (2%)
    psum x1, waiting for transfers between devices, body(): gram_cell = lax.psum(cell_local, 'cell')  87.4 us
    dot_general x1, matrix products, body(): jnp.dot(tensor.reshape(image_rows * cell_count, bin_count), bin_factor, p...  43.8 us
    psum x1, waiting for transfers between devices, body(): gram_bin = lax.psum(bin_local, 'bin')  24.7 us
    all_gather x1, waiting for transfers between devices, body(): lax.all_gather(cell_factor, 'cell', axis=0, tiled=True)[None, :, :]  20.2 us
    another operation x3, other arithmetic, body(): chol_lower = jnp.linalg.cholesky(gram)  12.4 us
    another operation x2, other arithmetic, body(): solved = jax.scipy.linalg.cho_solve((chol_lower, True), totals.T).T  10.5 us
    psum x1, blocking collectives, body(): totals = lax.psum(mttkrp, 'bin')  4.95 us
  transfers between devices with their start and end apart: 3, of which 3 were waited for; matrix products, arithmetic and copies ran while one was open for 11% of the time, Pallas kernels for 0%

commit v1 on v0

v1 whole, which is shorter than its diff:
```python
import jax
import jax.numpy as jnp
from jax import lax
from jax.sharding import PartitionSpec as P


def exchange_sum(value, axis):
    size = lax.axis_size(axis)
    stride = 1
    while stride < size:
        pairs = [(i, i ^ stride) for i in range(size)]
        value = value + lax.ppermute(value, axis, pairs)
        stride *= 2
    return value


def body(tensor, cell_factor, bin_factor):
    highest = lax.Precision.HIGHEST
    image_rows, cell_count, bin_count = tensor.shape
    rank_cols = bin_factor.shape[1]
    cell_full = lax.all_gather(cell_factor, "cell", axis=0, tiled=True)
    gram_bin = exchange_sum(jnp.dot(bin_factor.T, bin_factor, precision=highest), "bin")
    projected = jnp.dot(
        tensor.reshape(image_rows * cell_count, bin_count), bin_factor, precision=highest
    )
    projected = projected.reshape(image_rows, cell_count, rank_cols)
    mttkrp = jnp.sum(projected * cell_full[None, :, :], axis=1)
    gram_cell = jnp.dot(cell_full.T, cell_full, precision=highest)
    gram = gram_cell * gram_bin
    chol_lower = jnp.linalg.cholesky(gram)
    totals = exchange_sum(mttkrp, "bin")
    solved = jax.scipy.linalg.cho_solve((chol_lower, True), totals.T).T
    own_cols = rank_cols // lax.axis_size("bin")
    updated = lax.dynamic_slice_in_dim(solved, lax.axis_index("bin") * own_cols, own_cols, 1)
    return updated


def solution(mesh):
    placed = (P("cell", None, "bin"), P("cell", None), P("bin", None))
    return jax.shard_map(
        body, mesh=mesh, in_specs=placed, out_specs=P("cell", "bin"), check_vma=False
    )
```

time: 224 us -> 136 us (0.61)
  waiting for transfers between devices: 133 us -> 43.3 us
  blocking collectives: 4.95 us -> 0 us
  starting transfers between devices: 0.09 us -> 4.54 us
  matrix products: 47.5 us -> 50.4 us
    psum x2 -> x0, waiting for transfers between devices: 112 us -> none  [the longest x1 87.4 us: body(): gram_cell = lax.psum(cell_local, 'cell')]
    all_gather x1, waiting for transfers between devices: 20.2 us -> 40.3 us  [body(): cell_full = lax.all_gather(cell_factor, 'cell', axis=0, tiled=True)]
    psum x1 -> x0, blocking collectives: 4.95 us -> none  [body(): totals = lax.psum(mttkrp, 'bin')]
    ppermute x0 -> x2, starting transfers between devices: none -> 4.54 us  [exchange_sum(): value = value + lax.ppermute(value, axis, pairs)]
    dot_general x2, matrix products: 3.22 us -> 6.42 us  [the longest x1 5.83 us: body(): gram_cell = jnp.dot(cell_full.T, cell_full, precision=highest)]
    ppermute x0 -> x2, waiting for transfers between devices: none -> 2.25 us  [exchange_sum(): value = value + lax.ppermute(value, axis, pairs)]
  transfers between devices with their start and end apart: 3 -> 3, of which waited for: 3 -> 2; matrix products, arithmetic and copies ran while one was open for 11% -> 8% of each run, Pallas kernels for 0% -> 0%
where the time goes in v1:
time: 136 us
  matrix products  50.4 us (37%)
  waiting for transfers between devices  43.3 us (32%)
  other arithmetic  22.9 us (17%)
  between operations  13.5 us (10%)
  starting transfers between devices  4.54 us (3%)
    dot_general x1, matrix products, body(): jnp.dot(tensor.reshape(image_rows * cell_count, bin_count), bin_factor, p...  43.5 us
    all_gather x1, waiting for transfers between devices, body(): cell_full = lax.all_gather(cell_factor, 'cell', axis=0, tiled=True)  40.3 us
    another operation x3, other arithmetic, body(): chol_lower = jnp.linalg.cholesky(gram)  12.4 us
    another operation x2, other arithmetic, body(): solved = jax.scipy.linalg.cho_solve((chol_lower, True), totals.T).T  10.5 us
    dot_general x1, matrix products, body(): gram_cell = jnp.dot(cell_full.T, cell_full, precision=highest)  5.83 us
    ppermute x2, starting transfers between devices, exchange_sum(): value = value + lax.ppermute(value, axis, pairs)  4.54 us
  transfers between devices with their start and end apart: 3, of which 2 were waited for; matrix products, arithmetic and copies ran while one was open for 8% of the time, Pallas kernels for 0%

profile of v1, /device:TPU:0, one launch (start us, length us, event | category | flops | bytes accessed | tf_op | source)
XLA Modules:
  0.0 135.6 jit_solution(293633196473035220)
XLA Ops:
  6.5 0.0 copy-start
  6.5 0.0 all-gather.2.cloned.1.call-start
  6.5 0.7 all-gather.2.cloned.1.call-update
  7.3 0.2 copy-done
  7.5 0.6 fusion.8
  8.1 3.0 %collective-permute-start = (f32[128,128]{0,1:T(8,128)S(1)}, f32[128,128]{0,1:T(8,128)S(1)}, u32[]{:S(2)}, u32[]{:S(2)}) collective-permute-start(f32[128,128]{0,1:T(8,128)S(1)} %fusion.8), channel_id=1, source_target_pairs={{0,1},{1,0},{2,3},{3,2},{4,5},{5,4},{6,7},{7,6},{8,9},{9,8},{10,11... | collective-permute-start | bytes 196616 | tf_op jit(solution)/shard_map/ppermute | solution.py:12
  11.1 2.2 %collective-permute-done = f32[128,128]{0,1:T(8,128)S(1)} collective-permute-done((f32[128,128]{0,1:T(8,128)S(1)}, f32[128,128]{0,1:T(8,128)S(1)}, u32[]{:S(2)}, u32[]{:S(2)}) %collective-permute-start) | collective-permute-done | bytes 65568 | tf_op jit(solution)/shard_map/ppermute | solution.py:12
  13.3 40.3 %all-gather.2.cloned.1.call-done = f32[4096,128]{1,0:T(8,128)} async-done(((f32[256,128]{1,0:T(8,128)}), f32[4096,128]{1,0:T(8,128)}) %all-gather.2.cloned.1.call-update) | async-done | bytes 2097168 | tf_op jit(solution)/shard_map/all_gather | solution.py:21
  53.7 0.0 copy-start.1
  53.7 5.8 %add_multiply_fusion = f32[128,128]{0,1:T(8,128)S(1)} fusion(f32[128,128]{0,1:T(8,128)S(1)} %fusion.8, f32[128,128]{0,1:T(8,128)S(1)} %collective-permute-done, f32[4096,128]{1,0:T(8,128)} %all-gather.2.cloned.1.call-done), kind=kOutput, calls=%fused_computation.11 | convolution fusion | flops 805339136 | bytes 2293760 | tf_op jit(solution)/shard_map/dot_general | solution.py:28
  59.5 0.1 copy.7
  59.6 11.7 %cholesky.16 = f32[128,128]{1,0:T(8,128)S(1)} custom-call(f32[128,128]{1,0:T(8,128)S(1)} %fusion.6), custom_call_target="Cholesky" | custom-call | tf_op jit(solution)/shard_map/jit(cholesky)/cholesky | solution.py:30
  71.4 0.6 compare_reduce_fusion
  72.0 0.0 copy-done.1
  72.0 43.5 %multiply_reduce_fusion = f32[6,128]{1,0:T(8,128)S(1)} fusion(f32[6,4096,512]{2,1,0:T(8,128)} %param.3, f32[4096,128]{1,0:T(8,128)S(1)} %copy-done.1, f32[512,128]{1,0:T(8,128)S(1)} %copy-done), kind=kOutput, calls=%fused_computation | convolution fusion | flops 19333644288 | bytes 52694016 | tf_op jit(solution)/shard_map/dot_general | solution.py:23
  115.5 1.5 %collective-permute-start.1 = (f32[6,128]{1,0:T(8,128)S(1)}, f32[6,128]{1,0:T(8,128)S(1)}, u32[]{:S(2)}, u32[]{:S(2)}) collective-permute-start(f32[6,128]{1,0:T(8,128)S(1)} %multiply_reduce_fusion), channel_id=1, source_target_pairs={{0,1},{1,0},{2,3},{3,2},{4,5},{5,4},{6,7},{7,6},{8,9},{9,8},{10,11... | collective-permute-start | bytes 9224 | tf_op jit(solution)/shard_map/ppermute | solution.py:12
  117.1 0.7 fusion.1
  117.7 9.8 %custom-call.10 = f32[1,128,128]{1,2,0:T(8,128)S(1)} custom-call(f32[1,128,128]{2,1,0:T(8,128)S(1)} %fusion.1), custom_call_target="InvertDiagBlocksLowerTriangular" | custom-call | tf_op jit(solution)/shard_map/jit(_cho_solve)/triangular_solve | solution.py:32
  127.5 0.0 collective-permute-done.1
  127.5 0.3 fusion.4
  127.8 0.2 fusion.2
  128.0 0.7 constant_dynamic-slice_fusion
  (2 shorter events, 0.0 us)
Async XLA Ops:
  6.5 1.0 copy-start
  6.5 47.1 %all-gather.2.cloned.1.call-start = ((), (), s32[]{:S(2)}) async-start(), calls=%async_computation | async-start | bytes 2228224 | tf_op jit(solution)/shard_map/all_gather | solution.py:21
  8.1 5.2 %collective-permute-start = (f32[128,128]{0,1:T(8,128)S(1)}, f32[128,128]{0,1:T(8,128)S(1)}, u32[]{:S(2)}, u32[]{:S(2)}) collective-permute-start(f32[128,128]{0,1:T(8,128)S(1)} %fusion.8), channel_id=1, source_target_pairs={{0,1},{1,0},{2,3},{3,2},{4,5},{5,4},{6,7},{7,6},{8,9},{9,8},{10,11... | collective-permute-start | bytes 196616 | tf_op jit(solution)/shard_map/ppermute | solution.py:12
  53.7 18.3 %copy-start.1 = (f32[4096,128]{1,0:T(8,128)S(1)}, f32[4096,128]{1,0:T(8,128)}, u32[]{:S(2)}) copy-start(f32[4096,128]{1,0:T(8,128)} %all-gather.2.cloned.1.call-done) | copy-start | bytes 6291460
  115.5 12.0 %collective-permute-start.1 = (f32[6,128]{1,0:T(8,128)S(1)}, f32[6,128]{1,0:T(8,128)S(1)}, u32[]{:S(2)}, u32[]{:S(2)}) collective-permute-start(f32[6,128]{1,0:T(8,128)S(1)} %multiply_reduce_fusion), channel_id=1, source_target_pairs={{0,1},{1,0},{2,3},{3,2},{4,5},{5,4},{6,7},{7,6},{8,9},{9,8},{10,11... | collective-permute-start | bytes 9224 | tf_op jit(solution)/shard_map/ppermute | solution.py:12
Sparse Core Ops, SparseCore 0:
  9.5 44.0 all-gather.1

commit v2 on v1

--- a/solution.py
+++ b/solution.py
@@ -1,6 +1,8 @@
 import jax
 import jax.numpy as jnp
 from jax import lax
+from jax.experimental import pallas as pl
+from jax.experimental.pallas import tpu as pltpu
 from jax.sharding import PartitionSpec as P
 
 
@@ -14,19 +16,63 @@
     return value
 
 
+def split_pair(x):
+    scaled = x * 65537.0
+    hi = scaled - (scaled - x)
+    lo = x - hi
+    return hi.astype(jnp.bfloat16), lo.astype(jnp.bfloat16)
+
+
+def gram_of(x):
+    hi, lo = split_pair(x)
+    both = jnp.concatenate([hi, lo], axis=1)
+    full = lax.dot_general(
+        both, both, (((0,), (0,)), ((), ())), preferred_element_type=jnp.float32
+    )
+    n = x.shape[1]
+    return (full[:n, :n] + full[n:, n:]) + (full[:n, n:] + full[n:, :n])
+
+
+def project_kernel(t_ref, b_ref, o_ref):
+    rank_cols = o_ref.shape[1]
+    hi, lo = split_pair(t_ref[...])
+    pair = b_ref[...]
+    acc = jnp.dot(hi, pair, preferred_element_type=jnp.float32)
+    acc = acc + jnp.dot(lo, pair, preferred_element_type=jnp.float32)
+    o_ref[...] = acc[:, :rank_cols] + acc[:, rank_cols:]
+
+
+def project(flat, bin_factor, block_rows=1024):
+    rows, bin_count = flat.shape
+    rank_cols = bin_factor.shape[1]
+    b_hi, b_lo = split_pair(bin_factor)
+    pair = jnp.concatenate([b_hi, b_lo], axis=1)
+    return pl.pallas_call(
+        project_kernel,
+        out_shape=jax.ShapeDtypeStruct((rows, rank_cols), jnp.float32),
+        grid=(rows // block_rows,),
+        in_specs=[
+            pl.BlockSpec((block_rows, bin_count), lambda i: (i, 0)),
+            pl.BlockSpec((bin_count, 2 * rank_cols), lambda i: (0, 0)),
+        ],
+        out_specs=pl.BlockSpec((block_rows, rank_cols), lambda i: (i, 0)),
+        cost_estimate=pl.CostEstimate(
+            flops=8 * rows * bin_count * rank_cols,
+            transcendentals=0,
+            bytes_accessed=4 * rows * (bin_count + rank_cols),
+        ),
+    )(flat, pair)
+
+
 def body(tensor, cell_factor, bin_factor):
-    highest = lax.Precision.HIGHEST
     image_rows, cell_count, bin_count = tensor.shape
     rank_cols = bin_factor.shape[1]
     cell_full = lax.all_gather(cell_factor, "cell", axis=0, tiled=True)
-    gram_bin = exchange_sum(jnp.dot(bin_factor.T, bin_factor, precision=highest), "bin")
-    projected = jnp.dot(
-        tensor.reshape(image_rows * cell_count, bin_count), bin_factor, precision=highest
-    )
+    gram_bin = exchange_sum(gram_of(bin_factor), "bin")
+    projected = project(tensor.reshape(image_rows * cell_count, bin_count), bin_factor)
     projected = projected.reshape(image_rows, cell_count, rank_cols)
     mttkrp = jnp.sum(projected * cell_full[None, :, :], axis=1)
-    gram_cell = jnp.dot(cell_full.T, cell_full, precision=highest)
-    gram = gram_cell * gram_bin
+    gram = gram_of(cell_full) * gram_bin
     chol_lower = jnp.linalg.cholesky(gram)
     totals = exchange_sum(mttkrp, "bin")
     solved = jax.scipy.linalg.cho_solve((chol_lower, True), totals.T).T

time: 136 us -> 95.3 us (0.70)
  matrix products: 50.4 us -> 1.71 us
  waiting for transfers between devices: 43.3 us -> 8.66 us
  Pallas kernels: 0 us -> 33.4 us
  other arithmetic: 22.9 us -> 32.1 us
    dot_general x3 -> x2, matrix products: 49.9 us -> 1.22 us  [gram_of(): lax.dot_general(both, both, (((0,), (0,)), ((), ())), preferred_element_t...]
    pallas_call x0 -> x1, Pallas kernels: none -> 33.4 us  [project(): pl.pallas_call(project_kernel, out_shape=jax.ShapeDtypeStruct((rows, rank...]
    all_gather x1, waiting for transfers between devices: 40.3 us -> 7.95 us  [body(): cell_full = lax.all_gather(cell_factor, 'cell', axis=0, tiled=True)]
    reduce_sum x0 -> x1, other arithmetic: none -> 5.4 us  [body(): mttkrp = jnp.sum(projected * cell_full[None, :, :], axis=1)]
    convert_element_type x0 -> x2, other arithmetic: none -> 3.01 us  [split_pair(): return (hi.astype(jnp.bfloat16), lo.astype(jnp.bfloat16))]
    ppermute x2, waiting for transfers between devices: 2.25 us -> 0.01 us  [exchange_sum(): value = value + lax.ppermute(value, axis, pairs)]
  transfers between devices with their start and end apart: 3 -> 3, of which waited for: 2 -> 1; matrix products, arithmetic and copies ran while one was open for 8% -> 16% of each run, Pallas kernels for 0% -> 35%
where the time goes in v2:
time: 95.3 us; the launch traced here: 94.7 us
  Pallas kernels  33.4 us (35%)
  other arithmetic  32.1 us (34%)
  between operations  13.5 us (14%)
  waiting for transfers between devices  8.66 us (9%)
  starting transfers between devices  4.54 us (5%)
  matrix products  1.71 us (2%)
    pallas_call x1, Pallas kernels, project(): pl.pallas_call(project_kernel, out_shape=jax.ShapeDtypeStruct((rows, rank...  33.4 us
    another operation x3, other arithmetic, body(): chol_lower = jnp.linalg.cholesky(gram)  12.4 us
    another operation x2, other arithmetic, body(): solved = jax.scipy.linalg.cho_solve((chol_lower, True), totals.T).T  10.5 us
    all_gather x1, waiting for transfers between devices, body(): cell_full = lax.all_gather(cell_factor, 'cell', axis=0, tiled=True)  7.95 us
    reduce_sum x1, other arithmetic, body(): mttkrp = jnp.sum(projected * cell_full[None, :, :], axis=1)  5.4 us
    ppermute x2, starting transfers between devices, exchange_sum(): value = value + lax.ppermute(value, axis, pairs)  4.54 us
    convert_element_type x2, other arithmetic, split_pair(): return (hi.astype(jnp.bfloat16), lo.astype(jnp.bfloat16))  3.01 us
  transfers between devices with their start and end apart: 3, of which 1 were waited for; matrix products, arithmetic and copies ran while one was open for 16% of the time, Pallas kernels for 35%

profile of v2, /device:TPU:0, one launch (start us, length us, event | category | flops | bytes accessed | tf_op | source)
XLA Modules:
  0.0 94.7 jit_solution(3995725228430654641)
XLA Ops:
  6.5 0.0 all-gather.2.cloned.1.call-start
  6.5 0.7 all-gather.2.cloned.1.call-update
  7.3 1.0 %fusion.8 = (bf16[512,128]{1,0:T(8,128)(2,1)S(1)}, bf16[512,128]{1,0:T(8,128)(2,1)S(1)}) fusion(f32[512,128]{1,0:T(8,128)} %param.5), kind=kLoop, calls=%fused_computation.11 | loop fusion | flops 393216 | bytes 524288 | tf_op jit(solution)/shard_map/convert_element_type | solution.py:23
  8.3 0.3 fusion.21
  8.6 3.0 %collective-permute-start = (f32[128,128]{0,1:T(8,128)S(1)}, f32[128,128]{0,1:T(8,128)S(1)}, u32[]{:S(2)}, u32[]{:S(2)}) collective-permute-start(f32[128,128]{0,1:T(8,128)S(1)} %fusion.11), channel_id=1, source_target_pairs={{0,1},{1,0},{2,3},{3,2},{4,5},{5,4},{6,7},{7,6},{8,9},{9,8},{10,11... | collective-permute-start | bytes 196616 | tf_op jit(solution)/shard_map/ppermute | solution.py:14
  11.6 0.7 pad_maximum_fusion.b_ref
  12.3 33.4 %shard_map.37 = f32[24576,128]{1,0:T(8,128)} custom-call(f32[24576,512]{1,0:T(8,128)} %bitcast.14, bf16[512,256]{1,0:T(8,128)(2,1)} %pad_maximum_fusion.b_ref), custom_call_target="tpu_custom_call" | custom-call | flops 12884901888 | bytes 62914560 | tf_op jit(solution)/shard_map/pallas_call | solution.py:50
  45.7 7.9 %all-gather.2.cloned.1.call-done = f32[4096,128]{1,0:T(8,128)} async-done(((f32[256,128]{1,0:T(8,128)}), f32[4096,128]{1,0:T(8,128)}) %all-gather.2.cloned.1.call-update) | async-done | bytes 2097168 | tf_op jit(solution)/shard_map/all_gather | solution.py:70
  53.7 2.0 %fusion.1 = (bf16[4096,128]{1,0:T(8,128)(2,1)S(1)}, bf16[4096,128]{1,0:T(8,128)(2,1)S(1)}) fusion(f32[4096,128]{1,0:T(8,128)} %all-gather.2.cloned.1.call-done), kind=kLoop, calls=%fused_computation.3 | loop fusion | flops 3145728 | bytes 4194304 | tf_op jit(solution)/shard_map/convert_element_type | solution.py:23
  55.7 0.0 copy-start
  55.7 0.9 fusion.3
  56.6 0.0 collective-permute-done
  56.6 0.1 fusion.13
  56.7 0.1 copy.12
  56.8 11.7 %cholesky.16 = f32[128,128]{1,0:T(8,128)S(1)} custom-call(f32[128,128]{1,0:T(8,128)S(1)} %fusion.18), custom_call_target="Cholesky" | custom-call | tf_op jit(solution)/shard_map/jit(cholesky)/cholesky | solution.py:76
  68.5 0.6 compare_reduce_fusion
  69.2 0.0 copy-done
  69.2 5.4 %multiply_reduce_fusion = f32[6,128]{1,0:T(8,128)S(1)} fusion(f32[6,4096,128]{2,1,0:T(8,128)} %bitcast.15, f32[4096,128]{1,0:T(8,128)S(1)} %copy-done), kind=kLoop, calls=%fused_computation | loop fusion | flops 6290688 | bytes 14683136 | tf_op jit(solution)/shard_map/reduce_sum | solution.py:74
  74.6 1.5 %collective-permute-start.1 = (f32[6,128]{1,0:T(8,128)S(1)}, f32[6,128]{1,0:T(8,128)S(1)}, u32[]{:S(2)}, u32[]{:S(2)}) collective-permute-start(f32[6,128]{1,0:T(8,128)S(1)} %multiply_reduce_fusion), channel_id=1, source_target_pairs={{0,1},{1,0},{2,3},{3,2},{4,5},{5,4},{6,7},{7,6},{8,9},{9,8},{10,11... | collective-permute-start | bytes 9224 | tf_op jit(solution)/shard_map/ppermute | solution.py:14
  76.1 0.7 fusion.10
  76.8 9.8 %custom-call.10 = f32[1,128,128]{1,2,0:T(8,128)S(1)} custom-call(f32[1,128,128]{2,1,0:T(8,128)S(1)} %fusion.10), custom_call_target="InvertDiagBlocksLowerTriangular" | custom-call | tf_op jit(solution)/shard_map/jit(_cho_solve)/triangular_solve | solution.py:78
  86.6 0.0 collective-permute-done.1
  86.6 0.3 fusion.16
  86.9 0.2 fusion.14
  87.1 0.7 constant_dynamic-slice_fusion
  (3 shorter events, 0.1 us)
Async XLA Ops:
  6.5 47.1 %all-gather.2.cloned.1.call-start = ((), (), s32[]{:S(2)}) async-start(), calls=%async_computation | async-start | bytes 2228224 | tf_op jit(solution)/shard_map/all_gather | solution.py:70
  8.6 48.1 %collective-permute-start = (f32[128,128]{0,1:T(8,128)S(1)}, f32[128,128]{0,1:T(8,128)S(1)}, u32[]{:S(2)}, u32[]{:S(2)}) collective-permute-start(f32[128,128]{0,1:T(8,128)S(1)} %fusion.11), channel_id=1, source_target_pairs={{0,1},{1,0},{2,3},{3,2},{4,5},{5,4},{6,7},{7,6},{8,9},{9,8},{10,11... | collective-permute-start | bytes 196616 | tf_op jit(solution)/shard_map/ppermute | solution.py:14
  55.7 13.5 %copy-start = (f32[4096,128]{1,0:T(8,128)S(1)}, f32[4096,128]{1,0:T(8,128)}, u32[]{:S(2)}) copy-start(f32[4096,128]{1,0:T(8,128)} %all-gather.2.cloned.1.call-done) | copy-start | bytes 6291460
  74.6 12.0 %collective-permute-start.1 = (f32[6,128]{1,0:T(8,128)S(1)}, f32[6,128]{1,0:T(8,128)S(1)}, u32[]{:S(2)}, u32[]{:S(2)}) collective-permute-start(f32[6,128]{1,0:T(8,128)S(1)} %multiply_reduce_fusion), channel_id=1, source_target_pairs={{0,1},{1,0},{2,3},{3,2},{4,5},{5,4},{6,7},{7,6},{8,9},{9,8},{10,11... | collective-permute-start | bytes 9224 | tf_op jit(solution)/shard_map/ppermute | solution.py:14
Sparse Core Ops, SparseCore 0:
  9.5 44.0 all-gather.1

commit v3 on v2

--- a/solution.py
+++ b/solution.py
@@ -67,7 +67,9 @@
 def body(tensor, cell_factor, bin_factor):
     image_rows, cell_count, bin_count = tensor.shape
     rank_cols = bin_factor.shape[1]
-    cell_full = lax.all_gather(cell_factor, "cell", axis=0, tiled=True)
+    cell_size = lax.axis_size("cell")
+    spread = jnp.broadcast_to(cell_factor[None], (cell_size,) + cell_factor.shape)
+    cell_full = lax.all_to_all(spread, "cell", 0, 0, tiled=True).reshape(-1, rank_cols)
     gram_bin = exchange_sum(gram_of(bin_factor), "bin")
     projected = project(tensor.reshape(image_rows * cell_count, bin_count), bin_factor)
     projected = projected.reshape(image_rows, cell_count, rank_cols)

time: 95.3 us -> 89.7 us (0.941)
  the two profiles are of different devices: /device:TPU:0 before, /device:TPU:16 now
where the time goes in v3:
time: 89.7 us; the launch traced here: 89 us
  Pallas kernels  33.4 us (37%)
  other arithmetic  29.5 us (33%)
  waiting for transfers between devices  11.6 us (13%)
  starting transfers between devices  9.43 us (11%)
  local copies, waits for them, and re-layouts  3.27 us (4%)
  matrix products  1.71 us (2%)
    pallas_call x1, Pallas kernels, project(): pl.pallas_call(project_kernel, out_shape=jax.ShapeDtypeStruct((rows, rank...  33.4 us
    another operation x3, other arithmetic, body(): chol_lower = jnp.linalg.cholesky(gram)  12.4 us
    all_to_all x1, waiting for transfers between devices, body(): lax.all_to_all(spread, 'cell', 0, 0, tiled=True).reshape(-1, rank_cols)  11.6 us
    another operation x2, other arithmetic, body(): solved = jax.scipy.linalg.cho_solve((chol_lower, True), totals.T).T  10.5 us
    all_to_all x1, starting transfers between devices, body(): lax.all_to_all(spread, 'cell', 0, 0, tiled=True).reshape(-1, rank_cols)  6.32 us
    reduce_sum x1, other arithmetic, body(): mttkrp = jnp.sum(projected * cell_full[None, :, :], axis=1)  5.39 us
    ppermute x2, starting transfers between devices, exchange_sum(): value = value + lax.ppermute(value, axis, pairs)  3.11 us
    broadcast_in_dim x1, local copies, waits for them, and re-layouts, body(): jnp.broadcast_to(cell_factor[None], (cell_size,) + cell_factor.shape)  2.47 us
  transfers between devices with their start and end apart: 3, of which 1 were waited for; matrix products, arithmetic and copies ran while one was open for 15% of the time, Pallas kernels for 38%

profile of v3, /device:TPU:16, one launch (start us, length us, event | category | flops | bytes accessed | tf_op | source)
XLA Modules:
  0.0 89.0 jit_solution(10967077481100745701)
XLA Ops:
  0.0 2.5 %broadcast_in_dim.3 = f32[16,256,128]{2,1,0:T(8,128)} broadcast(f32[256,128]{1,0:T(8,128)} %param.4), dimensions={1,2} | broadcast | bytes 2228224 | tf_op jit(solution)/shard_map/broadcast_in_dim | solution.py:71
  2.5 0.0 copy-start
  2.5 6.3 %all-to-all-start = ((f32[16,256,128]{2,1,0:T(8,128)}), f32[16,256,128]{2,1,0:T(8,128)S(1)}, u32[]{:S(2)}, u32[]{:S(2)}) async-start(f32[16,256,128]{2,1,0:T(8,128)} %broadcast_in_dim.3), calls=%async_computation | async-start | bytes 4194304 | tf_op jit(solution)/shard_map/all_to_all | solution.py:72
  8.8 0.0 copy-done
  8.8 0.1 fusion.8
  8.9 0.3 fusion.21
  9.2 1.6 %collective-permute-start = (f32[128,128]{0,1:T(8,128)S(1)}, f32[128,128]{0,1:T(8,128)S(1)}, u32[]{:S(2)}, u32[]{:S(2)}) collective-permute-start(f32[128,128]{0,1:T(8,128)S(1)} %fusion.11), channel_id=1, source_target_pairs={{0,1},{1,0},{2,3},{3,2},{4,5},{5,4},{6,7},{7,6},{8,9},{9,8},{10,11... | collective-permute-start | bytes 196616 | tf_op jit(solution)/shard_map/ppermute | solution.py:14
  10.7 0.7 pad_maximum_fusion.b_ref
  11.5 33.4 %shard_map.37 = f32[24576,128]{1,0:T(8,128)} custom-call(f32[24576,512]{1,0:T(8,128)} %bitcast.17, bf16[512,256]{1,0:T(8,128)(2,1)} %pad_maximum_fusion.b_ref), custom_call_target="tpu_custom_call" | custom-call | flops 12884901888 | bytes 62914560 | tf_op jit(solution)/shard_map/pallas_call | solution.py:50
  44.8 11.6 %all-to-all-done = f32[16,256,128]{2,1,0:T(8,128)S(1)} async-done(((f32[16,256,128]{2,1,0:T(8,128)}), f32[16,256,128]{2,1,0:T(8,128)S(1)}, u32[]{:S(2)}, u32[]{:S(2)}) %all-to-all-start) | async-done | bytes 2097184 | tf_op jit(solution)/shard_map/all_to_all | solution.py:72
  56.4 0.4 fusion.1
  56.9 0.9 %fusion.3 = f32[256,256]{0,1:T(8,128)S(1)} fusion(bf16[4096,128]{1,0:T(8,128)(2,1)S(1)} %get-tuple-element.6, bf16[4096,128]{1,0:T(8,128)(2,1)S(1)} %get-tuple-element.5), kind=kOutput, calls=%fused_computation.5 | convolution fusion | flops 541065216 | bytes 2359296 | tf_op jit(solution)/shard_map/dot_general | solution.py:29
  57.8 0.0 collective-permute-done
  57.8 0.1 fusion.13
  57.9 0.1 copy.12
  58.0 11.7 %cholesky.16 = f32[128,128]{1,0:T(8,128)S(1)} custom-call(f32[128,128]{1,0:T(8,128)S(1)} %fusion.18), custom_call_target="Cholesky" | custom-call | tf_op jit(solution)/shard_map/jit(cholesky)/cholesky | solution.py:78
  69.7 0.6 compare_reduce_fusion
  70.4 5.4 %multiply_reduce_fusion = f32[6,128]{1,0:T(8,128)S(1)} fusion(f32[6,4096,128]{2,1,0:T(8,128)} %bitcast.18, f32[4096,128]{1,0:T(8,128)S(1)} %bitcast.19), kind=kLoop, calls=%fused_computation | loop fusion | flops 6290688 | bytes 14683136 | tf_op jit(solution)/shard_map/reduce_sum | solution.py:76
  75.8 1.6 %collective-permute-start.1 = (f32[6,128]{1,0:T(8,128)S(1)}, f32[6,128]{1,0:T(8,128)S(1)}, u32[]{:S(2)}, u32[]{:S(2)}) collective-permute-start(f32[6,128]{1,0:T(8,128)S(1)} %multiply_reduce_fusion), channel_id=1, source_target_pairs={{0,1},{1,0},{2,3},{3,2},{4,5},{5,4},{6,7},{7,6},{8,9},{9,8},{10,11... | collective-permute-start | bytes 9224 | tf_op jit(solution)/shard_map/ppermute | solution.py:14
  77.3 0.7 fusion.10
  78.0 9.8 %custom-call.10 = f32[1,128,128]{1,2,0:T(8,128)S(1)} custom-call(f32[1,128,128]{2,1,0:T(8,128)S(1)} %fusion.10), custom_call_target="InvertDiagBlocksLowerTriangular" | custom-call | tf_op jit(solution)/shard_map/jit(_cho_solve)/triangular_solve | solution.py:80
  87.8 0.0 collective-permute-done.1
  87.8 0.3 fusion.16
  88.1 0.2 fusion.14
  88.3 0.7 constant_dynamic-slice_fusion
  (3 shorter events, 0.1 us)
Async XLA Ops:
  2.5 6.3 %copy-start = (f32[512,128]{1,0:T(8,128)S(1)}, f32[512,128]{1,0:T(8,128)}, u32[]{:S(2)}) copy-start(f32[512,128]{1,0:T(8,128)} %param.5) | copy-start | bytes 786436
  2.5 54.0 %all-to-all-start = ((f32[16,256,128]{2,1,0:T(8,128)}), f32[16,256,128]{2,1,0:T(8,128)S(1)}, u32[]{:S(2)}, u32[]{:S(2)}) async-start(f32[16,256,128]{2,1,0:T(8,128)} %broadcast_in_dim.3), calls=%async_computation | async-start | bytes 4194304 | tf_op jit(solution)/shard_map/all_to_all | solution.py:72
  9.2 48.7 %collective-permute-start = (f32[128,128]{0,1:T(8,128)S(1)}, f32[128,128]{0,1:T(8,128)S(1)}, u32[]{:S(2)}, u32[]{:S(2)}) collective-permute-start(f32[128,128]{0,1:T(8,128)S(1)} %fusion.11), channel_id=1, source_target_pairs={{0,1},{1,0},{2,3},{3,2},{4,5},{5,4},{6,7},{7,6},{8,9},{9,8},{10,11... | collective-permute-start | bytes 196616 | tf_op jit(solution)/shard_map/ppermute | solution.py:14
  75.8 12.0 %collective-permute-start.1 = (f32[6,128]{1,0:T(8,128)S(1)}, f32[6,128]{1,0:T(8,128)S(1)}, u32[]{:S(2)}, u32[]{:S(2)}) collective-permute-start(f32[6,128]{1,0:T(8,128)S(1)} %multiply_reduce_fusion), channel_id=1, source_target_pairs={{0,1},{1,0},{2,3},{3,2},{4,5},{5,4},{6,7},{7,6},{8,9},{9,8},{10,11... | collective-permute-start | bytes 9224 | tf_op jit(solution)/shard_map/ppermute | solution.py:14

commit v4 on v3

--- a/solution.py
+++ b/solution.py
@@ -42,7 +42,7 @@
     o_ref[...] = acc[:, :rank_cols] + acc[:, rank_cols:]
 
 
-def project(flat, bin_factor, block_rows=1024):
+def project(flat, bin_factor, block_rows=4096):
     rows, bin_count = flat.shape
     rank_cols = bin_factor.shape[1]
     b_hi, b_lo = split_pair(bin_factor)

time: 89.7 us -> 89.4 us (level)
  waiting for transfers between devices: 11.6 us -> 20.7 us
  Pallas kernels: 33.4 us -> 24.3 us
    pallas_call x1, Pallas kernels: 33.4 us -> 24.3 us  [project(): pl.pallas_call(project_kernel, out_shape=jax.ShapeDtypeStruct((rows, rank...]
    all_to_all x1, waiting for transfers between devices: 11.6 us -> 20.7 us  [body(): lax.all_to_all(spread, 'cell', 0, 0, tiled=True).reshape(-1, rank_cols)]
  transfers between devices with their start and end apart: 3 -> 3, of which waited for: 1 -> 1; matrix products, arithmetic and copies ran while one was open for 15% -> 15% of each run, Pallas kernels for 38% -> 27%
where the time goes in v4:
time: 89.4 us; the launch traced here: 89 us
  other arithmetic  29.5 us (33%)
  Pallas kernels  24.3 us (27%)
  waiting for transfers between devices  20.7 us (23%)
  starting transfers between devices  9.43 us (11%)
  local copies, waits for them, and re-layouts  3.27 us (4%)
  matrix products  1.71 us (2%)
    pallas_call x1, Pallas kernels, project(): pl.pallas_call(project_kernel, out_shape=jax.ShapeDtypeStruct((rows, rank...  24.3 us
    all_to_all x1, waiting for transfers between devices, body(): lax.all_to_all(spread, 'cell', 0, 0, tiled=True).reshape(-1, rank_cols)  20.7 us
    another operation x3, other arithmetic, body(): chol_lower = jnp.linalg.cholesky(gram)  12.4 us
    another operation x2, other arithmetic, body(): solved = jax.scipy.linalg.cho_solve((chol_lower, True), totals.T).T  10.5 us
    all_to_all x1, starting transfers between devices, body(): lax.all_to_all(spread, 'cell', 0, 0, tiled=True).reshape(-1, rank_cols)  6.32 us
    reduce_sum x1, other arithmetic, body(): mttkrp = jnp.sum(projected * cell_full[None, :, :], axis=1)  5.39 us
    ppermute x2, starting transfers between devices, exchange_sum(): value = value + lax.ppermute(value, axis, pairs)  3.11 us
    broadcast_in_dim x1, local copies, waits for them, and re-layouts, body(): jnp.broadcast_to(cell_factor[None], (cell_size,) + cell_factor.shape)  2.47 us
  transfers between devices with their start and end apart: 3, of which 1 were waited for; matrix products, arithmetic and copies ran while one was open for 15% of the time, Pallas kernels for 27%

profile of v4, /device:TPU:16, one launch (start us, length us, event | category | flops | bytes accessed | tf_op | source)
XLA Modules:
  0.0 89.0 jit_solution(16281265506303045056)
XLA Ops:
  0.0 2.5 %broadcast_in_dim.3 = f32[16,256,128]{2,1,0:T(8,128)} broadcast(f32[256,128]{1,0:T(8,128)} %param.4), dimensions={1,2} | broadcast | bytes 2228224 | tf_op jit(solution)/shard_map/broadcast_in_dim | solution.py:71
  2.5 0.0 copy-start
  2.5 6.3 %all-to-all-start = ((f32[16,256,128]{2,1,0:T(8,128)}), f32[16,256,128]{2,1,0:T(8,128)S(1)}, u32[]{:S(2)}, u32[]{:S(2)}) async-start(f32[16,256,128]{2,1,0:T(8,128)} %broadcast_in_dim.3), calls=%async_computation | async-start | bytes 4194304 | tf_op jit(solution)/shard_map/all_to_all | solution.py:72
  8.8 0.0 copy-done
  8.8 0.1 fusion.8
  8.9 0.3 fusion.21
  9.2 1.6 %collective-permute-start = (f32[128,128]{0,1:T(8,128)S(1)}, f32[128,128]{0,1:T(8,128)S(1)}, u32[]{:S(2)}, u32[]{:S(2)}) collective-permute-start(f32[128,128]{0,1:T(8,128)S(1)} %fusion.11), channel_id=1, source_target_pairs={{0,1},{1,0},{2,3},{3,2},{4,5},{5,4},{6,7},{7,6},{8,9},{9,8},{10,11... | collective-permute-start | bytes 196616 | tf_op jit(solution)/shard_map/ppermute | solution.py:14
  10.7 0.7 pad_maximum_fusion.b_ref
  11.5 24.3 %shard_map.37 = f32[24576,128]{1,0:T(8,128)} custom-call(f32[24576,512]{1,0:T(8,128)} %bitcast.17, bf16[512,256]{1,0:T(8,128)(2,1)} %pad_maximum_fusion.b_ref), custom_call_target="tpu_custom_call" | custom-call | flops 12884901888 | bytes 62914560 | tf_op jit(solution)/shard_map/pallas_call | solution.py:50
  35.8 20.7 %all-to-all-done = f32[16,256,128]{2,1,0:T(8,128)S(1)} async-done(((f32[16,256,128]{2,1,0:T(8,128)}), f32[16,256,128]{2,1,0:T(8,128)S(1)}, u32[]{:S(2)}, u32[]{:S(2)}) %all-to-all-start) | async-done | bytes 2097184 | tf_op jit(solution)/shard_map/all_to_all | solution.py:72
  56.4 0.4 fusion.1
  56.9 0.9 %fusion.3 = f32[256,256]{0,1:T(8,128)S(1)} fusion(bf16[4096,128]{1,0:T(8,128)(2,1)S(1)} %get-tuple-element.6, bf16[4096,128]{1,0:T(8,128)(2,1)S(1)} %get-tuple-element.5), kind=kOutput, calls=%fused_computation.5 | convolution fusion | flops 541065216 | bytes 2359296 | tf_op jit(solution)/shard_map/dot_general | solution.py:29
  57.8 0.0 collective-permute-done
  57.8 0.1 fusion.13
  57.9 0.1 copy.12
  58.0 11.7 %cholesky.16 = f32[128,128]{1,0:T(8,128)S(1)} custom-call(f32[128,128]{1,0:T(8,128)S(1)} %fusion.18), custom_call_target="Cholesky" | custom-call | tf_op jit(solution)/shard_map/jit(cholesky)/cholesky | solution.py:78
  69.7 0.6 compare_reduce_fusion
  70.4 5.4 %multiply_reduce_fusion = f32[6,128]{1,0:T(8,128)S(1)} fusion(f32[6,4096,128]{2,1,0:T(8,128)} %bitcast.18, f32[4096,128]{1,0:T(8,128)S(1)} %bitcast.19), kind=kLoop, calls=%fused_computation | loop fusion | flops 6290688 | bytes 14683136 | tf_op jit(solution)/shard_map/reduce_sum | solution.py:76
  75.8 1.6 %collective-permute-start.1 = (f32[6,128]{1,0:T(8,128)S(1)}, f32[6,128]{1,0:T(8,128)S(1)}, u32[]{:S(2)}, u32[]{:S(2)}) collective-permute-start(f32[6,128]{1,0:T(8,128)S(1)} %multiply_reduce_fusion), channel_id=1, source_target_pairs={{0,1},{1,0},{2,3},{3,2},{4,5},{5,4},{6,7},{7,6},{8,9},{9,8},{10,11... | collective-permute-start | bytes 9224 | tf_op jit(solution)/shard_map/ppermute | solution.py:14
  77.3 0.7 fusion.10
  78.0 9.8 %custom-call.10 = f32[1,128,128]{1,2,0:T(8,128)S(1)} custom-call(f32[1,128,128]{2,1,0:T(8,128)S(1)} %fusion.10), custom_call_target="InvertDiagBlocksLowerTriangular" | custom-call | tf_op jit(solution)/shard_map/jit(_cho_solve)/triangular_solve | solution.py:80
  87.8 0.0 collective-permute-done.1
  87.8 0.3 fusion.16
  88.1 0.2 fusion.14
  88.3 0.7 constant_dynamic-slice_fusion
  (3 shorter events, 0.1 us)
Async XLA Ops:
  2.5 6.3 %copy-start = (f32[512,128]{1,0:T(8,128)S(1)}, f32[512,128]{1,0:T(8,128)}, u32[]{:S(2)}) copy-start(f32[512,128]{1,0:T(8,128)} %param.5) | copy-start | bytes 786436
  2.5 54.0 %all-to-all-start = ((f32[16,256,128]{2,1,0:T(8,128)}), f32[16,256,128]{2,1,0:T(8,128)S(1)}, u32[]{:S(2)}, u32[]{:S(2)}) async-start(f32[16,256,128]{2,1,0:T(8,128)} %broadcast_in_dim.3), calls=%async_computation | async-start | bytes 4194304 | tf_op jit(solution)/shard_map/all_to_all | solution.py:72
  9.2 48.7 %collective-permute-start = (f32[128,128]{0,1:T(8,128)S(1)}, f32[128,128]{0,1:T(8,128)S(1)}, u32[]{:S(2)}, u32[]{:S(2)}) collective-permute-start(f32[128,128]{0,1:T(8,128)S(1)} %fusion.11), channel_id=1, source_target_pairs={{0,1},{1,0},{2,3},{3,2},{4,5},{5,4},{6,7},{7,6},{8,9},{9,8},{10,11... | collective-permute-start | bytes 196616 | tf_op jit(solution)/shard_map/ppermute | solution.py:14
  75.8 12.0 %collective-permute-start.1 = (f32[6,128]{1,0:T(8,128)S(1)}, f32[6,128]{1,0:T(8,128)S(1)}, u32[]{:S(2)}, u32[]{:S(2)}) collective-permute-start(f32[6,128]{1,0:T(8,128)S(1)} %multiply_reduce_fusion), channel_id=1, source_target_pairs={{0,1},{1,0},{2,3},{3,2},{4,5},{5,4},{6,7},{7,6},{8,9},{9,8},{10,11... | collective-permute-start | bytes 9224 | tf_op jit(solution)/shard_map/ppermute | solution.py:14

commit v5 on v2

--- a/solution.py
+++ b/solution.py
@@ -3,7 +3,7 @@
 from jax import lax
 from jax.experimental import pallas as pl
 from jax.experimental.pallas import tpu as pltpu
-from jax.sharding import PartitionSpec as P
+from jax.sharding import Mesh, PartitionSpec as P
 
 
 def exchange_sum(value, axis):
@@ -42,8 +42,9 @@
     o_ref[...] = acc[:, :rank_cols] + acc[:, rank_cols:]
 
 
-def project(flat, bin_factor, block_rows=1024):
-    rows, bin_count = flat.shape
+def project(flat, bin_factor, first_row, rows, block_rows=4096):
+    bin_count = flat.shape[1]
+    start = first_row // block_rows
     rank_cols = bin_factor.shape[1]
     b_hi, b_lo = split_pair(bin_factor)
     pair = jnp.concatenate([b_hi, b_lo], axis=1)
@@ -52,7 +53,7 @@
         out_shape=jax.ShapeDtypeStruct((rows, rank_cols), jnp.float32),
         grid=(rows // block_rows,),
         in_specs=[
-            pl.BlockSpec((block_rows, bin_count), lambda i: (i, 0)),
+            pl.BlockSpec((block_rows, bin_count), lambda i: (i + start, 0)),
             pl.BlockSpec((bin_count, 2 * rank_cols), lambda i: (0, 0)),
         ],
         out_specs=pl.BlockSpec((block_rows, rank_cols), lambda i: (i, 0)),
@@ -64,12 +65,33 @@
     )(flat, pair)
 
 
+def gather_cells(cell_factor, project_first):
+    outer = lax.axis_size("cell_outer")
+    spread = jnp.broadcast_to(cell_factor[None], (outer,) + cell_factor.shape)
+    mine = lax.all_to_all(spread, "cell_outer", 0, 0, tiled=True)
+    mine, first_part = lax.optimization_barrier((mine, project_first()))
+    core_count = lax.axis_size("cell_core")
+    if core_count == 1:
+        return mine.reshape(-1, cell_factor.shape[1]), first_part
+    other = lax.ppermute(mine, "cell_core", [(0, 1), (1, 0)])
+    first = lax.axis_index("cell_core") == 0
+    pair = (jnp.where(first, mine, other), jnp.where(first, other, mine))
+    return jnp.stack(pair, axis=1).reshape(-1, cell_factor.shape[1]), first_part
+
+
 def body(tensor, cell_factor, bin_factor):
     image_rows, cell_count, bin_count = tensor.shape
     rank_cols = bin_factor.shape[1]
-    cell_full = lax.all_gather(cell_factor, "cell", axis=0, tiled=True)
+    half = image_rows // 2
+    flat = tensor.reshape(image_rows * cell_count, bin_count)
+    cell_full, first_part = gather_cells(
+        cell_factor, lambda: project(flat, bin_factor, 0, half * cell_count)
+    )
     gram_bin = exchange_sum(gram_of(bin_factor), "bin")
-    projected = project(tensor.reshape(image_rows * cell_count, bin_count), bin_factor)
+    second_part = project(
+        flat, bin_factor, half * cell_count, (image_rows - half) * cell_count
+    )
+    projected = jnp.concatenate([first_part, second_part], axis=0)
     projected = projected.reshape(image_rows, cell_count, rank_cols)
     mttkrp = jnp.sum(projected * cell_full[None, :, :], axis=1)
     gram = gram_of(cell_full) * gram_bin
@@ -82,7 +104,14 @@
 
 
 def solution(mesh):
-    placed = (P("cell", None, "bin"), P("cell", None), P("bin", None))
+    cell_size, bin_size = mesh.shape["cell"], mesh.shape["bin"]
+    core_count = 2 if cell_size % 2 == 0 else 1
+    split = Mesh(
+        mesh.devices.reshape(cell_size // core_count, core_count, bin_size),
+        ("cell_outer", "cell_core", "bin"),
+    )
+    cell = ("cell_outer", "cell_core")
+    placed = (P(cell, None, "bin"), P(cell, None), P("bin", None))
     return jax.shard_map(
-        body, mesh=mesh, in_specs=placed, out_specs=P("cell", "bin"), check_vma=False
+        body, mesh=split, in_specs=placed, out_specs=P(cell, "bin"), check_vma=False
     )

time: 95.3 us -> 83.7 us (0.88)
  between operations: 13.5 us -> 0.13 us
  waiting for transfers between devices: 8.66 us -> 0.01 us
  other arithmetic: 32.1 us -> 37 us
  starting transfers between devices: 4.54 us -> 9.43 us
  Pallas kernels: 33.4 us -> 28.8 us
  local copies, waits for them, and re-layouts: 0.8 us -> 4.08 us
  matrix products: 1.71 us -> 3.87 us
    all_gather x1 -> x0, waiting for transfers between devices: 7.95 us -> none  [body(): cell_full = lax.all_gather(cell_factor, 'cell', axis=0, tiled=True)]
    all_to_all x0 -> x1, starting transfers between devices: none -> 7.28 us  [gather_cells(): mine = lax.all_to_all(spread, 'cell_outer', 0, 0, tiled=True)]
    concatenate x1 -> x2, other arithmetic: 0.74 us -> 7.31 us  [the longest x1 6.58 us: body(): projected = jnp.concatenate([first_part, second_part], axis=0)]
    pallas_call x1 -> x2, Pallas kernels: 33.4 us -> 28.8 us  [project(): pl.pallas_call(project_kernel, out_shape=jax.ShapeDtypeStruct((rows, rank...]
    reduce_sum x1, other arithmetic: 5.4 us -> 2.41 us  [body(): mttkrp = jnp.sum(projected * cell_full[None, :, :], axis=1)]
    ppermute x2, starting transfers between devices: 4.54 us -> 2.15 us  [exchange_sum(): value = value + lax.ppermute(value, axis, pairs)]
    dot_general x2, matrix products: 1.22 us -> 3.38 us  [gram_of(): lax.dot_general(both, both, (((0,), (0,)), ((), ())), preferred_element_t...]
    broadcast_in_dim x0 -> x1, local copies, waits for them, and re-layouts: none -> 1.94 us  [gather_cells(): spread = jnp.broadcast_to(cell_factor[None], (outer,) + cell_factor.shape)]
  transfers between devices with their start and end apart: 3 -> 4, of which waited for: 1 -> 0; matrix products, arithmetic and copies ran while one was open for 16% -> 49% of each run, Pallas kernels for 35% -> 35%
where the time goes in v5:
time: 83.7 us; the launch traced here: 83.3 us
  other arithmetic  37 us (44%)
  Pallas kernels  28.8 us (34%)
  starting transfers between devices  9.43 us (11%)
  local copies, waits for them, and re-layouts  4.08 us (5%)
  matrix products  3.87 us (5%)
    pallas_call x2, Pallas kernels, project(): pl.pallas_call(project_kernel, out_shape=jax.ShapeDtypeStruct((rows, rank...  28.8 us
    another operation x3, other arithmetic, body(): chol_lower = jnp.linalg.cholesky(gram)  12.4 us
    another operation x2, other arithmetic, body(): solved = jax.scipy.linalg.cho_solve((chol_lower, True), totals.T).T  10.5 us
    all_to_all x1, starting transfers between devices, gather_cells(): mine = lax.all_to_all(spread, 'cell_outer', 0, 0, tiled=True)  7.28 us
    concatenate x1, other arithmetic, body(): projected = jnp.concatenate([first_part, second_part], axis=0)  6.58 us
    dot_general x2, matrix products, gram_of(): lax.dot_general(both, both, (((0,), (0,)), ((), ())), preferred_element_t...  3.38 us
    convert_element_type x2, other arithmetic, split_pair(): return (hi.astype(jnp.bfloat16), lo.astype(jnp.bfloat16))  2.73 us
    reduce_sum x1, other arithmetic, body(): mttkrp = jnp.sum(projected * cell_full[None, :, :], axis=1)  2.41 us
  transfers between devices with their start and end apart: 4, of which 0 were waited for; matrix products, arithmetic and copies ran while one was open for 49% of the time, Pallas kernels for 35%

profile of v5, /device:TPU:0, one launch (start us, length us, event | category | flops | bytes accessed | tf_op | source)
XLA Modules:
  0.0 83.3 jit_solution(9568627158059190920)
XLA Ops:
  0.0 1.9 %broadcast_in_dim.3 = f32[8,256,128]{2,1,0:T(8,128)} broadcast(f32[256,128]{1,0:T(8,128)} %param.4), dimensions={1,2} | broadcast | bytes 1179648 | tf_op jit(solution)/shard_map/broadcast_in_dim | solution.py:70
  1.9 7.3 %all-to-all-start = ((f32[8,256,128]{2,1,0:T(8,128)}), f32[8,256,128]{2,1,0:T(8,128)}, u32[]{:S(2)}, u32[]{:S(2)}) async-start(f32[8,256,128]{2,1,0:T(8,128)} %broadcast_in_dim.3), calls=%async_computation | async-start | bytes 2097152 | tf_op jit(solution)/shard_map/all_to_all | solution.py:71
  9.2 1.0 %fusion.8 = (bf16[512,128]{1,0:T(8,128)(2,1)S(1)}, bf16[512,128]{1,0:T(8,128)(2,1)S(1)}) fusion(f32[512,128]{1,0:T(8,128)} %param.5), kind=kLoop, calls=%fused_computation.15 | loop fusion | flops 393216 | bytes 524288 | tf_op jit(solution)/shard_map/convert_element_type | solution.py:23
  10.2 0.3 fusion.21
  10.5 1.6 %collective-permute-start.1 = (f32[128,128]{0,1:T(8,128)S(1)}, f32[128,128]{0,1:T(8,128)S(1)}, u32[]{:S(2)}, u32[]{:S(2)}) collective-permute-start(f32[128,128]{0,1:T(8,128)S(1)} %fusion.11), channel_id=1, source_target_pairs={{0,1},{1,0},{2,3},{3,2},{4,5},{5,4},{6,7},{7,6},{8,9},{9,8},{10,11... | collective-permute-start | bytes 196616 | tf_op jit(solution)/shard_map/ppermute | solution.py:14
  12.1 0.7 pad_maximum_fusion.2.b_ref
  12.8 14.4 %shard_map.38 = f32[12288,128]{1,0:T(8,128)} custom-call(f32[24576,512]{1,0:T(8,128)} %bitcast.23, bf16[512,256]{1,0:T(8,128)(2,1)} %pad_maximum_fusion.2.b_ref), custom_call_target="tpu_custom_call" | custom-call | flops 6442450944 | bytes 31457280 | tf_op jit(solution)/shard_map/pallas_call | solution.py:51
  27.2 14.4 %shard_map.37 = f32[12288,128]{1,0:T(8,128)} custom-call(f32[24576,512]{1,0:T(8,128)} %bitcast.24, bf16[512,256]{1,0:T(8,128)(2,1)} %pad_maximum_fusion.2.b_ref), custom_call_target="tpu_custom_call" | custom-call | flops 6442450944 | bytes 31457280 | tf_op jit(solution)/shard_map/pallas_call | solution.py:51
  41.6 0.0 all-to-all-done
  41.6 0.0 collective-permute-start
  41.6 6.6 %pad_maximum_fusion = f32[24576,128]{1,0:T(8,128)S(1)} fusion(f32[12288,128]{1,0:T(8,128)} %shard_map.38, f32[12288,128]{1,0:T(8,128)} %shard_map.37), kind=kLoop, calls=%fused_computation | loop fusion | flops 3145728 | bytes 25165824 | tf_op jit(solution)/shard_map/concatenate | solution.py:94
  48.2 0.0 collective-permute-done
  48.2 1.4 %select_bitcast_fusion.1 = (f32[8,1,256,128]{3,2,1,0:T(8,128)S(1)}, f32[8,1,256,128]{3,2,1,0:T(8,128)S(1)}) fusion(f32[8,256,128]{2,1,0:T(8,128)} %all-to-all-done, f32[8,256,128]{2,1,0:T(8,128)S(1)} %collective-permute-done, pred[]{:T(512)S(6)} %eq.3), kind=kLoop, calls=%fused_computation.12 | loop fusion | flops 524288 | bytes 4194305 | tf_op jit(solution)/shard_map/stack | solution.py:79
  49.6 0.2 pad_maximum_fusion.1
  49.8 0.0 copy-start
  49.8 1.3 %copy-done = f32[8,2,256,128]{3,2,1,0:T(8,128)} copy-done((f32[8,2,256,128]{3,2,1,0:T(8,128)}, f32[8,2,256,128]{3,2,1,0:T(8,128)S(1)}, u32[]{:S(2)}) %copy-start) | copy-done | bytes 2097176
  51.2 1.7 %fusion.1 = (bf16[4096,128]{1,0:T(8,128)(2,1)}, bf16[4096,128]{1,0:T(8,128)(2,1)}) fusion(f32[8,2,256,128]{3,2,1,0:T(8,128)S(1)} %pad_maximum_fusion.1), kind=kLoop, calls=%fused_computation.4 | loop fusion | flops 3145728 | bytes 4194304 | tf_op jit(solution)/shard_map/convert_element_type | solution.py:23
  52.9 2.4 %multiply_reduce_fusion = f32[6,128]{1,0:T(8,128)S(1)} fusion(f32[6,4096,128]{2,1,0:T(8,128)S(1)} %bitcast.25, f32[4096,128]{1,0:T(8,128)} %bitcast.26), kind=kLoop, calls=%fused_computation.1 | loop fusion | flops 6290688 | bytes 14683136 | tf_op jit(solution)/shard_map/reduce_sum | solution.py:96
  55.3 0.6 collective-permute-start.2
  55.9 3.1 %fusion.3 = f32[256,256]{0,1:T(8,128)S(1)} fusion(bf16[4096,128]{1,0:T(8,128)(2,1)} %get-tuple-element.10, bf16[4096,128]{1,0:T(8,128)(2,1)} %get-tuple-element.9), kind=kOutput, calls=%fused_computation.7 | convolution fusion | flops 541065216 | bytes 2359296 | tf_op jit(solution)/shard_map/dot_general | solution.py:29
  59.0 0.0 collective-permute-done.1
  59.0 0.1 fusion.13
  59.1 0.1 copy.13
  59.2 11.7 %cholesky.16 = f32[128,128]{1,0:T(8,128)S(1)} custom-call(f32[128,128]{1,0:T(8,128)S(1)} %fusion.18), custom_call_target="Cholesky" | custom-call | tf_op jit(solution)/shard_map/jit(cholesky)/cholesky | solution.py:98
  71.0 0.6 compare_reduce_fusion
  71.6 0.7 fusion.10
  72.3 9.8 %custom-call.10 = f32[1,128,128]{1,2,0:T(8,128)S(1)} custom-call(f32[1,128,128]{2,1,0:T(8,128)S(1)} %fusion.10), custom_call_target="InvertDiagBlocksLowerTriangular" | custom-call | tf_op jit(solution)/shard_map/jit(_cho_solve)/triangular_solve | solution.py:100
  82.1 0.0 collective-permute-done.2
  82.1 0.3 fusion.16
  82.4 0.2 fusion.14
  82.6 0.7 constant_dynamic-slice_fusion
  (3 shorter events, 0.1 us)
Async XLA Ops:
  1.9 39.7 %all-to-all-start = ((f32[8,256,128]{2,1,0:T(8,128)}), f32[8,256,128]{2,1,0:T(8,128)}, u32[]{:S(2)}, u32[]{:S(2)}) async-start(f32[8,256,128]{2,1,0:T(8,128)} %broadcast_in_dim.3), calls=%async_computation | async-start | bytes 2097152 | tf_op jit(solution)/shard_map/all_to_all | solution.py:71
  10.5 48.5 %collective-permute-start.1 = (f32[128,128]{0,1:T(8,128)S(1)}, f32[128,128]{0,1:T(8,128)S(1)}, u32[]{:S(2)}, u32[]{:S(2)}) collective-permute-start(f32[128,128]{0,1:T(8,128)S(1)} %fusion.11), channel_id=1, source_target_pairs={{0,1},{1,0},{2,3},{3,2},{4,5},{5,4},{6,7},{7,6},{8,9},{9,8},{10,11... | collective-permute-start | bytes 196616 | tf_op jit(solution)/shard_map/ppermute | solution.py:14
  41.6 6.6 %collective-permute-start = (f32[8,256,128]{2,1,0:T(8,128)}, f32[8,256,128]{2,1,0:T(8,128)S(1)}, u32[]{:S(2)}, u32[]{:S(2)}) collective-permute-start(f32[8,256,128]{2,1,0:T(8,128)} %all-to-all-done), channel_id=1, source_target_pairs={{0,2},{2,0},{1,3},{3,1},{4,6},{6,4},{5,7},{7,5},{8,10},{10,8},{9,1... | collective-permute-start | bytes 3145736 | tf_op jit(solution)/shard_map/ppermute | solution.py:76
  49.8 1.3 %copy-start = (f32[8,2,256,128]{3,2,1,0:T(8,128)}, f32[8,2,256,128]{3,2,1,0:T(8,128)S(1)}, u32[]{:S(2)}) copy-start(f32[8,2,256,128]{3,2,1,0:T(8,128)S(1)} %pad_maximum_fusion.1) | copy-start | bytes 6291460
  55.3 26.8 %collective-permute-start.2 = (f32[6,128]{1,0:T(8,128)S(1)}, f32[6,128]{1,0:T(8,128)S(1)}, u32[]{:S(2)}, u32[]{:S(2)}) collective-permute-start(f32[6,128]{1,0:T(8,128)S(1)} %multiply_reduce_fusion), channel_id=1, source_target_pairs={{0,1},{1,0},{2,3},{3,2},{4,5},{5,4},{6,7},{7,6},{8,9},{9,8},{10,11... | collective-permute-start | bytes 9224 | tf_op jit(solution)/shard_map/ppermute | solution.py:14

commit v6 on v5

--- a/solution.py
+++ b/solution.py
@@ -91,9 +91,13 @@
     second_part = project(
         flat, bin_factor, half * cell_count, (image_rows - half) * cell_count
     )
-    projected = jnp.concatenate([first_part, second_part], axis=0)
-    projected = projected.reshape(image_rows, cell_count, rank_cols)
-    mttkrp = jnp.sum(projected * cell_full[None, :, :], axis=1)
+    mttkrp = jnp.concatenate(
+        [
+            jnp.sum(part.reshape(-1, cell_count, rank_cols) * cell_full[None], axis=1)
+            for part in (first_part, second_part)
+        ],
+        axis=0,
+    )
     gram = gram_of(cell_full) * gram_bin
     chol_lower = jnp.linalg.cholesky(gram)
     totals = exchange_sum(mttkrp, "bin")

time: 83.7 us -> 83.7 us (level)
  waiting for transfers between devices: 0.01 us -> 10.6 us
  other arithmetic: 37 us -> 29.9 us
  matrix products: 3.87 us -> 1.72 us
  local copies, waits for them, and re-layouts: 4.08 us -> 2.82 us
    all_to_all x1, waiting for transfers between devices: 0.01 us -> 10.5 us  [gather_cells(): mine = lax.all_to_all(spread, 'cell_outer', 0, 0, tiled=True)]
    concatenate x1, other arithmetic: 6.58 us -> 0.01 us  [body(): jnp.concatenate([jnp.sum(part.reshape(-1, cell_count, rank_cols) * cell_f...]
    reduce_sum x1, other arithmetic: 2.41 us -> 5.43 us  [body(): jnp.sum(part.reshape(-1, cell_count, rank_cols) * cell_full[None], axis=1)]
    convert_element_type x2, other arithmetic: 2.73 us -> 0.48 us  [split_pair(): return (hi.astype(jnp.bfloat16), lo.astype(jnp.bfloat16))]
    dot_general x2, matrix products: 3.38 us -> 1.22 us  [gram_of(): lax.dot_general(both, both, (((0,), (0,)), ((), ())), preferred_element_t...]
    unnamed x2, local copies, waits for them, and re-layouts: 1.34 us -> 0.01 us
    another operation x2, other arithmetic: 1.59 us -> 0.35 us  [gather_cells(): jnp.stack(pair, axis=1).reshape(-1, cell_factor.shape[1])]
  transfers between devices with their start and end apart: 4 -> 4, of which waited for: 0 -> 1; matrix products, arithmetic and copies ran while one was open for 49% -> 16% of each run, Pallas kernels for 35% -> 35%
where the time goes in v6:
time: 83.7 us; the launch traced here: 83.4 us
  other arithmetic  29.9 us (36%)
  Pallas kernels  28.8 us (34%)
  waiting for transfers between devices  10.6 us (13%)
  starting transfers between devices  9.45 us (11%)
  local copies, waits for them, and re-layouts  2.82 us (3%)
  matrix products  1.72 us (2%)
    pallas_call x2, Pallas kernels, project(): pl.pallas_call(project_kernel, out_shape=jax.ShapeDtypeStruct((rows, rank...  28.8 us
    another operation x3, other arithmetic, body(): chol_lower = jnp.linalg.cholesky(gram)  12.4 us
    all_to_all x1, waiting for transfers between devices, gather_cells(): mine = lax.all_to_all(spread, 'cell_outer', 0, 0, tiled=True)  10.5 us
    another operation x2, other arithmetic, body(): solved = jax.scipy.linalg.cho_solve((chol_lower, True), totals.T).T  10.5 us
    all_to_all x1, starting transfers between devices, gather_cells(): mine = lax.all_to_all(spread, 'cell_outer', 0, 0, tiled=True)  7.28 us
    reduce_sum x1, other arithmetic, body(): jnp.sum(part.reshape(-1, cell_count, rank_cols) * cell_full[None], axis=1)  5.43 us
    ppermute x2, starting transfers between devices, exchange_sum(): value = value + lax.ppermute(value, axis, pairs)  2.16 us
    broadcast_in_dim x1, local copies, waits for them, and re-layouts, gather_cells(): spread = jnp.broadcast_to(cell_factor[None], (outer,) + cell_factor.shape)  2.02 us
  transfers between devices with their start and end apart: 4, of which 1 were waited for; matrix products, arithmetic and copies ran while one was open for 16% of the time, Pallas kernels for 35%

profile of v6, /device:TPU:0, one launch (start us, length us, event | category | flops | bytes accessed | tf_op | source)
XLA Modules:
  0.0 83.4 jit_solution(8040830658313995134)
XLA Ops:
  0.0 0.0 copy-start
  0.0 2.0 %broadcast_in_dim.3 = f32[8,256,128]{2,1,0:T(8,128)} broadcast(f32[256,128]{1,0:T(8,128)} %param.4), dimensions={1,2} | broadcast | bytes 1179648 | tf_op jit(solution)/shard_map/broadcast_in_dim | solution.py:70
  2.0 7.3 %all-to-all-start = ((f32[8,256,128]{2,1,0:T(8,128)}), f32[8,256,128]{2,1,0:T(8,128)S(1)}, u32[]{:S(2)}, u32[]{:S(2)}) async-start(f32[8,256,128]{2,1,0:T(8,128)} %broadcast_in_dim.3), calls=%async_computation | async-start | bytes 2097152 | tf_op jit(solution)/shard_map/all_to_all | solution.py:71
  9.3 0.0 copy-done
  9.3 0.1 fusion.8
  9.4 0.7 pad_maximum_fusion.1.b_ref
  10.1 14.4 %shard_map.37 = f32[12288,128]{1,0:T(8,128)} custom-call(f32[24576,512]{1,0:T(8,128)} %bitcast.24, bf16[512,256]{1,0:T(8,128)(2,1)} %pad_maximum_fusion.1.b_ref), custom_call_target="tpu_custom_call" | custom-call | flops 6442450944 | bytes 31457280 | tf_op jit(solution)/shard_map/pallas_call | solution.py:51
  24.5 10.5 %all-to-all-done = f32[8,256,128]{2,1,0:T(8,128)S(1)} async-done(((f32[8,256,128]{2,1,0:T(8,128)}), f32[8,256,128]{2,1,0:T(8,128)S(1)}, u32[]{:S(2)}, u32[]{:S(2)}) %all-to-all-start) | async-done | bytes 1048608 | tf_op jit(solution)/shard_map/all_to_all | solution.py:71
  35.1 0.0 collective-permute-start
  35.1 0.3 fusion.21
  35.4 1.6 %collective-permute-start.1 = (f32[128,128]{0,1:T(8,128)S(1)}, f32[128,128]{0,1:T(8,128)S(1)}, u32[]{:S(2)}, u32[]{:S(2)}) collective-permute-start(f32[128,128]{0,1:T(8,128)S(1)} %fusion.11), channel_id=1, source_target_pairs={{0,1},{1,0},{2,3},{3,2},{4,5},{5,4},{6,7},{7,6},{8,9},{9,8},{10,11... | collective-permute-start | bytes 196616 | tf_op jit(solution)/shard_map/ppermute | solution.py:14
  36.9 14.4 %shard_map.38 = f32[12288,128]{1,0:T(8,128)} custom-call(f32[24576,512]{1,0:T(8,128)} %bitcast.25, bf16[512,256]{1,0:T(8,128)(2,1)} %pad_maximum_fusion.1.b_ref), custom_call_target="tpu_custom_call" | custom-call | flops 6442450944 | bytes 31457280 | tf_op jit(solution)/shard_map/pallas_call | solution.py:51
  51.3 0.0 collective-permute-done
  51.3 0.2 select_bitcast_fusion.1
  51.5 0.2 pad_maximum_fusion
  51.7 0.4 fusion.1
  52.1 0.9 %fusion.3 = f32[256,256]{0,1:T(8,128)S(1)} fusion(bf16[4096,128]{1,0:T(8,128)(2,1)S(1)} %get-tuple-element.12, bf16[4096,128]{1,0:T(8,128)(2,1)S(1)} %get-tuple-element.11), kind=kOutput, calls=%fused_computation.7 | convolution fusion | flops 541065216 | bytes 2359296 | tf_op jit(solution)/shard_map/dot_general | solution.py:29
  53.1 0.0 collective-permute-done.1
  53.1 0.1 fusion.13
  53.1 0.1 copy.13
  53.2 11.7 %cholesky.16 = f32[128,128]{1,0:T(8,128)S(1)} custom-call(f32[128,128]{1,0:T(8,128)S(1)} %fusion.18), custom_call_target="Cholesky" | custom-call | tf_op jit(solution)/shard_map/jit(cholesky)/cholesky | solution.py:102
  65.0 0.6 compare_reduce_fusion
  65.6 5.4 %multiply_reduce_fusion.1 = (f32[3,128]{1,0:T(4,128)S(1)}, f32[3,128]{1,0:T(4,128)S(1)}) fusion(f32[3,4096,128]{2,1,0:T(8,128)} %bitcast.26, f32[4096,128]{1,0:T(8,128)S(1)} %bitcast.28, f32[3,4096,128]{2,1,0:T(8,128)} %bitcast.27), kind=kLoop, calls=%fused_computation.1 | loop fusion | flops 6290688 | bytes 14683136 | tf_op jit(solution)/shard_map/reduce_sum | solution.py:96
  71.1 0.6 collective-permute-start.2
  71.7 0.7 fusion.10
  72.4 9.8 %custom-call.10 = f32[1,128,128]{1,2,0:T(8,128)S(1)} custom-call(f32[1,128,128]{2,1,0:T(8,128)S(1)} %fusion.10), custom_call_target="InvertDiagBlocksLowerTriangular" | custom-call | tf_op jit(solution)/shard_map/jit(_cho_solve)/triangular_solve | solution.py:104
  82.2 0.0 collective-permute-done.2
  82.2 0.3 fusion.16
  82.5 0.2 fusion.14
  82.7 0.7 constant_dynamic-slice_fusion
  (4 shorter events, 0.1 us)
Async XLA Ops:
  0.0 9.3 %copy-start = (f32[512,128]{1,0:T(8,128)S(1)}, f32[512,128]{1,0:T(8,128)}, u32[]{:S(2)}) copy-start(f32[512,128]{1,0:T(8,128)} %param.5) | copy-start | bytes 786436
  2.0 33.0 %all-to-all-start = ((f32[8,256,128]{2,1,0:T(8,128)}), f32[8,256,128]{2,1,0:T(8,128)S(1)}, u32[]{:S(2)}, u32[]{:S(2)}) async-start(f32[8,256,128]{2,1,0:T(8,128)} %broadcast_in_dim.3), calls=%async_computation | async-start | bytes 2097152 | tf_op jit(solution)/shard_map/all_to_all | solution.py:71
  35.1 16.2 %collective-permute-start = (f32[8,256,128]{2,1,0:T(8,128)S(1)}, f32[8,256,128]{2,1,0:T(8,128)S(1)}, u32[]{:S(2)}, u32[]{:S(2)}) collective-permute-start(f32[8,256,128]{2,1,0:T(8,128)S(1)} %all-to-all-done), channel_id=1, source_target_pairs={{0,2},{2,0},{1,3},{3,1},{4,6},{6,4},{5,7},{7,5},{8,10},{10,8},{9,1... | collective-permute-start | bytes 3145736 | tf_op jit(solution)/shard_map/ppermute | solution.py:76
  35.4 17.7 %collective-permute-start.1 = (f32[128,128]{0,1:T(8,128)S(1)}, f32[128,128]{0,1:T(8,128)S(1)}, u32[]{:S(2)}, u32[]{:S(2)}) collective-permute-start(f32[128,128]{0,1:T(8,128)S(1)} %fusion.11), channel_id=1, source_target_pairs={{0,1},{1,0},{2,3},{3,2},{4,5},{5,4},{6,7},{7,6},{8,9},{9,8},{10,11... | collective-permute-start | bytes 196616 | tf_op jit(solution)/shard_map/ppermute | solution.py:14
  71.1 11.1 %collective-permute-start.2 = (f32[6,128]{1,0:T(8,128)S(1)}, f32[6,128]{1,0:T(8,128)S(1)}, u32[]{:S(2)}, u32[]{:S(2)}) collective-permute-start(f32[6,128]{1,0:T(8,128)S(1)} %pad_maximum_fusion.2), channel_id=1, source_target_pairs={{0,1},{1,0},{2,3},{3,2},{4,5},{5,4},{6,7},{7,6},{8,9},{9,8},{10,11... | collective-permute-start | bytes 9224 | tf_op jit(solution)/shard_map/ppermute | solution.py:14

commit v7 on v5

--- a/solution.py
+++ b/solution.py
@@ -82,18 +82,14 @@
 def body(tensor, cell_factor, bin_factor):
     image_rows, cell_count, bin_count = tensor.shape
     rank_cols = bin_factor.shape[1]
-    half = image_rows // 2
-    flat = tensor.reshape(image_rows * cell_count, bin_count)
-    cell_full, first_part = gather_cells(
-        cell_factor, lambda: project(flat, bin_factor, 0, half * cell_count)
+    rows = image_rows * cell_count
+    flat = tensor.reshape(rows, bin_count)
+    gram_bin = exchange_sum(gram_of(bin_factor), "bin")
+    cell_full, projected = gather_cells(
+        cell_factor, lambda: project(flat, bin_factor, 0, rows)
     )
-    gram_bin = exchange_sum(gram_of(bin_factor), "bin")
-    second_part = project(
-        flat, bin_factor, half * cell_count, (image_rows - half) * cell_count
-    )
-    projected = jnp.concatenate([first_part, second_part], axis=0)
     projected = projected.reshape(image_rows, cell_count, rank_cols)
-    mttkrp = jnp.sum(projected * cell_full[None, :, :], axis=1)
+    mttkrp = jnp.sum(projected * cell_full[None], axis=1)
     gram = gram_of(cell_full) * gram_bin
     chol_lower = jnp.linalg.cholesky(gram)
     totals = exchange_sum(mttkrp, "bin")

time: 83.7 us -> 76.3 us (0.912)
  other arithmetic: 37 us -> 29.9 us
  Pallas kernels: 28.8 us -> 24.3 us
  local copies, waits for them, and re-layouts: 4.08 us -> 5.78 us
  waiting for transfers between devices: 0.01 us -> 1.58 us
  starting transfers between devices: 9.43 us -> 10.4 us
    concatenate x1 -> x0, other arithmetic: 6.58 us -> none  [body(): projected = jnp.concatenate([first_part, second_part], axis=0)]
    pallas_call x2 -> x1, Pallas kernels: 28.8 us -> 24.3 us  [project(): pl.pallas_call(project_kernel, out_shape=jax.ShapeDtypeStruct((rows, rank...]
    unnamed x2 -> x8, local copies, waits for them, and re-layouts: 1.34 us -> 2.93 us
    ppermute x2, starting transfers between devices: 2.15 us -> 3.11 us  [exchange_sum(): value = value + lax.ppermute(value, axis, pairs)]
    convert_element_type x2, other arithmetic: 2.73 us -> 1.8 us  [split_pair(): return (hi.astype(jnp.bfloat16), lo.astype(jnp.bfloat16))]
    ppermute x1, waiting for transfers between devices: 0.01 us -> 0.93 us  [gather_cells(): other = lax.ppermute(mine, 'cell_core', [(0, 1), (1, 0)])]
  transfers between devices with their start and end apart: 4 -> 4, of which waited for: 0 -> 2; matrix products, arithmetic and copies ran while one was open for 49% -> 44% of each run, Pallas kernels for 35% -> 32%
where the time goes in v7:
time: 76.3 us; the launch traced here: 76 us
  other arithmetic  29.9 us (39%)
  Pallas kernels  24.3 us (32%)
  starting transfers between devices  10.4 us (14%)
  local copies, waits for them, and re-layouts  5.78 us (8%)
  matrix products  3.87 us (5%)
  waiting for transfers between devices  1.58 us (2%)
    pallas_call x1, Pallas kernels, project(): pl.pallas_call(project_kernel, out_shape=jax.ShapeDtypeStruct((rows, rank...  24.3 us
    another operation x3, other arithmetic, body(): chol_lower = jnp.linalg.cholesky(gram)  12.4 us
    another operation x2, other arithmetic, body(): solved = jax.scipy.linalg.cho_solve((chol_lower, True), totals.T).T  10.5 us
    all_to_all x1, starting transfers between devices, gather_cells(): mine = lax.all_to_all(spread, 'cell_outer', 0, 0, tiled=True)  7.28 us
    dot_general x2, matrix products, gram_of(): lax.dot_general(both, both, (((0,), (0,)), ((), ())), preferred_element_t...  3.38 us
    ppermute x2, starting transfers between devices, exchange_sum(): value = value + lax.ppermute(value, axis, pairs)  3.11 us
    unnamed x8, local copies, waits for them, and re-layouts  2.93 us
    reduce_sum x1, other arithmetic, body(): mttkrp = jnp.sum(projected * cell_full[None], axis=1)  2.41 us
  transfers between devices with their start and end apart: 4, of which 2 were waited for; matrix products, arithmetic and copies ran while one was open for 44% of the time, Pallas kernels for 32%

profile of v7, /device:TPU:0, one launch (start us, length us, event | category | flops | bytes accessed | tf_op | source)
XLA Modules:
  0.0 76.0 jit_solution(17727207789726299005)
XLA Ops:
  0.0 0.0 copy-start.3
  0.0 2.0 %broadcast_in_dim.3 = f32[8,256,128]{2,1,0:T(8,128)} broadcast(f32[256,128]{1,0:T(8,128)} %param.4), dimensions={1,2} | broadcast | bytes 1179648 | tf_op jit(solution)/shard_map/broadcast_in_dim | solution.py:70
  2.1 7.3 %all-to-all-start = ((f32[8,256,128]{2,1,0:T(8,128)}), f32[8,256,128]{2,1,0:T(8,128)S(1)}, u32[]{:S(2)}, u32[]{:S(2)}) async-start(f32[8,256,128]{2,1,0:T(8,128)} %broadcast_in_dim.3), calls=%async_computation | async-start | bytes 2097152 | tf_op jit(solution)/shard_map/all_to_all | solution.py:71
  9.3 0.0 copy-done.3
  9.3 0.1 fusion.8
  9.4 0.7 pad_maximum_fusion.1.b_ref
  10.1 24.3 %shard_map.37 = f32[24576,128]{1,0:T(8,128)} custom-call(f32[24576,512]{1,0:T(8,128)} %bitcast.23, bf16[512,256]{1,0:T(8,128)(2,1)} %pad_maximum_fusion.1.b_ref), custom_call_target="tpu_custom_call" | custom-call | flops 12884901888 | bytes 62914560 | tf_op jit(solution)/shard_map/pallas_call | solution.py:51
  34.5 0.6 all-to-all-done
  35.1 0.0 collective-permute-start
  35.1 0.3 fusion.21
  35.4 1.6 %collective-permute-start.1 = (f32[128,128]{0,1:T(8,128)S(1)}, f32[128,128]{0,1:T(8,128)S(1)}, u32[]{:S(2)}, u32[]{:S(2)}) collective-permute-start(f32[128,128]{0,1:T(8,128)S(1)} %fusion.11), channel_id=1, source_target_pairs={{0,1},{1,0},{2,3},{3,2},{4,5},{5,4},{6,7},{7,6},{8,9},{9,8},{10,11... | collective-permute-start | bytes 196616 | tf_op jit(solution)/shard_map/ppermute | solution.py:14
  37.0 0.0 copy-done.2
  37.0 0.9 %collective-permute-done = f32[8,256,128]{2,1,0:T(8,128)} collective-permute-done((f32[8,256,128]{2,1,0:T(8,128)S(1)}, f32[8,256,128]{2,1,0:T(8,128)}, u32[]{:S(2)}, u32[]{:S(2)}) %collective-permute-start) | collective-permute-done | bytes 1048608 | tf_op jit(solution)/shard_map/ppermute | solution.py:76
  37.9 1.8 %select_bitcast_fusion.1 = (f32[8,1,256,128]{3,2,1,0:T(8,128)S(1)}, f32[8,1,256,128]{3,2,1,0:T(8,128)S(1)}) fusion(f32[8,256,128]{2,1,0:T(8,128)} %copy-done.2, f32[8,256,128]{2,1,0:T(8,128)} %collective-permute-done, pred[]{:T(512)S(6)} %eq.3), kind=kLoop, calls=%fused_computation.11 | loop fusion | flops 524288 | bytes 4194305 | tf_op jit(solution)/shard_map/stack | solution.py:79
  39.7 0.2 pad_maximum_fusion
  39.9 0.0 copy-start.1
  39.9 1.7 %fusion.1 = (bf16[4096,128]{1,0:T(8,128)(2,1)}, bf16[4096,128]{1,0:T(8,128)(2,1)}) fusion(f32[8,2,256,128]{3,2,1,0:T(8,128)S(1)} %pad_maximum_fusion), kind=kLoop, calls=%fused_computation.3 | loop fusion | flops 3145728 | bytes 4194304 | tf_op jit(solution)/shard_map/convert_element_type | solution.py:23
  41.7 0.4 copy-done.1
  42.1 2.5 %copy-done = f32[24576,128]{1,0:T(8,128)S(1)} copy-done((f32[24576,128]{1,0:T(8,128)S(1)}, f32[24576,128]{1,0:T(8,128)}, u32[]{:S(2)}) %copy-start) | copy-done | bytes 12582936
  44.6 2.4 %multiply_reduce_fusion = f32[6,128]{1,0:T(8,128)S(1)} fusion(f32[6,4096,128]{2,1,0:T(8,128)S(1)} %bitcast.24, f32[4096,128]{1,0:T(8,128)} %bitcast.25), kind=kLoop, calls=%fused_computation | loop fusion | flops 6290688 | bytes 14683136 | tf_op jit(solution)/shard_map/reduce_sum | solution.py:92
  47.0 1.6 %collective-permute-start.2 = (f32[6,128]{1,0:T(8,128)S(1)}, f32[6,128]{1,0:T(8,128)S(1)}, u32[]{:S(2)}, u32[]{:S(2)}) collective-permute-start(f32[6,128]{1,0:T(8,128)S(1)} %multiply_reduce_fusion), channel_id=1, source_target_pairs={{0,1},{1,0},{2,3},{3,2},{4,5},{5,4},{6,7},{7,6},{8,9},{9,8},{10,11... | collective-permute-start | bytes 9224 | tf_op jit(solution)/shard_map/ppermute | solution.py:14
  48.6 3.1 %fusion.3 = f32[256,256]{0,1:T(8,128)S(1)} fusion(bf16[4096,128]{1,0:T(8,128)(2,1)} %get-tuple-element.10, bf16[4096,128]{1,0:T(8,128)(2,1)} %get-tuple-element.9), kind=kOutput, calls=%fused_computation.6 | convolution fusion | flops 541065216 | bytes 2359296 | tf_op jit(solution)/shard_map/dot_general | solution.py:29
  51.7 0.0 collective-permute-done.1
  51.7 0.1 copy.13
  51.9 11.7 %cholesky.16 = f32[128,128]{1,0:T(8,128)S(1)} custom-call(f32[128,128]{1,0:T(8,128)S(1)} %fusion.18), custom_call_target="Cholesky" | custom-call | tf_op jit(solution)/shard_map/jit(cholesky)/cholesky | solution.py:94
  63.6 0.6 compare_reduce_fusion
  64.3 0.7 fusion.10
  64.9 9.8 %custom-call.10 = f32[1,128,128]{1,2,0:T(8,128)S(1)} custom-call(f32[1,128,128]{2,1,0:T(8,128)S(1)} %fusion.10), custom_call_target="InvertDiagBlocksLowerTriangular" | custom-call | tf_op jit(solution)/shard_map/jit(_cho_solve)/triangular_solve | solution.py:96
  74.7 0.0 collective-permute-done.2
  74.7 0.3 fusion.16
  75.0 0.2 fusion.14
  75.2 0.7 constant_dynamic-slice_fusion
  (6 shorter events, 0.1 us)
Async XLA Ops:
  0.0 9.3 %copy-start.3 = (f32[512,128]{1,0:T(8,128)S(1)}, f32[512,128]{1,0:T(8,128)}, u32[]{:S(2)}) copy-start(f32[512,128]{1,0:T(8,128)} %param.5) | copy-start | bytes 786436
  2.1 33.0 %all-to-all-start = ((f32[8,256,128]{2,1,0:T(8,128)}), f32[8,256,128]{2,1,0:T(8,128)S(1)}, u32[]{:S(2)}, u32[]{:S(2)}) async-start(f32[8,256,128]{2,1,0:T(8,128)} %broadcast_in_dim.3), calls=%async_computation | async-start | bytes 2097152 | tf_op jit(solution)/shard_map/all_to_all | solution.py:71
  35.1 1.9 %copy-start.2 = (f32[8,256,128]{2,1,0:T(8,128)}, f32[8,256,128]{2,1,0:T(8,128)S(1)}, u32[]{:S(2)}) copy-start(f32[8,256,128]{2,1,0:T(8,128)S(1)} %all-to-all-done) | copy-start | bytes 3145732
  35.1 2.8 %collective-permute-start = (f32[8,256,128]{2,1,0:T(8,128)S(1)}, f32[8,256,128]{2,1,0:T(8,128)}, u32[]{:S(2)}, u32[]{:S(2)}) collective-permute-start(f32[8,256,128]{2,1,0:T(8,128)S(1)} %all-to-all-done), channel_id=1, source_target_pairs={{0,2},{2,0},{1,3},{3,1},{4,6},{6,4},{5,7},{7,5},{8,10},{10,8},{9,1... | collective-permute-start | bytes 3145736 | tf_op jit(solution)/shard_map/ppermute | solution.py:76
  35.4 16.3 %collective-permute-start.1 = (f32[128,128]{0,1:T(8,128)S(1)}, f32[128,128]{0,1:T(8,128)S(1)}, u32[]{:S(2)}, u32[]{:S(2)}) collective-permute-start(f32[128,128]{0,1:T(8,128)S(1)} %fusion.11), channel_id=1, source_target_pairs={{0,1},{1,0},{2,3},{3,2},{4,5},{5,4},{6,7},{7,6},{8,9},{9,8},{10,11... | collective-permute-start | bytes 196616 | tf_op jit(solution)/shard_map/ppermute | solution.py:14
  37.9 6.7 %copy-start = (f32[24576,128]{1,0:T(8,128)S(1)}, f32[24576,128]{1,0:T(8,128)}, u32[]{:S(2)}) copy-start(f32[24576,128]{1,0:T(8,128)} %shard_map.37) | copy-start | bytes 37748740
  39.9 2.1 %copy-start.1 = (f32[8,2,256,128]{3,2,1,0:T(8,128)}, f32[8,2,256,128]{3,2,1,0:T(8,128)S(1)}, u32[]{:S(2)}) copy-start(f32[8,2,256,128]{3,2,1,0:T(8,128)S(1)} %pad_maximum_fusion) | copy-start | bytes 6291460
  47.0 27.7 %collective-permute-start.2 = (f32[6,128]{1,0:T(8,128)S(1)}, f32[6,128]{1,0:T(8,128)S(1)}, u32[]{:S(2)}, u32[]{:S(2)}) collective-permute-start(f32[6,128]{1,0:T(8,128)S(1)} %multiply_reduce_fusion), channel_id=1, source_target_pairs={{0,1},{1,0},{2,3},{3,2},{4,5},{5,4},{6,7},{7,6},{8,9},{9,8},{10,11... | collective-permute-start | bytes 9224 | tf_op jit(solution)/shard_map/ppermute | solution.py:14

commit v8 on v7

--- a/solution.py
+++ b/solution.py
@@ -79,6 +79,33 @@
     return jnp.stack(pair, axis=1).reshape(-1, cell_factor.shape[1]), first_part
 
 
+def sweep_kernel(g_ref, o_ref):
+    n = g_ref.shape[0]
+    sub = lax.broadcasted_iota(jnp.int32, (n, n), 0)
+    lane = lax.broadcasted_iota(jnp.int32, (n, n), 1)
+
+    def step(k, a):
+        on_row = sub == k
+        on_col = lane == k
+        row = jnp.sum(jnp.where(on_row, a, 0.0), axis=0, keepdims=True)
+        col = jnp.sum(jnp.where(on_col, a, 0.0), axis=1, keepdims=True)
+        pivot = jnp.sum(jnp.where(on_col[:1], row, 0.0), axis=1, keepdims=True)
+        inv = 1.0 / pivot
+        scaled_row = row * inv
+        upd = a - col * scaled_row
+        upd = jnp.where(on_col, col * inv, upd)
+        upd = jnp.where(on_row, scaled_row, upd)
+        return jnp.where(on_row & on_col, -inv, upd)
+
+    o_ref[...] = lax.fori_loop(0, n, step, g_ref[...], unroll=8)
+
+
+def negated_inverse(gram):
+    return pl.pallas_call(
+        sweep_kernel, out_shape=jax.ShapeDtypeStruct(gram.shape, jnp.float32)
+    )(gram)
+
+
 def body(tensor, cell_factor, bin_factor):
     image_rows, cell_count, bin_count = tensor.shape
     rank_cols = bin_factor.shape[1]
@@ -91,12 +118,11 @@
     projected = projected.reshape(image_rows, cell_count, rank_cols)
     mttkrp = jnp.sum(projected * cell_full[None], axis=1)
     gram = gram_of(cell_full) * gram_bin
-    chol_lower = jnp.linalg.cholesky(gram)
+    neg_inv = negated_inverse(gram)
     totals = exchange_sum(mttkrp, "bin")
-    solved = jax.scipy.linalg.cho_solve((chol_lower, True), totals.T).T
     own_cols = rank_cols // lax.axis_size("bin")
-    updated = lax.dynamic_slice_in_dim(solved, lax.axis_index("bin") * own_cols, own_cols, 1)
-    return updated
+    own = lax.dynamic_slice_in_dim(neg_inv, lax.axis_index("bin") * own_cols, own_cols, 1)
+    return -jnp.dot(totals, own, precision=lax.Precision.HIGHEST)
 
 
 def solution(mesh):

time: 76.3 us -> 70.7 us (0.927)
  other arithmetic: 29.9 us -> 7.67 us
  Pallas kernels: 24.3 us -> 40.8 us
  matrix products: 3.87 us -> 4.85 us
  local copies, waits for them, and re-layouts: 5.78 us -> 4.96 us
    another operation x5 -> x0, other arithmetic: 22.9 us -> none  [the longest x3 12.4 us: body(): chol_lower = jnp.linalg.cholesky(gram)]
    pallas_call x0 -> x1, Pallas kernels: none -> 16.4 us  [negated_inverse(): pl.pallas_call(sweep_kernel, out_shape=jax.ShapeDtypeStruct(gram.shape, j...]
    dot_general x0 -> x1, matrix products: none -> 1.67 us  [body(): return -jnp.dot(totals, own, precision=lax.Precision.HIGHEST)]
  transfers between devices with their start and end apart: 4 -> 4, of which waited for: 2 -> 2; matrix products, arithmetic and copies ran while one was open for 44% -> 15% of each run, Pallas kernels for 32% -> 58%
where the time goes in v8:
time: 70.7 us; the launch traced here: 70.3 us
  Pallas kernels  40.8 us (58%)
  starting transfers between devices  10.4 us (15%)
  other arithmetic  7.67 us (11%)
  local copies, waits for them, and re-layouts  4.96 us (7%)
  matrix products  4.85 us (7%)
  waiting for transfers between devices  1.55 us (2%)
    pallas_call x1, Pallas kernels, project(): pl.pallas_call(project_kernel, out_shape=jax.ShapeDtypeStruct((rows, rank...  24.3 us
    pallas_call x1, Pallas kernels, negated_inverse(): pl.pallas_call(sweep_kernel, out_shape=jax.ShapeDtypeStruct(gram.shape, j...  16.4 us
    all_to_all x1, starting transfers between devices, gather_cells(): mine = lax.all_to_all(spread, 'cell_outer', 0, 0, tiled=True)  7.28 us
    dot_general x2, matrix products, gram_of(): lax.dot_general(both, both, (((0,), (0,)), ((), ())), preferred_element_t...  3.17 us
    ppermute x2, starting transfers between devices, exchange_sum(): value = value + lax.ppermute(value, axis, pairs)  3.11 us
    unnamed x8, local copies, waits for them, and re-layouts  2.91 us
    reduce_sum x1, other arithmetic, body(): mttkrp = jnp.sum(projected * cell_full[None], axis=1)  2.41 us
    broadcast_in_dim x1, local copies, waits for them, and re-layouts, gather_cells(): spread = jnp.broadcast_to(cell_factor[None], (outer,) + cell_factor.shape)  2.05 us
  transfers between devices with their start and end apart: 4, of which 2 were waited for; matrix products, arithmetic and copies ran while one was open for 15% of the time, Pallas kernels for 58%

profile of v8, /device:TPU:0, one launch (start us, length us, event | category | flops | bytes accessed | tf_op | source)
XLA Modules:
  0.0 70.3 jit_solution(13162450314831751724)
XLA Ops:
  0.0 0.0 copy-start.3
  0.0 2.1 %broadcast_in_dim.2 = f32[8,256,128]{2,1,0:T(8,128)} broadcast(f32[256,128]{1,0:T(8,128)} %param.4), dimensions={1,2} | broadcast | bytes 1179648 | tf_op jit(solution)/shard_map/broadcast_in_dim | solution.py:70
  2.1 7.3 %all-to-all-start = ((f32[8,256,128]{2,1,0:T(8,128)}), f32[8,256,128]{2,1,0:T(8,128)S(1)}, u32[]{:S(2)}, u32[]{:S(2)}) async-start(f32[8,256,128]{2,1,0:T(8,128)} %broadcast_in_dim.2), calls=%async_computation | async-start | bytes 2097152 | tf_op jit(solution)/shard_map/all_to_all | solution.py:71
  9.3 0.0 copy-done.3
  9.3 0.1 fusion.8
  9.4 0.7 %pad_maximum_fusion.1.b_ref = bf16[512,256]{1,0:T(8,128)(2,1)} fusion(bf16[512,128]{1,0:T(8,128)(2,1)S(1)} %get-tuple-element.14, bf16[512,128]{1,0:T(8,128)(2,1)S(1)} %get-tuple-element.13), kind=kLoop, calls=%fused_computation.17 | loop fusion | flops 524288 | bytes 524288 | tf_op jit(solution)/shard_map/concatenate | solution.py:50
  10.1 24.3 %shard_map.37 = f32[24576,128]{1,0:T(8,128)} custom-call(f32[24576,512]{1,0:T(8,128)} %bitcast.11, bf16[512,256]{1,0:T(8,128)(2,1)} %pad_maximum_fusion.1.b_ref), custom_call_target="tpu_custom_call" | custom-call | flops 12884901888 | bytes 62914560 | tf_op jit(solution)/shard_map/pallas_call | solution.py:51
  34.5 0.6 all-to-all-done
  35.1 0.0 copy-start.2
  35.1 0.0 collective-permute-start
  35.1 0.3 fusion.17
  35.4 1.6 %collective-permute-start.2 = (f32[128,128]{1,0:T(8,128)S(1)}, f32[128,128]{1,0:T(8,128)S(1)}, u32[]{:S(2)}, u32[]{:S(2)}) collective-permute-start(f32[128,128]{1,0:T(8,128)S(1)} %fusion.10), channel_id=1, source_target_pairs={{0,1},{1,0},{2,3},{3,2},{4,5},{5,4},{6,7},{7,6},{8,9},{9,8},{10,11... | collective-permute-start | bytes 196616 | tf_op jit(solution)/shard_map/ppermute | solution.py:14
  37.0 0.0 copy-done.2
  37.0 0.9 %collective-permute-done = f32[8,256,128]{2,1,0:T(8,128)} collective-permute-done((f32[8,256,128]{2,1,0:T(8,128)S(1)}, f32[8,256,128]{2,1,0:T(8,128)}, u32[]{:S(2)}, u32[]{:S(2)}) %collective-permute-start) | collective-permute-done | bytes 1048608 | tf_op jit(solution)/shard_map/ppermute | solution.py:76
  37.9 0.0 copy-start
  37.9 1.9 %select_bitcast_fusion.1 = (f32[8,1,256,128]{3,2,1,0:T(8,128)S(1)}, f32[8,1,256,128]{3,2,1,0:T(8,128)S(1)}) fusion(f32[8,256,128]{2,1,0:T(8,128)} %copy-done.2, f32[8,256,128]{2,1,0:T(8,128)} %collective-permute-done, pred[]{:T(512)S(6)} %eq.3), kind=kLoop, calls=%fused_computation.12 | loop fusion | flops 524288 | bytes 4194305 | tf_op jit(solution)/shard_map/stack | solution.py:79
  39.8 0.2 pad_maximum_fusion
  40.0 0.0 copy-start.1
  40.0 1.7 %fusion.1 = (bf16[4096,128]{1,0:T(8,128)(2,1)}, bf16[4096,128]{1,0:T(8,128)(2,1)}) fusion(f32[8,2,256,128]{3,2,1,0:T(8,128)S(1)} %pad_maximum_fusion), kind=kLoop, calls=%fused_computation.3 | loop fusion | flops 3145728 | bytes 4194304 | tf_op jit(solution)/shard_map/convert_element_type | solution.py:23
  41.7 0.4 copy-done.1
  42.1 2.5 %copy-done = f32[24576,128]{1,0:T(8,128)S(1)} copy-done((f32[24576,128]{1,0:T(8,128)S(1)}, f32[24576,128]{1,0:T(8,128)}, u32[]{:S(2)}) %copy-start) | copy-done | bytes 12582936
  44.6 2.4 %multiply_reduce_fusion = f32[6,128]{1,0:T(8,128)S(1)} fusion(f32[6,4096,128]{2,1,0:T(8,128)S(1)} %bitcast.12, f32[4096,128]{1,0:T(8,128)} %bitcast.13), kind=kLoop, calls=%fused_computation | loop fusion | flops 6290688 | bytes 14683136 | tf_op jit(solution)/shard_map/reduce_sum | solution.py:119
  47.0 1.6 %collective-permute-start.1 = (f32[6,128]{1,0:T(8,128)S(1)}, f32[6,128]{1,0:T(8,128)S(1)}, u32[]{:S(2)}, u32[]{:S(2)}) collective-permute-start(f32[6,128]{1,0:T(8,128)S(1)} %multiply_reduce_fusion), channel_id=1, source_target_pairs={{0,1},{1,0},{2,3},{3,2},{4,5},{5,4},{6,7},{7,6},{8,9},{9,8},{10,11... | collective-permute-start | bytes 9224 | tf_op jit(solution)/shard_map/ppermute | solution.py:14
  48.6 2.9 %fusion.3 = f32[256,256]{1,0:T(8,128)S(1)} fusion(bf16[4096,128]{1,0:T(8,128)(2,1)} %get-tuple-element.10, bf16[4096,128]{1,0:T(8,128)(2,1)} %get-tuple-element.9), kind=kOutput, calls=%fused_computation.6 | convolution fusion | flops 541065216 | bytes 2359296 | tf_op jit(solution)/shard_map/dot_general | solution.py:29
  51.5 0.0 collective-permute-done.2
  51.5 0.7 fusion.12.g_ref
  52.2 16.4 %shard_map.38 = f32[128,128]{1,0:T(8,128)} custom-call(f32[128,128]{1,0:T(8,128)} %fusion.12.g_ref), custom_call_target="tpu_custom_call" | custom-call | tf_op jit(solution)/shard_map/pallas_call | solution.py:104
  68.6 0.0 collective-permute-done.1
  68.6 1.7 %convolution_negate_fusion = f32[6,64]{1,0:T(8,128)} fusion(f32[128,128]{1,0:T(8,128)} %shard_map.38, s32[]{:T(128)S(6)} %select_n.18, f32[6,128]{1,0:T(8,128)S(1)} %multiply_reduce_fusion, f32[6,128]{1,0:T(8,128)S(1)} %collective-permute-done.1), kind=kOutput, calls=%fused_computation.10 | convolution fusion | flops 590976 | bytes 73220 | tf_op jit(solution)/shard_map/dot_general | solution.py:125
  (1 shorter events, 0.0 us)
Async XLA Ops:
  0.0 9.3 %copy-start.3 = (f32[512,128]{1,0:T(8,128)S(1)}, f32[512,128]{1,0:T(8,128)}, u32[]{:S(2)}) copy-start(f32[512,128]{1,0:T(8,128)} %param.5) | copy-start | bytes 786436
  2.1 33.0 %all-to-all-start = ((f32[8,256,128]{2,1,0:T(8,128)}), f32[8,256,128]{2,1,0:T(8,128)S(1)}, u32[]{:S(2)}, u32[]{:S(2)}) async-start(f32[8,256,128]{2,1,0:T(8,128)} %broadcast_in_dim.2), calls=%async_computation | async-start | bytes 2097152 | tf_op jit(solution)/shard_map/all_to_all | solution.py:71
  35.1 1.9 %copy-start.2 = (f32[8,256,128]{2,1,0:T(8,128)}, f32[8,256,128]{2,1,0:T(8,128)S(1)}, u32[]{:S(2)}) copy-start(f32[8,256,128]{2,1,0:T(8,128)S(1)} %all-to-all-done) | copy-start | bytes 3145732
  35.1 2.8 %collective-permute-start = (f32[8,256,128]{2,1,0:T(8,128)S(1)}, f32[8,256,128]{2,1,0:T(8,128)}, u32[]{:S(2)}, u32[]{:S(2)}) collective-permute-start(f32[8,256,128]{2,1,0:T(8,128)S(1)} %all-to-all-done), channel_id=1, source_target_pairs={{0,2},{2,0},{1,3},{3,1},{4,6},{6,4},{5,7},{7,5},{8,10},{10,8},{9,1... | collective-permute-start | bytes 3145736 | tf_op jit(solution)/shard_map/ppermute | solution.py:76
  35.4 16.1 %collective-permute-start.2 = (f32[128,128]{1,0:T(8,128)S(1)}, f32[128,128]{1,0:T(8,128)S(1)}, u32[]{:S(2)}, u32[]{:S(2)}) collective-permute-start(f32[128,128]{1,0:T(8,128)S(1)} %fusion.10), channel_id=1, source_target_pairs={{0,1},{1,0},{2,3},{3,2},{4,5},{5,4},{6,7},{7,6},{8,9},{9,8},{10,11... | collective-permute-start | bytes 196616 | tf_op jit(solution)/shard_map/ppermute | solution.py:14
  37.9 6.7 %copy-start = (f32[24576,128]{1,0:T(8,128)S(1)}, f32[24576,128]{1,0:T(8,128)}, u32[]{:S(2)}) copy-start(f32[24576,128]{1,0:T(8,128)} %shard_map.37) | copy-start | bytes 37748740
  40.0 2.1 %copy-start.1 = (f32[8,2,256,128]{3,2,1,0:T(8,128)}, f32[8,2,256,128]{3,2,1,0:T(8,128)S(1)}, u32[]{:S(2)}) copy-start(f32[8,2,256,128]{3,2,1,0:T(8,128)S(1)} %pad_maximum_fusion) | copy-start | bytes 6291460
  47.0 21.6 %collective-permute-start.1 = (f32[6,128]{1,0:T(8,128)S(1)}, f32[6,128]{1,0:T(8,128)S(1)}, u32[]{:S(2)}, u32[]{:S(2)}) collective-permute-start(f32[6,128]{1,0:T(8,128)S(1)} %multiply_reduce_fusion), channel_id=1, source_target_pairs={{0,1},{1,0},{2,3},{3,2},{4,5},{5,4},{6,7},{7,6},{8,9},{9,8},{10,11... | collective-permute-start | bytes 9224 | tf_op jit(solution)/shard_map/ppermute | solution.py:14

commit v9 on v8

--- a/solution.py
+++ b/solution.py
@@ -65,18 +65,17 @@
     )(flat, pair)
 
 
-def gather_cells(cell_factor, project_first):
+def gather_cells(cell_factor, project_all):
     outer = lax.axis_size("cell_outer")
     spread = jnp.broadcast_to(cell_factor[None], (outer,) + cell_factor.shape)
     mine = lax.all_to_all(spread, "cell_outer", 0, 0, tiled=True)
-    mine, first_part = lax.optimization_barrier((mine, project_first()))
+    mine, projected = lax.optimization_barrier((mine, project_all()))
     core_count = lax.axis_size("cell_core")
     if core_count == 1:
-        return mine.reshape(-1, cell_factor.shape[1]), first_part
+        return [mine], projected
     other = lax.ppermute(mine, "cell_core", [(0, 1), (1, 0)])
     first = lax.axis_index("cell_core") == 0
-    pair = (jnp.where(first, mine, other), jnp.where(first, other, mine))
-    return jnp.stack(pair, axis=1).reshape(-1, cell_factor.shape[1]), first_part
+    return [jnp.where(first, mine, other), jnp.where(first, other, mine)], projected
 
 
 def sweep_kernel(g_ref, o_ref):
@@ -112,12 +111,16 @@
     rows = image_rows * cell_count
     flat = tensor.reshape(rows, bin_count)
     gram_bin = exchange_sum(gram_of(bin_factor), "bin")
-    cell_full, projected = gather_cells(
+    blocks, projected = gather_cells(
         cell_factor, lambda: project(flat, bin_factor, 0, rows)
     )
-    projected = projected.reshape(image_rows, cell_count, rank_cols)
-    mttkrp = jnp.sum(projected * cell_full[None], axis=1)
-    gram = gram_of(cell_full) * gram_bin
+    outer, block_rows = blocks[0].shape[:2]
+    projected = projected.reshape(image_rows, outer, len(blocks), block_rows, rank_cols)
+    mttkrp = sum(
+        jnp.sum(projected[:, :, c] * blocks[c][None], axis=(1, 2)) for c in range(len(blocks))
+    )
+    gram_cell = sum(gram_of(b.reshape(-1, rank_cols)) for b in blocks)
+    gram = gram_cell * gram_bin
     neg_inv = negated_inverse(gram)
     totals = exchange_sum(mttkrp, "bin")
     own_cols = rank_cols // lax.axis_size("bin")

time: 70.7 us -> 65.6 us (0.928)
  local copies, waits for them, and re-layouts: 4.96 us -> 2.01 us
  matrix products: 4.85 us -> 2.9 us
  waiting for transfers between devices: 1.55 us -> 0.82 us
    unnamed x8 -> x0, local copies, waits for them, and re-layouts: 2.91 us -> none
    reduce_sum x1, other arithmetic: 2.41 us -> 5.26 us  [body(): jnp.sum(projected[:, :, c] * blocks[c][None], axis=(1, 2))]
    another operation x2 -> x0, other arithmetic: 2.05 us -> none  [gather_cells(): jnp.stack(pair, axis=1).reshape(-1, cell_factor.shape[1])]
    dot_general x2 -> x3, matrix products: 3.17 us -> 1.22 us  [gram_of(): lax.dot_general(both, both, (((0,), (0,)), ((), ())), preferred_element_t...]
  transfers between devices with their start and end apart: 4 -> 4, of which waited for: 2 -> 1; matrix products, arithmetic and copies ran while one was open for 15% -> 15% of each run, Pallas kernels for 58% -> 63%
where the time goes in v9:
time: 65.6 us; the launch traced here: 65.2 us
  Pallas kernels  40.8 us (62%)
  starting transfers between devices  10.4 us (16%)
  other arithmetic  8.29 us (13%)
  matrix products  2.9 us (4%)
  local copies, waits for them, and re-layouts  2.01 us (3%)
  waiting for transfers between devices  0.82 us (1%)
    pallas_call x1, Pallas kernels, project(): pl.pallas_call(project_kernel, out_shape=jax.ShapeDtypeStruct((rows, rank...  24.3 us
    pallas_call x1, Pallas kernels, negated_inverse(): pl.pallas_call(sweep_kernel, out_shape=jax.ShapeDtypeStruct(gram.shape, j...  16.4 us
    all_to_all x1, starting transfers between devices, gather_cells(): mine = lax.all_to_all(spread, 'cell_outer', 0, 0, tiled=True)  7.28 us
    reduce_sum x1, other arithmetic, body(): jnp.sum(projected[:, :, c] * blocks[c][None], axis=(1, 2))  5.26 us
    ppermute x2, starting transfers between devices, exchange_sum(): value = value + lax.ppermute(value, axis, pairs)  3.11 us
    broadcast_in_dim x1, local copies, waits for them, and re-layouts, gather_cells(): spread = jnp.broadcast_to(cell_factor[None], (outer,) + cell_factor.shape)  2.01 us
    dot_general x1, matrix products, body(): return -jnp.dot(totals, own, precision=lax.Precision.HIGHEST)  1.67 us
    convert_element_type x2, other arithmetic, split_pair(): return (hi.astype(jnp.bfloat16), lo.astype(jnp.bfloat16))  1.44 us
  transfers between devices with their start and end apart: 4, of which 1 were waited for; matrix products, arithmetic and copies ran while one was open for 15% of the time, Pallas kernels for 63%

profile of v9, /device:TPU:0, one launch (start us, length us, event | category | flops | bytes accessed | tf_op | source)
XLA Modules:
  0.0 65.2 jit_solution(2646401915823004699)
XLA Ops:
  0.0 2.0 %broadcast_in_dim.2 = f32[8,256,128]{2,1,0:T(8,128)} broadcast(f32[256,128]{1,0:T(8,128)} %param.4), dimensions={1,2} | broadcast | bytes 1179648 | tf_op jit(solution)/shard_map/broadcast_in_dim | solution.py:70
  2.0 7.3 %all-to-all-start = ((f32[8,256,128]{2,1,0:T(8,128)}), f32[8,256,128]{2,1,0:T(8,128)S(1)}, u32[]{:S(2)}, u32[]{:S(2)}) async-start(f32[8,256,128]{2,1,0:T(8,128)} %broadcast_in_dim.2), calls=%async_computation | async-start | bytes 2097152 | tf_op jit(solution)/shard_map/all_to_all | solution.py:71
  9.3 1.0 %fusion.19 = (bf16[512,128]{1,0:T(8,128)(2,1)S(1)}, bf16[512,128]{1,0:T(8,128)(2,1)S(1)}) fusion(f32[512,128]{1,0:T(8,128)} %param.5), kind=kLoop, calls=%fused_computation.27 | loop fusion | flops 393216 | bytes 524288 | tf_op jit(solution)/shard_map/convert_element_type | solution.py:23
  10.3 0.7 %pad_maximum_fusion.b_ref = bf16[512,256]{1,0:T(8,128)(2,1)} fusion(bf16[512,128]{1,0:T(8,128)(2,1)S(1)} %get-tuple-element.18, bf16[512,128]{1,0:T(8,128)(2,1)S(1)} %get-tuple-element.17), kind=kLoop, calls=%fused_computation.29 | loop fusion | flops 524288 | bytes 524288 | tf_op jit(solution)/shard_map/concatenate | solution.py:50
  11.0 24.3 %shard_map.37 = f32[24576,128]{1,0:T(8,128)} custom-call(f32[24576,512]{1,0:T(8,128)} %bitcast.20, bf16[512,256]{1,0:T(8,128)(2,1)} %pad_maximum_fusion.b_ref), custom_call_target="tpu_custom_call" | custom-call | flops 12884901888 | bytes 62914560 | tf_op jit(solution)/shard_map/pallas_call | solution.py:51
  35.4 0.0 all-to-all-done
  35.4 0.0 collective-permute-start
  35.4 0.3 fusion.31
  35.7 1.6 %collective-permute-start.2 = (f32[128,128]{1,0:T(8,128)S(1)}, f32[128,128]{1,0:T(8,128)S(1)}, u32[]{:S(2)}, u32[]{:S(2)}) collective-permute-start(f32[128,128]{1,0:T(8,128)S(1)} %fusion.21), channel_id=1, source_target_pairs={{0,1},{1,0},{2,3},{3,2},{4,5},{5,4},{6,7},{7,6},{8,9},{9,8},{10,11... | collective-permute-start | bytes 196616 | tf_op jit(solution)/shard_map/ppermute | solution.py:14
  37.2 0.8 %collective-permute-done = f32[8,256,128]{2,1,0:T(8,128)S(1)} collective-permute-done((f32[8,256,128]{2,1,0:T(8,128)S(1)}, f32[8,256,128]{2,1,0:T(8,128)S(1)}, u32[]{:S(2)}, u32[]{:S(2)}) %collective-permute-start) | collective-permute-done | bytes 1048608 | tf_op jit(solution)/shard_map/ppermute | solution.py:76
  38.0 0.2 broadcast_select_fusion.1
  38.2 0.4 fusion.5
  38.6 5.3 %fusion.1 = (f32[6,128]{1,0:T(8,128)S(1)}, f32[6,128]{1,0:T(8,128)S(1)}) fusion(f32[6,8,2,256,128]{4,3,2,1,0:T(8,128)} %bitcast.21, f32[8,256,128]{2,1,0:T(8,128)S(1)} %get-tuple-element.12, f32[8,256,128]{2,1,0:T(8,128)S(1)} %get-tuple-element.11), kind=kLoop, calls=%fused_computation.2 | loop fusion | flops 6289920 | bytes 14686208 | tf_op jit(solution)/shard_map/reduce_sum | solution.py:120
  43.9 1.6 %collective-permute-start.1 = (f32[6,128]{1,0:T(8,128)S(1)}, f32[6,128]{1,0:T(8,128)S(1)}, u32[]{:S(2)}, u32[]{:S(2)}) collective-permute-start(f32[6,128]{1,0:T(8,128)S(1)} %add.42), channel_id=1, source_target_pairs={{0,1},{1,0},{2,3},{3,2},{4,5},{5,4},{6,7},{7,6},{8,9},{9,8},{10,11... | collective-permute-start | bytes 9224 | tf_op jit(solution)/shard_map/ppermute | solution.py:14
  45.5 0.5 fusion.10
  46.0 0.5 fusion.14
  46.5 0.0 collective-permute-done.2
  46.5 0.7 %fusion.24.g_ref = f32[128,128]{1,0:T(8,128)} fusion(f32[256,256]{1,0:T(8,128)S(1)} %fusion.14, f32[256,256]{1,0:T(8,128)S(1)} %fusion.10, f32[128,128]{1,0:T(8,128)S(1)} %collective-permute-done.2, f32[256,256]{1,0:T(8,128)S(1)} %fusion.31), kind=kLoop, calls=%fused_computation.36 | loop fusion | flops 196608 | bytes 917504 | tf_op jit(solution)/shard_map/mul | solution.py:123
  47.1 16.4 %shard_map.38 = f32[128,128]{1,0:T(8,128)} custom-call(f32[128,128]{1,0:T(8,128)} %fusion.24.g_ref), custom_call_target="tpu_custom_call" | custom-call | tf_op jit(solution)/shard_map/pallas_call | solution.py:103
  63.6 0.0 collective-permute-done.1
  63.6 1.7 %convolution_negate_fusion = f32[6,64]{1,0:T(8,128)} fusion(f32[128,128]{1,0:T(8,128)} %shard_map.38, s32[]{:T(128)S(6)} %select_n.18, f32[6,128]{1,0:T(8,128)S(1)} %add.42, f32[6,128]{1,0:T(8,128)S(1)} %collective-permute-done.1), kind=kOutput, calls=%fused_computation.12 | convolution fusion | flops 590976 | bytes 73220 | tf_op jit(solution)/shard_map/dot_general | solution.py:128
  (2 shorter events, 0.0 us)
Async XLA Ops:
  2.0 33.3 %all-to-all-start = ((f32[8,256,128]{2,1,0:T(8,128)}), f32[8,256,128]{2,1,0:T(8,128)S(1)}, u32[]{:S(2)}, u32[]{:S(2)}) async-start(f32[8,256,128]{2,1,0:T(8,128)} %broadcast_in_dim.2), calls=%async_computation | async-start | bytes 2097152 | tf_op jit(solution)/shard_map/all_to_all | solution.py:71
  35.4 2.7 %collective-permute-start = (f32[8,256,128]{2,1,0:T(8,128)S(1)}, f32[8,256,128]{2,1,0:T(8,128)S(1)}, u32[]{:S(2)}, u32[]{:S(2)}) collective-permute-start(f32[8,256,128]{2,1,0:T(8,128)S(1)} %all-to-all-done), channel_id=1, source_target_pairs={{0,2},{2,0},{1,3},{3,1},{4,6},{6,4},{5,7},{7,5},{8,10},{10,8},{9,1... | collective-permute-start | bytes 3145736 | tf_op jit(solution)/shard_map/ppermute | solution.py:76
  35.7 10.8 %collective-permute-start.2 = (f32[128,128]{1,0:T(8,128)S(1)}, f32[128,128]{1,0:T(8,128)S(1)}, u32[]{:S(2)}, u32[]{:S(2)}) collective-permute-start(f32[128,128]{1,0:T(8,128)S(1)} %fusion.21), channel_id=1, source_target_pairs={{0,1},{1,0},{2,3},{3,2},{4,5},{5,4},{6,7},{7,6},{8,9},{9,8},{10,11... | collective-permute-start | bytes 196616 | tf_op jit(solution)/shard_map/ppermute | solution.py:14
  43.9 19.6 %collective-permute-start.1 = (f32[6,128]{1,0:T(8,128)S(1)}, f32[6,128]{1,0:T(8,128)S(1)}, u32[]{:S(2)}, u32[]{:S(2)}) collective-permute-start(f32[6,128]{1,0:T(8,128)S(1)} %add.42), channel_id=1, source_target_pairs={{0,1},{1,0},{2,3},{3,2},{4,5},{5,4},{6,7},{7,6},{8,9},{9,8},{10,11... | collective-permute-start | bytes 9224 | tf_op jit(solution)/shard_map/ppermute | solution.py:14

commit v10 on v9

--- a/solution.py
+++ b/solution.py
@@ -65,17 +65,17 @@
     )(flat, pair)
 
 
-def gather_cells(cell_factor, project_all):
+def gather_cells(cell_factor, early_work):
     outer = lax.axis_size("cell_outer")
     spread = jnp.broadcast_to(cell_factor[None], (outer,) + cell_factor.shape)
     mine = lax.all_to_all(spread, "cell_outer", 0, 0, tiled=True)
-    mine, projected = lax.optimization_barrier((mine, project_all()))
+    mine, early = lax.optimization_barrier((mine, early_work()))
     core_count = lax.axis_size("cell_core")
     if core_count == 1:
-        return [mine], projected
+        return [mine], early
     other = lax.ppermute(mine, "cell_core", [(0, 1), (1, 0)])
     first = lax.axis_index("cell_core") == 0
-    return [jnp.where(first, mine, other), jnp.where(first, other, mine)], projected
+    return [jnp.where(first, mine, other), jnp.where(first, other, mine)], early
 
 
 def sweep_kernel(g_ref, o_ref):
@@ -110,9 +110,9 @@
     rank_cols = bin_factor.shape[1]
     rows = image_rows * cell_count
     flat = tensor.reshape(rows, bin_count)
-    gram_bin = exchange_sum(gram_of(bin_factor), "bin")
-    blocks, projected = gather_cells(
-        cell_factor, lambda: project(flat, bin_factor, 0, rows)
+    blocks, (projected, gram_bin) = gather_cells(
+        cell_factor,
+        lambda: (project(flat, bin_factor, 0, rows), exchange_sum(gram_of(bin_factor), "bin")),
     )
     outer, block_rows = blocks[0].shape[:2]
     projected = projected.reshape(image_rows, outer, len(blocks), block_rows, rank_cols)

time: 65.6 us -> 66.6 us (1.015)
  waiting for transfers between devices: 0.82 us -> 2.65 us
  starting transfers between devices: 10.4 us -> 9.51 us
    ppermute x1, waiting for transfers between devices: 0.81 us -> 2.64 us  [gather_cells(): other = lax.ppermute(mine, 'cell_core', [(0, 1), (1, 0)])]
    ppermute x2, starting transfers between devices: 3.11 us -> 2.16 us  [exchange_sum(): value = value + lax.ppermute(value, axis, pairs)]
  transfers between devices with their start and end apart: 4 -> 4, of which waited for: 1 -> 1; matrix products, arithmetic and copies ran while one was open for 15% -> 6% of each run, Pallas kernels for 63% -> 62%
where the time goes in v10:
time: 66.6 us; the launch traced here: 66.2 us
  Pallas kernels  40.8 us (61%)
  starting transfers between devices  9.51 us (14%)
  other arithmetic  8.29 us (12%)
  matrix products  2.9 us (4%)
  waiting for transfers between devices  2.65 us (4%)
  local copies, waits for them, and re-layouts  2.01 us (3%)
    pallas_call x1, Pallas kernels, project(): pl.pallas_call(project_kernel, out_shape=jax.ShapeDtypeStruct((rows, rank...  24.3 us
    pallas_call x1, Pallas kernels, negated_inverse(): pl.pallas_call(sweep_kernel, out_shape=jax.ShapeDtypeStruct(gram.shape, j...  16.4 us
    all_to_all x1, starting transfers between devices, gather_cells(): mine = lax.all_to_all(spread, 'cell_outer', 0, 0, tiled=True)  7.28 us
    reduce_sum x1, other arithmetic, body(): jnp.sum(projected[:, :, c] * blocks[c][None], axis=(1, 2))  5.26 us
    ppermute x1, waiting for transfers between devices, gather_cells(): other = lax.ppermute(mine, 'cell_core', [(0, 1), (1, 0)])  2.64 us
    ppermute x2, starting transfers between devices, exchange_sum(): value = value + lax.ppermute(value, axis, pairs)  2.16 us
    broadcast_in_dim x1, local copies, waits for them, and re-layouts, gather_cells(): spread = jnp.broadcast_to(cell_factor[None], (outer,) + cell_factor.shape)  2.01 us
    dot_general x1, matrix products, body(): return -jnp.dot(totals, own, precision=lax.Precision.HIGHEST)  1.67 us
  transfers between devices with their start and end apart: 4, of which 1 were waited for; matrix products, arithmetic and copies ran while one was open for 6% of the time, Pallas kernels for 62%

profile of v10, /device:TPU:0, one launch (start us, length us, event | category | flops | bytes accessed | tf_op | source)
XLA Modules:
  0.0 66.2 jit_solution(10642751787104589884)
XLA Ops:
  0.0 2.0 %broadcast_in_dim.2 = f32[8,256,128]{2,1,0:T(8,128)} broadcast(f32[256,128]{1,0:T(8,128)} %param.4), dimensions={1,2} | broadcast | bytes 1179648 | tf_op jit(solution)/shard_map/broadcast_in_dim | solution.py:70
  2.0 7.3 %all-to-all-start = ((f32[8,256,128]{2,1,0:T(8,128)}), f32[8,256,128]{2,1,0:T(8,128)S(1)}, u32[]{:S(2)}, u32[]{:S(2)}) async-start(f32[8,256,128]{2,1,0:T(8,128)} %broadcast_in_dim.2), calls=%async_computation | async-start | bytes 2097152 | tf_op jit(solution)/shard_map/all_to_all | solution.py:71
  9.3 1.0 %fusion.19 = (bf16[512,128]{1,0:T(8,128)(2,1)S(1)}, bf16[512,128]{1,0:T(8,128)(2,1)S(1)}) fusion(f32[512,128]{1,0:T(8,128)} %param.5), kind=kLoop, calls=%fused_computation.27 | loop fusion | flops 393216 | bytes 524288 | tf_op jit(solution)/shard_map/convert_element_type | solution.py:23
  10.3 0.3 fusion.31
  10.6 1.6 %collective-permute-start = (f32[128,128]{1,0:T(8,128)S(1)}, f32[128,128]{1,0:T(8,128)S(1)}, u32[]{:S(2)}, u32[]{:S(2)}) collective-permute-start(f32[128,128]{1,0:T(8,128)S(1)} %fusion.25), channel_id=1, source_target_pairs={{0,1},{1,0},{2,3},{3,2},{4,5},{5,4},{6,7},{7,6},{8,9},{9,8},{10,11... | collective-permute-start | bytes 196616 | tf_op jit(solution)/shard_map/ppermute | solution.py:14
  12.1 0.7 %pad_maximum_fusion.b_ref = bf16[512,256]{1,0:T(8,128)(2,1)} fusion(bf16[512,128]{1,0:T(8,128)(2,1)S(1)} %get-tuple-element.20, bf16[512,128]{1,0:T(8,128)(2,1)S(1)} %get-tuple-element.19), kind=kLoop, calls=%fused_computation.29 | loop fusion | flops 524288 | bytes 524288 | tf_op jit(solution)/shard_map/concatenate | solution.py:50
  12.9 24.3 %shard_map.37 = f32[24576,128]{1,0:T(8,128)} custom-call(f32[24576,512]{1,0:T(8,128)} %bitcast.20, bf16[512,256]{1,0:T(8,128)(2,1)} %pad_maximum_fusion.b_ref), custom_call_target="tpu_custom_call" | custom-call | flops 12884901888 | bytes 62914560 | tf_op jit(solution)/shard_map/pallas_call | solution.py:51
  37.2 0.0 collective-permute-done
  37.2 0.0 all-to-all-done
  37.2 0.1 collective-permute-start.1
  37.3 2.6 %collective-permute-done.1 = f32[8,256,128]{2,1,0:T(8,128)S(1)} collective-permute-done((f32[8,256,128]{2,1,0:T(8,128)S(1)}, f32[8,256,128]{2,1,0:T(8,128)S(1)}, u32[]{:S(2)}, u32[]{:S(2)}) %collective-permute-start.1) | collective-permute-done | bytes 1048608 | tf_op jit(solution)/shard_map/ppermute | solution.py:76
  40.0 0.2 broadcast_select_fusion.1
  40.1 0.4 fusion.5
  40.6 5.3 %fusion.1 = (f32[6,128]{1,0:T(8,128)S(1)}, f32[6,128]{1,0:T(8,128)S(1)}) fusion(f32[6,8,2,256,128]{4,3,2,1,0:T(8,128)} %bitcast.21, f32[8,256,128]{2,1,0:T(8,128)S(1)} %get-tuple-element.14, f32[8,256,128]{2,1,0:T(8,128)S(1)} %get-tuple-element.13), kind=kLoop, calls=%fused_computation.2 | loop fusion | flops 6289920 | bytes 14686208 | tf_op jit(solution)/shard_map/reduce_sum | solution.py:120
  45.9 0.6 collective-permute-start.2
  46.5 0.5 fusion.10
  47.0 0.5 fusion.14
  47.5 0.6 fusion.23.g_ref
  48.1 16.4 %shard_map.38 = f32[128,128]{1,0:T(8,128)} custom-call(f32[128,128]{1,0:T(8,128)} %fusion.23.g_ref), custom_call_target="tpu_custom_call" | custom-call | tf_op jit(solution)/shard_map/pallas_call | solution.py:103
  64.5 0.0 collective-permute-done.2
  64.5 1.7 %convolution_negate_fusion = f32[6,64]{1,0:T(8,128)} fusion(f32[128,128]{1,0:T(8,128)} %shard_map.38, s32[]{:T(128)S(6)} %select_n.18, f32[6,128]{1,0:T(8,128)S(1)} %add.46, f32[6,128]{1,0:T(8,128)S(1)} %collective-permute-done.2), kind=kOutput, calls=%fused_computation.12 | convolution fusion | flops 590976 | bytes 73220 | tf_op jit(solution)/shard_map/dot_general | solution.py:128
  (3 shorter events, 0.0 us)
Async XLA Ops:
  2.0 35.2 %all-to-all-start = ((f32[8,256,128]{2,1,0:T(8,128)}), f32[8,256,128]{2,1,0:T(8,128)S(1)}, u32[]{:S(2)}, u32[]{:S(2)}) async-start(f32[8,256,128]{2,1,0:T(8,128)} %broadcast_in_dim.2), calls=%async_computation | async-start | bytes 2097152 | tf_op jit(solution)/shard_map/all_to_all | solution.py:71
  10.6 26.6 %collective-permute-start = (f32[128,128]{1,0:T(8,128)S(1)}, f32[128,128]{1,0:T(8,128)S(1)}, u32[]{:S(2)}, u32[]{:S(2)}) collective-permute-start(f32[128,128]{1,0:T(8,128)S(1)} %fusion.25), channel_id=1, source_target_pairs={{0,1},{1,0},{2,3},{3,2},{4,5},{5,4},{6,7},{7,6},{8,9},{9,8},{10,11... | collective-permute-start | bytes 196616 | tf_op jit(solution)/shard_map/ppermute | solution.py:14
  37.2 2.7 %collective-permute-start.1 = (f32[8,256,128]{2,1,0:T(8,128)S(1)}, f32[8,256,128]{2,1,0:T(8,128)S(1)}, u32[]{:S(2)}, u32[]{:S(2)}) collective-permute-start(f32[8,256,128]{2,1,0:T(8,128)S(1)} %all-to-all-done), channel_id=1, source_target_pairs={{0,2},{2,0},{1,3},{3,1},{4,6},{6,4},{5,7},{7,5},{8,10},{10,8},{9,1... | collective-permute-start | bytes 3145736 | tf_op jit(solution)/shard_map/ppermute | solution.py:76
  45.9 18.7 %collective-permute-start.2 = (f32[6,128]{1,0:T(8,128)S(1)}, f32[6,128]{1,0:T(8,128)S(1)}, u32[]{:S(2)}, u32[]{:S(2)}) collective-permute-start(f32[6,128]{1,0:T(8,128)S(1)} %add.46), channel_id=1, source_target_pairs={{0,1},{1,0},{2,3},{3,2},{4,5},{5,4},{6,7},{7,6},{8,9},{9,8},{10,11... | collective-permute-start | bytes 9224 | tf_op jit(solution)/shard_map/ppermute | solution.py:14

commit v11 on v9

--- a/solution.py
+++ b/solution.py
@@ -105,6 +105,64 @@
     )(gram)
 
 
+def fused_kernel(g_ref, p_ref, x0_ref, x1_ref, o_ref, m_ref, a_ref):
+    o = pl.program_id(0)
+    n = g_ref.shape[0]
+    share = n // pl.num_programs(0)
+    sub = lax.broadcasted_iota(jnp.int32, (n, n), 0)
+    lane = lax.broadcasted_iota(jnp.int32, (n, n), 1)
+
+    @pl.when(o == 0)
+    def _():
+        a_ref[...] = g_ref[...]
+        m_ref[...] = jnp.zeros_like(m_ref)
+
+    def step(s, a):
+        k = o * share + s
+        on_row = sub == k
+        on_col = lane == k
+        row = jnp.sum(jnp.where(on_row, a, 0.0), axis=0, keepdims=True)
+        col = jnp.sum(jnp.where(on_col, a, 0.0), axis=1, keepdims=True)
+        pivot = jnp.sum(jnp.where(on_col[:1], row, 0.0), axis=1, keepdims=True)
+        inv = 1.0 / pivot
+        scaled_row = row * inv
+        upd = a - col * scaled_row
+        upd = jnp.where(on_col, col * inv, upd)
+        upd = jnp.where(on_row, scaled_row, upd)
+        return jnp.where(on_row & on_col, -inv, upd)
+
+    a_ref[...] = lax.fori_loop(0, share, step, a_ref[...], unroll=8)
+    p = p_ref[...]
+    m_ref[...] += jnp.sum(p[:, 0, 0] * x0_ref[...], axis=1) + jnp.sum(
+        p[:, 0, 1] * x1_ref[...], axis=1
+    )
+    o_ref[...] = a_ref[...]
+
+
+def fused_solve_parts(gram, projected, x0, x1):
+    images, outer, _, rows, rank = projected.shape
+    n = gram.shape[0]
+    return pl.pallas_call(
+        fused_kernel,
+        out_shape=(
+            jax.ShapeDtypeStruct(gram.shape, jnp.float32),
+            jax.ShapeDtypeStruct((images, rank), jnp.float32),
+        ),
+        grid=(outer,),
+        in_specs=[
+            pl.BlockSpec((n, n), lambda o: (0, 0)),
+            pl.BlockSpec((images, 1, 2, rows, rank), lambda o: (0, o, 0, 0, 0)),
+            pl.BlockSpec((1, rows, rank), lambda o: (o, 0, 0)),
+            pl.BlockSpec((1, rows, rank), lambda o: (o, 0, 0)),
+        ],
+        out_specs=(
+            pl.BlockSpec((n, n), lambda o: (0, 0)),
+            pl.BlockSpec((images, rank), lambda o: (0, 0)),
+        ),
+        scratch_shapes=[pltpu.VMEM((n, n), jnp.float32)],
+    )(gram, projected, x0, x1)
+
+
 def body(tensor, cell_factor, bin_factor):
     image_rows, cell_count, bin_count = tensor.shape
     rank_cols = bin_factor.shape[1]
@@ -116,12 +174,16 @@
     )
     outer, block_rows = blocks[0].shape[:2]
     projected = projected.reshape(image_rows, outer, len(blocks), block_rows, rank_cols)
-    mttkrp = sum(
-        jnp.sum(projected[:, :, c] * blocks[c][None], axis=(1, 2)) for c in range(len(blocks))
-    )
     gram_cell = sum(gram_of(b.reshape(-1, rank_cols)) for b in blocks)
     gram = gram_cell * gram_bin
-    neg_inv = negated_inverse(gram)
+    if len(blocks) == 2 and rank_cols % outer == 0:
+        neg_inv, mttkrp = fused_solve_parts(gram, projected, blocks[0], blocks[1])
+    else:
+        mttkrp = sum(
+            jnp.sum(projected[:, :, c] * blocks[c][None], axis=(1, 2))
+            for c in range(len(blocks))
+        )
+        neg_inv = negated_inverse(gram)
     totals = exchange_sum(mttkrp, "bin")
     own_cols = rank_cols // lax.axis_size("bin")
     own = lax.dynamic_slice_in_dim(neg_inv, lax.axis_index("bin") * own_cols, own_cols, 1)

time: 65.6 us -> 66.6 us (1.015)
  other arithmetic: 8.29 us -> 3.3 us
  waiting for transfers between devices: 0.82 us -> 3.9 us
  Pallas kernels: 40.8 us -> 42.8 us
  local copies, waits for them, and re-layouts: 2.01 us -> 2.93 us
    reduce_sum x1 -> x0, other arithmetic: 5.26 us -> none  [body(): jnp.sum(projected[:, :, c] * blocks[c][None], axis=(1, 2))]
    ppermute x2, waiting for transfers between devices: 0.01 us -> 2.33 us  [exchange_sum(): value = value + lax.ppermute(value, axis, pairs)]
    pallas_call x1, Pallas kernels: 16.4 us -> 18.5 us  [fused_solve_parts(): pl.pallas_call(fused_kernel, out_shape=(jax.ShapeDtypeStruct(gram.shape,...]
    select_n x1, other arithmetic: 0.17 us -> 1.4 us  [gather_cells(): jnp.where(first, mine, other)]
    convert_element_type x2, other arithmetic: 1.44 us -> 0.5 us  [split_pair(): return (hi.astype(jnp.bfloat16), lo.astype(jnp.bfloat16))]
    unnamed x0 -> x6, local copies, waits for them, and re-layouts: none -> 0.87 us
  transfers between devices with their start and end apart: 4 -> 4, of which waited for: 1 -> 3; matrix products, arithmetic and copies ran while one was open for 15% -> 6% of each run, Pallas kernels for 63% -> 37%
where the time goes in v11:
time: 66.6 us; the launch traced here: 66.3 us
  Pallas kernels  42.8 us (64%)
  starting transfers between devices  10.3 us (15%)
  waiting for transfers between devices  3.9 us (6%)
  other arithmetic  3.3 us (5%)
  local copies, waits for them, and re-layouts  2.93 us (4%)
  matrix products  2.9 us (4%)
    pallas_call x1, Pallas kernels, project(): pl.pallas_call(project_kernel, out_shape=jax.ShapeDtypeStruct((rows, rank...  24.3 us
    pallas_call x1, Pallas kernels, fused_solve_parts(): pl.pallas_call(fused_kernel, out_shape=(jax.ShapeDtypeStruct(gram.shape,...  18.5 us
    all_to_all x1, starting transfers between devices, gather_cells(): mine = lax.all_to_all(spread, 'cell_outer', 0, 0, tiled=True)  7.28 us
    ppermute x2, starting transfers between devices, exchange_sum(): value = value + lax.ppermute(value, axis, pairs)  3.05 us
    ppermute x2, waiting for transfers between devices, exchange_sum(): value = value + lax.ppermute(value, axis, pairs)  2.33 us
    broadcast_in_dim x1, local copies, waits for them, and re-layouts, gather_cells(): spread = jnp.broadcast_to(cell_factor[None], (outer,) + cell_factor.shape)  2.06 us
    dot_general x1, matrix products, body(): return -jnp.dot(totals, own, precision=lax.Precision.HIGHEST)  1.68 us
    select_n x1, other arithmetic, gather_cells(): jnp.where(first, mine, other)  1.4 us
  transfers between devices with their start and end apart: 4, of which 3 were waited for; matrix products, arithmetic and copies ran while one was open for 6% of the time, Pallas kernels for 37%

profile of v11, /device:TPU:0, one launch (start us, length us, event | category | flops | bytes accessed | tf_op | source)
XLA Modules:
  0.0 66.3 jit_solution(2256525727607285823)
XLA Ops:
  0.0 0.0 copy-start.2
  0.0 2.1 %broadcast_in_dim.2 = f32[8,256,128]{2,1,0:T(8,128)} broadcast(f32[256,128]{1,0:T(8,128)} %param.4), dimensions={1,2} | broadcast | bytes 1179648 | tf_op jit(solution)/shard_map/broadcast_in_dim | solution.py:70
  2.1 7.3 %all-to-all-start = ((f32[8,256,128]{2,1,0:T(8,128)}), f32[8,256,128]{2,1,0:T(8,128)S(1)}, u32[]{:S(2)}, u32[]{:S(2)}) async-start(f32[8,256,128]{2,1,0:T(8,128)} %broadcast_in_dim.2), calls=%async_computation | async-start | bytes 2097152 | tf_op jit(solution)/shard_map/all_to_all | solution.py:71
  9.3 0.0 copy-done.2
  9.4 0.1 fusion.15
  9.4 0.7 %pad_maximum_fusion.b_ref = bf16[512,256]{1,0:T(8,128)(2,1)} fusion(bf16[512,128]{1,0:T(8,128)(2,1)S(1)} %get-tuple-element.20, bf16[512,128]{1,0:T(8,128)(2,1)S(1)} %get-tuple-element.19), kind=kLoop, calls=%fused_computation.23 | loop fusion | flops 524288 | bytes 524288 | tf_op jit(solution)/shard_map/concatenate | solution.py:50
  10.1 24.3 %shard_map.37 = f32[24576,128]{1,0:T(8,128)} custom-call(f32[24576,512]{1,0:T(8,128)} %bitcast.8, bf16[512,256]{1,0:T(8,128)(2,1)} %pad_maximum_fusion.b_ref), custom_call_target="tpu_custom_call" | custom-call | flops 12884901888 | bytes 62914560 | tf_op jit(solution)/shard_map/pallas_call | solution.py:51
  34.5 0.6 all-to-all-done
  35.1 0.0 collective-permute-start
  35.1 0.3 fusion.27
  35.4 1.6 %collective-permute-start.1 = (f32[128,128]{1,0:T(8,128)S(1)}, f32[128,128]{1,0:T(8,128)S(1)}, u32[]{:S(2)}, u32[]{:S(2)}) collective-permute-start(f32[128,128]{1,0:T(8,128)S(1)} %fusion.17), channel_id=1, source_target_pairs={{0,1},{1,0},{2,3},{3,2},{4,5},{5,4},{6,7},{7,6},{8,9},{9,8},{10,11... | collective-permute-start | bytes 196616 | tf_op jit(solution)/shard_map/ppermute | solution.py:14
  37.0 0.9 %collective-permute-done = f32[8,256,128]{2,1,0:T(8,128)} collective-permute-done((f32[8,256,128]{2,1,0:T(8,128)S(1)}, f32[8,256,128]{2,1,0:T(8,128)}, u32[]{:S(2)}, u32[]{:S(2)}) %collective-permute-start) | collective-permute-done | bytes 1048608 | tf_op jit(solution)/shard_map/ppermute | solution.py:76
  37.9 1.4 %broadcast_select_fusion.1 = (f32[8,256,128]{2,1,0:T(8,128)S(1)}, f32[8,256,128]{2,1,0:T(8,128)S(1)}) fusion(f32[8,256,128]{2,1,0:T(8,128)S(1)} %all-to-all-done, f32[8,256,128]{2,1,0:T(8,128)} %collective-permute-done, pred[]{:T(512)S(6)} %eq.3), kind=kLoop, calls=%fused_computation.18 | loop fusion | flops 524288 | bytes 4194305 | tf_op jit(solution)/shard_map/jit(_where)/select_n | solution.py:78
  39.3 0.0 copy-start
  39.3 0.0 copy-start.1
  39.3 0.4 fusion.1
  39.8 0.6 copy-done
  40.4 0.3 copy-done.1
  40.6 0.5 fusion.6
  41.1 0.5 fusion.10
  41.6 0.0 collective-permute-done.1
  41.6 0.7 %fusion.20.g_ref = f32[128,128]{1,0:T(8,128)} fusion(f32[256,256]{1,0:T(8,128)S(1)} %fusion.10, f32[256,256]{1,0:T(8,128)S(1)} %fusion.6, f32[128,128]{1,0:T(8,128)S(1)} %collective-permute-done.1, f32[256,256]{1,0:T(8,128)S(1)} %fusion.27), kind=kLoop, calls=%fused_computation.30 | loop fusion | flops 196608 | bytes 917504 | tf_op jit(solution)/shard_map/mul | solution.py:178
  42.3 18.5 %shard_map.38 = (f32[128,128]{1,0:T(8,128)}, f32[6,128]{1,0:T(8,128)}) custom-call(f32[128,128]{1,0:T(8,128)} %fusion.20.g_ref, f32[6,8,2,256,128]{4,3,2,1,0:T(8,128)} %bitcast.9, f32[8,256,128]{2,1,0:T(8,128)} %copy-done, f32[8,256,128]{2,1,0:T(8,128)} %copy-done.1), custom_call_target="tpu_custom_call" | custom-call | tf_op jit(solution)/shard_map/pallas_call | solution.py:145
  60.8 1.5 %collective-permute-start.2 = (f32[6,128]{1,0:T(8,128)}, f32[6,128]{1,0:T(8,128)S(1)}, u32[]{:S(2)}, u32[]{:S(2)}) collective-permute-start(f32[6,128]{1,0:T(8,128)} %get-tuple-element.11), channel_id=1, source_target_pairs={{0,1},{1,0},{2,3},{3,2},{4,5},{5,4},{6,7},{7,6},{8,9},{9,8},{10,11... | collective-permute-start | bytes 9224 | tf_op jit(solution)/shard_map/ppermute | solution.py:14
  62.3 2.3 %collective-permute-done.2 = f32[6,128]{1,0:T(8,128)S(1)} collective-permute-done((f32[6,128]{1,0:T(8,128)}, f32[6,128]{1,0:T(8,128)S(1)}, u32[]{:S(2)}, u32[]{:S(2)}) %collective-permute-start.2) | collective-permute-done | bytes 3104 | tf_op jit(solution)/shard_map/ppermute | solution.py:14
  64.6 1.7 %convolution_negate_fusion = f32[6,64]{1,0:T(8,128)} fusion(f32[128,128]{1,0:T(8,128)} %get-tuple-element.12, s32[]{:T(128)S(6)} %select_n.18, f32[6,128]{1,0:T(8,128)} %get-tuple-element.11, f32[6,128]{1,0:T(8,128)S(1)} %collective-permute-done.2), kind=kOutput, calls=%fused_computation.6 | convolution fusion | flops 590976 | bytes 73220 | tf_op jit(solution)/shard_map/dot_general | solution.py:190
  (1 shorter events, 0.0 us)
Async XLA Ops:
  0.0 9.4 %copy-start.2 = (f32[512,128]{1,0:T(8,128)S(1)}, f32[512,128]{1,0:T(8,128)}, u32[]{:S(2)}) copy-start(f32[512,128]{1,0:T(8,128)} %param.5) | copy-start | bytes 786436
  2.1 33.0 %all-to-all-start = ((f32[8,256,128]{2,1,0:T(8,128)}), f32[8,256,128]{2,1,0:T(8,128)S(1)}, u32[]{:S(2)}, u32[]{:S(2)}) async-start(f32[8,256,128]{2,1,0:T(8,128)} %broadcast_in_dim.2), calls=%async_computation | async-start | bytes 2097152 | tf_op jit(solution)/shard_map/all_to_all | solution.py:71
  35.1 2.8 %collective-permute-start = (f32[8,256,128]{2,1,0:T(8,128)S(1)}, f32[8,256,128]{2,1,0:T(8,128)}, u32[]{:S(2)}, u32[]{:S(2)}) collective-permute-start(f32[8,256,128]{2,1,0:T(8,128)S(1)} %all-to-all-done), channel_id=1, source_target_pairs={{0,2},{2,0},{1,3},{3,1},{4,6},{6,4},{5,7},{7,5},{8,10},{10,8},{9,1... | collective-permute-start | bytes 3145736 | tf_op jit(solution)/shard_map/ppermute | solution.py:76
  35.4 6.2 %collective-permute-start.1 = (f32[128,128]{1,0:T(8,128)S(1)}, f32[128,128]{1,0:T(8,128)S(1)}, u32[]{:S(2)}, u32[]{:S(2)}) collective-permute-start(f32[128,128]{1,0:T(8,128)S(1)} %fusion.17), channel_id=1, source_target_pairs={{0,1},{1,0},{2,3},{3,2},{4,5},{5,4},{6,7},{7,6},{8,9},{9,8},{10,11... | collective-permute-start | bytes 196616 | tf_op jit(solution)/shard_map/ppermute | solution.py:14
  39.3 1.1 %copy-start = (f32[8,256,128]{2,1,0:T(8,128)}, f32[8,256,128]{2,1,0:T(8,128)S(1)}, u32[]{:S(2)}) copy-start(f32[8,256,128]{2,1,0:T(8,128)S(1)} %get-tuple-element.13.x0_ref) | copy-start | bytes 3145732
  39.3 1.3 %copy-start.1 = (f32[8,256,128]{2,1,0:T(8,128)}, f32[8,256,128]{2,1,0:T(8,128)S(1)}, u32[]{:S(2)}) copy-start(f32[8,256,128]{2,1,0:T(8,128)S(1)} %get-tuple-element.14.x1_ref) | copy-start | bytes 3145732
  60.8 3.8 %collective-permute-start.2 = (f32[6,128]{1,0:T(8,128)}, f32[6,128]{1,0:T(8,128)S(1)}, u32[]{:S(2)}, u32[]{:S(2)}) collective-permute-start(f32[6,128]{1,0:T(8,128)} %get-tuple-element.11), channel_id=1, source_target_pairs={{0,1},{1,0},{2,3},{3,2},{4,5},{5,4},{6,7},{7,6},{8,9},{9,8},{10,11... | collective-permute-start | bytes 9224 | tf_op jit(solution)/shard_map/ppermute | solution.py:14

commit v12 on v10

--- a/solution.py
+++ b/solution.py
@@ -1,3 +1,5 @@
+import functools
+
 import jax
 import jax.numpy as jnp
 from jax import lax
@@ -70,20 +72,19 @@
     spread = jnp.broadcast_to(cell_factor[None], (outer,) + cell_factor.shape)
     mine = lax.all_to_all(spread, "cell_outer", 0, 0, tiled=True)
     mine, early = lax.optimization_barrier((mine, early_work()))
-    core_count = lax.axis_size("cell_core")
-    if core_count == 1:
-        return [mine], early
+    if lax.axis_size("cell_core") == 1:
+        return mine, None, early
     other = lax.ppermute(mine, "cell_core", [(0, 1), (1, 0)])
-    first = lax.axis_index("cell_core") == 0
-    return [jnp.where(first, mine, other), jnp.where(first, other, mine)], early
-
-
-def sweep_kernel(g_ref, o_ref):
-    n = g_ref.shape[0]
+    return mine, other, early
+
+
+def sweep_steps(a, first, count):
+    n = a.shape[0]
     sub = lax.broadcasted_iota(jnp.int32, (n, n), 0)
     lane = lax.broadcasted_iota(jnp.int32, (n, n), 1)
 
-    def step(k, a):
+    def step(s, a):
+        k = first + s
         on_row = sub == k
         on_col = lane == k
         row = jnp.sum(jnp.where(on_row, a, 0.0), axis=0, keepdims=True)
@@ -96,13 +97,64 @@
         upd = jnp.where(on_row, scaled_row, upd)
         return jnp.where(on_row & on_col, -inv, upd)
 
-    o_ref[...] = lax.fori_loop(0, n, step, g_ref[...], unroll=8)
-
-
-def negated_inverse(gram):
+    return lax.fori_loop(0, count, step, a, unroll=8)
+
+
+def sweep_kernel(first, g_ref, o_ref):
+    o_ref[...] = sweep_steps(g_ref[...], first, g_ref.shape[0] - first)
+
+
+def sweep_rest(a, first):
     return pl.pallas_call(
-        sweep_kernel, out_shape=jax.ShapeDtypeStruct(gram.shape, jnp.float32)
-    )(gram)
+        functools.partial(sweep_kernel, first),
+        out_shape=jax.ShapeDtypeStruct(a.shape, jnp.float32),
+    )(a)
+
+
+def fused_kernel(core_ref, g_ref, pm_ref, po_ref, xm_ref, xo_ref, o_ref, m_ref, a_ref):
+    o = pl.program_id(0)
+    share = g_ref.shape[0] // (2 * pl.num_programs(0))
+
+    @pl.when(o == 0)
+    def _():
+        a_ref[...] = g_ref[...]
+        m_ref[...] = jnp.zeros_like(m_ref)
+
+    a_ref[...] = sweep_steps(a_ref[...], o * share, share)
+    m_ref[...] += jnp.sum(pm_ref[:, 0, 0] * xm_ref[...], axis=1) + jnp.sum(
+        po_ref[:, 0, 0] * xo_ref[...], axis=1
+    )
+    o_ref[...] = a_ref[...]
+
+
+def fused_half(gram, projected, mine, other, core):
+    images, outer, _, rows, rank = projected.shape
+    n = gram.shape[0]
+    p_block = (images, 1, 1, rows, rank)
+    grid_spec = pltpu.PrefetchScalarGridSpec(
+        num_scalar_prefetch=1,
+        grid=(outer,),
+        in_specs=[
+            pl.BlockSpec((n, n), lambda o, c: (0, 0)),
+            pl.BlockSpec(p_block, lambda o, c: (0, o, c[0], 0, 0)),
+            pl.BlockSpec(p_block, lambda o, c: (0, o, 1 - c[0], 0, 0)),
+            pl.BlockSpec((1, rows, rank), lambda o, c: (o, 0, 0)),
+            pl.BlockSpec((1, rows, rank), lambda o, c: (o, 0, 0)),
+        ],
+        out_specs=(
+            pl.BlockSpec((n, n), lambda o, c: (0, 0)),
+            pl.BlockSpec((images, rank), lambda o, c: (0, 0)),
+        ),
+        scratch_shapes=[pltpu.VMEM((n, n), jnp.float32)],
+    )
+    return pl.pallas_call(
+        fused_kernel,
+        out_shape=(
+            jax.ShapeDtypeStruct(gram.shape, jnp.float32),
+            jax.ShapeDtypeStruct((images, rank), jnp.float32),
+        ),
+        grid_spec=grid_spec,
+    )(core, gram, projected, projected, mine, other)
 
 
 def body(tensor, cell_factor, bin_factor):
@@ -110,18 +162,30 @@
     rank_cols = bin_factor.shape[1]
     rows = image_rows * cell_count
     flat = tensor.reshape(rows, bin_count)
-    blocks, (projected, gram_bin) = gather_cells(
-        cell_factor,
-        lambda: (project(flat, bin_factor, 0, rows), exchange_sum(gram_of(bin_factor), "bin")),
-    )
-    outer, block_rows = blocks[0].shape[:2]
-    projected = projected.reshape(image_rows, outer, len(blocks), block_rows, rank_cols)
-    mttkrp = sum(
-        jnp.sum(projected[:, :, c] * blocks[c][None], axis=(1, 2)) for c in range(len(blocks))
-    )
+    gram_bin = exchange_sum(gram_of(bin_factor), "bin")
+    mine, other, projected = gather_cells(
+        cell_factor, lambda: project(flat, bin_factor, 0, rows)
+    )
+    outer, block_rows = mine.shape[:2]
+    blocks = [mine] if other is None else [mine, other]
     gram_cell = sum(gram_of(b.reshape(-1, rank_cols)) for b in blocks)
     gram = gram_cell * gram_bin
-    neg_inv = negated_inverse(gram)
+    half = rank_cols // 2
+    projected = projected.reshape(image_rows, outer, len(blocks), block_rows, rank_cols)
+    if other is not None and half % outer == 0:
+        core = lax.axis_index("cell_core").astype(jnp.int32).reshape(1)
+        partial, mttkrp = fused_half(gram, projected, mine, other, core)
+        neg_inv = sweep_rest(partial, half)
+    else:
+        if other is None:
+            mttkrp = jnp.sum(projected[:, :, 0] * mine[None], axis=(1, 2))
+        else:
+            first = lax.axis_index("cell_core") == 0
+            x0, x1 = jnp.where(first, mine, other), jnp.where(first, other, mine)
+            mttkrp = jnp.sum(projected[:, :, 0] * x0[None], axis=(1, 2)) + jnp.sum(
+                projected[:, :, 1] * x1[None], axis=(1, 2)
+            )
+        neg_inv = sweep_rest(gram, 0)
     totals = exchange_sum(mttkrp, "bin")
     own_cols = rank_cols // lax.axis_size("bin")
     own = lax.dynamic_slice_in_dim(neg_inv, lax.axis_index("bin") * own_cols, own_cols, 1)

time: 66.6 us -> 65 us (0.976)
  other arithmetic: 8.29 us -> 1.88 us
  Pallas kernels: 40.8 us -> 45 us
  starting transfers between devices: 9.51 us -> 10.3 us
  waiting for transfers between devices: 2.65 us -> 1.97 us
    reduce_sum x1 -> x0, other arithmetic: 5.26 us -> none  [body(): jnp.sum(projected[:, :, c] * blocks[c][None], axis=(1, 2))]
    pallas_call x1 -> x2, Pallas kernels: 16.4 us -> 20.7 us  [the longest x1 11.8 us: fused_half(): pl.pallas_call(fused_kernel, out_shape=(jax.ShapeDtypeStruct(gram.shape,...]
    ppermute x1, waiting for transfers between devices: 2.64 us -> 0.09 us  [gather_cells(): other = lax.ppermute(mine, 'cell_core', [(0, 1), (1, 0)])]
    ppermute x2, waiting for transfers between devices: 0.01 us -> 1.23 us  [exchange_sum(): value = value + lax.ppermute(value, axis, pairs)]
    convert_element_type x2 -> x3, other arithmetic: 1.44 us -> 0.49 us  [split_pair(): return (hi.astype(jnp.bfloat16), lo.astype(jnp.bfloat16))]
    ppermute x2, starting transfers between devices: 2.16 us -> 3.04 us  [exchange_sum(): value = value + lax.ppermute(value, axis, pairs)]
  transfers between devices with their start and end apart: 4 -> 4, of which waited for: 1 -> 3; matrix products, arithmetic and copies ran while one was open for 6% -> 4% of each run, Pallas kernels for 62% -> 52%
where the time goes in v12:
time: 65 us; the launch traced here: 64.5 us
  Pallas kernels  45 us (69%)
  starting transfers between devices  10.3 us (16%)
  matrix products  2.91 us (4%)
  local copies, waits for them, and re-layouts  2.34 us (4%)
  waiting for transfers between devices  1.97 us (3%)
  other arithmetic  1.88 us (3%)
    pallas_call x1, Pallas kernels, project(): pl.pallas_call(project_kernel, out_shape=jax.ShapeDtypeStruct((rows, rank...  24.3 us
    pallas_call x1, Pallas kernels, fused_half(): pl.pallas_call(fused_kernel, out_shape=(jax.ShapeDtypeStruct(gram.shape,...  11.8 us
    pallas_call x1, Pallas kernels, sweep_rest(): pl.pallas_call(functools.partial(sweep_kernel, first), out_shape=jax.Shap...  8.95 us
    all_to_all x1, starting transfers between devices, gather_cells(): mine = lax.all_to_all(spread, 'cell_outer', 0, 0, tiled=True)  7.28 us
    ppermute x2, starting transfers between devices, exchange_sum(): value = value + lax.ppermute(value, axis, pairs)  3.04 us
    broadcast_in_dim x1, local copies, waits for them, and re-layouts, gather_cells(): spread = jnp.broadcast_to(cell_factor[None], (outer,) + cell_factor.shape)  2.06 us
    dot_general x1, matrix products, body(): return -jnp.dot(totals, own, precision=lax.Precision.HIGHEST)  1.68 us
  transfers between devices with their start and end apart: 4, of which 3 were waited for; matrix products, arithmetic and copies ran while one was open for 4% of the time, Pallas kernels for 52%

profile of v12, /device:TPU:0, one launch (start us, length us, event | category | flops | bytes accessed | tf_op | source)
XLA Modules:
  0.0 64.5 jit_solution(5308427026407165139)
XLA Ops:
  0.0 0.0 copy-start.2
  0.0 2.1 %broadcast_in_dim.2 = f32[8,256,128]{2,1,0:T(8,128)} broadcast(f32[256,128]{1,0:T(8,128)} %param.4), dimensions={1,2} | broadcast | bytes 1179648 | tf_op jit(solution)/shard_map/broadcast_in_dim | solution.py:72
  2.1 7.3 %all-to-all-start = ((f32[8,256,128]{2,1,0:T(8,128)}), f32[8,256,128]{2,1,0:T(8,128)S(1)}, u32[]{:S(2)}, u32[]{:S(2)}) async-start(f32[8,256,128]{2,1,0:T(8,128)} %broadcast_in_dim.2), calls=%async_computation | async-start | bytes 2097152 | tf_op jit(solution)/shard_map/all_to_all | solution.py:73
  9.3 0.0 copy-done.2
  9.4 0.1 fusion.15
  9.4 0.7 %pad_maximum_fusion.b_ref = bf16[512,256]{1,0:T(8,128)(2,1)} fusion(bf16[512,128]{1,0:T(8,128)(2,1)S(1)} %get-tuple-element.18, bf16[512,128]{1,0:T(8,128)(2,1)S(1)} %get-tuple-element.17), kind=kLoop, calls=%fused_computation.21 | loop fusion | flops 524288 | bytes 524288 | tf_op jit(solution)/shard_map/concatenate | solution.py:52
  10.1 24.3 %shard_map.37 = f32[24576,128]{1,0:T(8,128)} custom-call(f32[24576,512]{1,0:T(8,128)} %bitcast.11, bf16[512,256]{1,0:T(8,128)(2,1)} %pad_maximum_fusion.b_ref), custom_call_target="tpu_custom_call" | custom-call | flops 12884901888 | bytes 62914560 | tf_op jit(solution)/shard_map/pallas_call | solution.py:53
  34.5 0.6 all-to-all-done.xm_ref
  35.1 0.0 copy-start
  35.1 0.0 collective-permute-start
  35.1 0.3 fusion.27
  35.4 1.6 %collective-permute-start.1 = (f32[128,128]{1,0:T(8,128)S(1)}, f32[128,128]{1,0:T(8,128)S(1)}, u32[]{:S(2)}, u32[]{:S(2)}) collective-permute-start(f32[128,128]{1,0:T(8,128)S(1)} %fusion.17), channel_id=1, source_target_pairs={{0,1},{1,0},{2,3},{3,2},{4,5},{5,4},{6,7},{7,6},{8,9},{9,8},{10,11... | collective-permute-start | bytes 196616 | tf_op jit(solution)/shard_map/ppermute | solution.py:16
  37.0 0.2 fusion.1
  37.2 0.5 fusion.6
  37.7 0.0 copy-done
  37.7 0.1 collective-permute-done.xo_ref
  37.8 0.0 copy-start.1
  37.8 0.2 fusion.3
  38.0 0.5 fusion.10
  38.5 0.3 copy-done.1
  38.8 1.2 %collective-permute-done.1 = f32[128,128]{1,0:T(8,128)S(1)} collective-permute-done((f32[128,128]{1,0:T(8,128)S(1)}, f32[128,128]{1,0:T(8,128)S(1)}, u32[]{:S(2)}, u32[]{:S(2)}) %collective-permute-start.1) | collective-permute-done | bytes 65568 | tf_op jit(solution)/shard_map/ppermute | solution.py:16
  40.0 0.7 %fusion.20.g_ref = f32[128,128]{1,0:T(8,128)} fusion(f32[256,256]{1,0:T(8,128)S(1)} %fusion.10, f32[256,256]{1,0:T(8,128)S(1)} %fusion.6, f32[128,128]{1,0:T(8,128)S(1)} %collective-permute-done.1, f32[256,256]{1,0:T(8,128)S(1)} %fusion.27), kind=kLoop, calls=%fused_computation.28 | loop fusion | flops 196608 | bytes 917504 | tf_op jit(solution)/shard_map/mul | solution.py:172
  40.6 11.8 %shard_map.38 = (f32[128,128]{1,0:T(8,128)}, f32[6,128]{1,0:T(8,128)}) custom-call(s32[1]{0:T(128)} %bitcast.core_ref, f32[128,128]{1,0:T(8,128)} %fusion.20.g_ref, f32[6,8,2,256,128]{4,3,2,1,0:T(8,128)} %bitcast.9, f32[6,8,2,256,128]{4,3,2,1,0:T(8,128)} %bitcast.10, f32[8,256,128]{2,1,0:T(8,128)} %copy-done, f32[8,256,128]{2,1,0:T(8,128)} %copy-done.1), custom_call_target="tpu_custom_call" | custom-call | tf_op jit(solution)/shard_map/pallas_call | solution.py:150
  52.4 1.5 %collective-permute-start.2 = (f32[6,128]{1,0:T(8,128)}, f32[6,128]{1,0:T(8,128)S(1)}, u32[]{:S(2)}, u32[]{:S(2)}) collective-permute-start(f32[6,128]{1,0:T(8,128)} %get-tuple-element.11), channel_id=1, source_target_pairs={{0,1},{1,0},{2,3},{3,2},{4,5},{5,4},{6,7},{7,6},{8,9},{9,8},{10,11... | collective-permute-start | bytes 9224 | tf_op jit(solution)/shard_map/ppermute | solution.py:16
  53.9 9.0 %shard_map.39 = f32[128,128]{1,0:T(8,128)} custom-call(f32[128,128]{1,0:T(8,128)} %get-tuple-element.12.g_ref), custom_call_target="tpu_custom_call" | custom-call | tf_op jit(solution)/shard_map/pallas_call | solution.py:108
  62.8 0.0 collective-permute-done.2
  62.8 1.7 %convolution_negate_fusion = f32[6,64]{1,0:T(8,128)} fusion(f32[128,128]{1,0:T(8,128)} %shard_map.39, s32[]{:T(128)S(6)} %select_n.3, f32[6,128]{1,0:T(8,128)} %get-tuple-element.11, f32[6,128]{1,0:T(8,128)S(1)} %collective-permute-done.2), kind=kOutput, calls=%fused_computation.6 | convolution fusion | flops 590976 | bytes 73220 | tf_op jit(solution)/shard_map/dot_general | solution.py:192
  (1 shorter events, 0.0 us)
Async XLA Ops:
  0.0 9.4 %copy-start.2 = (f32[512,128]{1,0:T(8,128)S(1)}, f32[512,128]{1,0:T(8,128)}, u32[]{:S(2)}) copy-start(f32[512,128]{1,0:T(8,128)} %param.5) | copy-start | bytes 786436
  2.1 33.0 %all-to-all-start = ((f32[8,256,128]{2,1,0:T(8,128)}), f32[8,256,128]{2,1,0:T(8,128)S(1)}, u32[]{:S(2)}, u32[]{:S(2)}) async-start(f32[8,256,128]{2,1,0:T(8,128)} %broadcast_in_dim.2), calls=%async_computation | async-start | bytes 2097152 | tf_op jit(solution)/shard_map/all_to_all | solution.py:73
  35.1 2.6 %copy-start = (f32[8,256,128]{2,1,0:T(8,128)}, f32[8,256,128]{2,1,0:T(8,128)S(1)}, u32[]{:S(2)}) copy-start(f32[8,256,128]{2,1,0:T(8,128)S(1)} %all-to-all-done.xm_ref) | copy-start | bytes 3145732
  35.1 2.7 %collective-permute-start = (f32[8,256,128]{2,1,0:T(8,128)S(1)}, f32[8,256,128]{2,1,0:T(8,128)S(1)}, u32[]{:S(2)}, u32[]{:S(2)}) collective-permute-start(f32[8,256,128]{2,1,0:T(8,128)S(1)} %all-to-all-done.xm_ref), channel_id=1, source_target_pairs={{0,2},{2,0},{1,3},{3,1},{4,6},{6,4},{5,7},{7,5},{8,10},{10,8},{9,1... | collective-permute-start | bytes 3145736 | tf_op jit(solution)/shard_map/ppermute | solution.py:77
  35.4 4.6 %collective-permute-start.1 = (f32[128,128]{1,0:T(8,128)S(1)}, f32[128,128]{1,0:T(8,128)S(1)}, u32[]{:S(2)}, u32[]{:S(2)}) collective-permute-start(f32[128,128]{1,0:T(8,128)S(1)} %fusion.17), channel_id=1, source_target_pairs={{0,1},{1,0},{2,3},{3,2},{4,5},{5,4},{6,7},{7,6},{8,9},{9,8},{10,11... | collective-permute-start | bytes 196616 | tf_op jit(solution)/shard_map/ppermute | solution.py:16
  37.8 1.0 %copy-start.1 = (f32[8,256,128]{2,1,0:T(8,128)}, f32[8,256,128]{2,1,0:T(8,128)S(1)}, u32[]{:S(2)}) copy-start(f32[8,256,128]{2,1,0:T(8,128)S(1)} %collective-permute-done.xo_ref) | copy-start | bytes 3145732
  52.4 10.4 %collective-permute-start.2 = (f32[6,128]{1,0:T(8,128)}, f32[6,128]{1,0:T(8,128)S(1)}, u32[]{:S(2)}, u32[]{:S(2)}) collective-permute-start(f32[6,128]{1,0:T(8,128)} %get-tuple-element.11), channel_id=1, source_target_pairs={{0,1},{1,0},{2,3},{3,2},{4,5},{5,4},{6,7},{7,6},{8,9},{9,8},{10,11... | collective-permute-start | bytes 9224 | tf_op jit(solution)/shard_map/ppermute | solution.py:16

commit v13 on v12

--- a/solution.py
+++ b/solution.py
@@ -189,7 +189,7 @@
     totals = exchange_sum(mttkrp, "bin")
     own_cols = rank_cols // lax.axis_size("bin")
     own = lax.dynamic_slice_in_dim(neg_inv, lax.axis_index("bin") * own_cols, own_cols, 1)
-    return -jnp.dot(totals, own, precision=lax.Precision.HIGHEST)
+    return -jnp.sum(totals[:, :, None] * own[None], axis=1)
 
 
 def solution(mesh):

time: 65 us -> 65.8 us (1.012)
  matrix products: 2.91 us -> 1.23 us
  other arithmetic: 1.88 us -> 3.33 us
  local copies, waits for them, and re-layouts: 2.34 us -> 3.32 us
    dot_general x1 -> x0, matrix products: 1.68 us -> none  [body(): return -jnp.dot(totals, own, precision=lax.Precision.HIGHEST)]
    dynamic_slice x0 -> x2, local copies, waits for them, and re-layouts: none -> 0.98 us  [body(): lax.dynamic_slice_in_dim(neg_inv, lax.axis_index('bin') * own_cols, own_c...]
    add x0 -> x1, other arithmetic: none -> 0.69 us  [exchange_sum(): value = value + lax.ppermute(value, axis, pairs)]
  transfers between devices with their start and end apart: 4 -> 4, of which waited for: 3 -> 3; matrix products, arithmetic and copies ran while one was open for 4% -> 5% of each run, Pallas kernels for 52% -> 51%
where the time goes in v13:
time: 65.8 us; the launch traced here: 65.3 us
  Pallas kernels  45 us (68%)
  starting transfers between devices  10.3 us (16%)
  other arithmetic  3.33 us (5%)
  local copies, waits for them, and re-layouts  3.32 us (5%)
  waiting for transfers between devices  1.95 us (3%)
  matrix products  1.23 us (2%)
    pallas_call x1, Pallas kernels, project(): pl.pallas_call(project_kernel, out_shape=jax.ShapeDtypeStruct((rows, rank...  24.3 us
    pallas_call x1, Pallas kernels, fused_half(): pl.pallas_call(fused_kernel, out_shape=(jax.ShapeDtypeStruct(gram.shape,...  11.8 us
    pallas_call x1, Pallas kernels, sweep_rest(): pl.pallas_call(functools.partial(sweep_kernel, first), out_shape=jax.Shap...  8.95 us
    all_to_all x1, starting transfers between devices, gather_cells(): mine = lax.all_to_all(spread, 'cell_outer', 0, 0, tiled=True)  7.28 us
    ppermute x2, starting transfers between devices, exchange_sum(): value = value + lax.ppermute(value, axis, pairs)  3.04 us
    broadcast_in_dim x1, local copies, waits for them, and re-layouts, gather_cells(): spread = jnp.broadcast_to(cell_factor[None], (outer,) + cell_factor.shape)  2.05 us
  transfers between devices with their start and end apart: 4, of which 3 were waited for; matrix products, arithmetic and copies ran while one was open for 5% of the time, Pallas kernels for 51%

profile of v13, /device:TPU:0, one launch (start us, length us, event | category | flops | bytes accessed | tf_op | source)
XLA Modules:
  0.0 65.3 jit_solution(8878751905050947142)
XLA Ops:
  0.0 0.0 copy-start.2
  0.0 2.1 %broadcast_in_dim.2 = f32[8,256,128]{2,1,0:T(8,128)} broadcast(f32[256,128]{1,0:T(8,128)} %param.4), dimensions={1,2} | broadcast | bytes 1179648 | tf_op jit(solution)/shard_map/broadcast_in_dim | solution.py:72
  2.1 7.3 %all-to-all-start = ((f32[8,256,128]{2,1,0:T(8,128)}), f32[8,256,128]{2,1,0:T(8,128)S(1)}, u32[]{:S(2)}, u32[]{:S(2)}) async-start(f32[8,256,128]{2,1,0:T(8,128)} %broadcast_in_dim.2), calls=%async_computation | async-start | bytes 2097152 | tf_op jit(solution)/shard_map/all_to_all | solution.py:73
  9.3 0.0 copy-done.2
  9.3 0.1 fusion.15
  9.4 0.7 %pad_maximum_fusion.b_ref = bf16[512,256]{1,0:T(8,128)(2,1)} fusion(bf16[512,128]{1,0:T(8,128)(2,1)S(1)} %get-tuple-element.18, bf16[512,128]{1,0:T(8,128)(2,1)S(1)} %get-tuple-element.17), kind=kLoop, calls=%fused_computation.20 | loop fusion | flops 524288 | bytes 524288 | tf_op jit(solution)/shard_map/concatenate | solution.py:52
  10.1 24.3 %shard_map.37 = f32[24576,128]{1,0:T(8,128)} custom-call(f32[24576,512]{1,0:T(8,128)} %bitcast.11, bf16[512,256]{1,0:T(8,128)(2,1)} %pad_maximum_fusion.b_ref), custom_call_target="tpu_custom_call" | custom-call | flops 12884901888 | bytes 62914560 | tf_op jit(solution)/shard_map/pallas_call | solution.py:53
  34.5 0.6 all-to-all-done.xm_ref
  35.1 0.0 copy-start
  35.1 0.0 collective-permute-start
  35.1 0.3 fusion.24
  35.4 1.6 %collective-permute-start.1 = (f32[128,128]{1,0:T(8,128)S(1)}, f32[128,128]{1,0:T(8,128)S(1)}, u32[]{:S(2)}, u32[]{:S(2)}) collective-permute-start(f32[128,128]{1,0:T(8,128)S(1)} %fusion.17), channel_id=1, source_target_pairs={{0,1},{1,0},{2,3},{3,2},{4,5},{5,4},{6,7},{7,6},{8,9},{9,8},{10,11... | collective-permute-start | bytes 196616 | tf_op jit(solution)/shard_map/ppermute | solution.py:16
  37.0 0.2 fusion.1
  37.2 0.5 fusion.6
  37.7 0.0 copy-done
  37.7 0.1 collective-permute-done.xo_ref
  37.8 0.0 copy-start.1
  37.8 0.2 fusion.3
  38.0 0.5 fusion.10
  38.5 0.3 copy-done.1
  38.7 1.2 %collective-permute-done.1 = f32[128,128]{1,0:T(8,128)S(1)} collective-permute-done((f32[128,128]{1,0:T(8,128)S(1)}, f32[128,128]{1,0:T(8,128)S(1)}, u32[]{:S(2)}, u32[]{:S(2)}) %collective-permute-start.1) | collective-permute-done | bytes 65568 | tf_op jit(solution)/shard_map/ppermute | solution.py:16
  40.0 0.7 %fusion.20.g_ref = f32[128,128]{1,0:T(8,128)} fusion(f32[256,256]{1,0:T(8,128)S(1)} %fusion.10, f32[256,256]{1,0:T(8,128)S(1)} %fusion.6, f32[128,128]{1,0:T(8,128)S(1)} %collective-permute-done.1, f32[256,256]{1,0:T(8,128)S(1)} %fusion.24), kind=kLoop, calls=%fused_computation.28 | loop fusion | flops 196608 | bytes 917504 | tf_op jit(solution)/shard_map/mul | solution.py:172
  40.6 11.8 %shard_map.38 = (f32[128,128]{1,0:T(8,128)}, f32[6,128]{1,0:T(8,128)}) custom-call(s32[1]{0:T(128)} %bitcast.core_ref, f32[128,128]{1,0:T(8,128)} %fusion.20.g_ref, f32[6,8,2,256,128]{4,3,2,1,0:T(8,128)} %bitcast.9, f32[6,8,2,256,128]{4,3,2,1,0:T(8,128)} %bitcast.10, f32[8,256,128]{2,1,0:T(8,128)} %copy-done, f32[8,256,128]{2,1,0:T(8,128)} %copy-done.1), custom_call_target="tpu_custom_call" | custom-call | tf_op jit(solution)/shard_map/pallas_call | solution.py:150
  52.4 1.5 %collective-permute-start.2 = (f32[6,128]{1,0:T(8,128)}, f32[6,128]{1,0:T(8,128)S(1)}, u32[]{:S(2)}, u32[]{:S(2)}) collective-permute-start(f32[6,128]{1,0:T(8,128)} %get-tuple-element.11), channel_id=1, source_target_pairs={{0,1},{1,0},{2,3},{3,2},{4,5},{5,4},{6,7},{7,6},{8,9},{9,8},{10,11... | collective-permute-start | bytes 9224 | tf_op jit(solution)/shard_map/ppermute | solution.py:16
  53.9 9.0 %shard_map.39 = f32[128,128]{1,0:T(8,128)} custom-call(f32[128,128]{1,0:T(8,128)} %get-tuple-element.12.g_ref), custom_call_target="tpu_custom_call" | custom-call | tf_op jit(solution)/shard_map/pallas_call | solution.py:108
  62.8 0.9 %constant_dynamic-slice_fusion = f32[128,64]{1,0:T(8,128)S(1)} fusion(f32[128,128]{1,0:T(8,128)} %shard_map.39, s32[]{:T(128)S(6)} %select_n.3), kind=kLoop, calls=%fused_computation.33 | loop fusion | bytes 65540 | tf_op jit(solution)/shard_map/dynamic_slice | solution.py:191
  63.8 0.1 copy.4
  63.8 0.0 collective-permute-done.2
  63.8 0.7 %add.50 = f32[6,128]{1,0:T(8,128)S(1)} add(f32[6,128]{1,0:T(8,128)} %get-tuple-element.11, f32[6,128]{1,0:T(8,128)S(1)} %collective-permute-done.2) | non-fusion elementwise | flops 768 | bytes 9216 | tf_op jit(solution)/shard_map/add | solution.py:16
  64.5 0.1 multiply_reduce_fusion
  64.7 0.6 neg.3
  (1 shorter events, 0.0 us)
Async XLA Ops:
  0.0 9.3 %copy-start.2 = (f32[512,128]{1,0:T(8,128)S(1)}, f32[512,128]{1,0:T(8,128)}, u32[]{:S(2)}) copy-start(f32[512,128]{1,0:T(8,128)} %param.5) | copy-start | bytes 786436
  2.1 33.0 %all-to-all-start = ((f32[8,256,128]{2,1,0:T(8,128)}), f32[8,256,128]{2,1,0:T(8,128)S(1)}, u32[]{:S(2)}, u32[]{:S(2)}) async-start(f32[8,256,128]{2,1,0:T(8,128)} %broadcast_in_dim.2), calls=%async_computation | async-start | bytes 2097152 | tf_op jit(solution)/shard_map/all_to_all | solution.py:73
  35.1 2.6 %copy-start = (f32[8,256,128]{2,1,0:T(8,128)}, f32[8,256,128]{2,1,0:T(8,128)S(1)}, u32[]{:S(2)}) copy-start(f32[8,256,128]{2,1,0:T(8,128)S(1)} %all-to-all-done.xm_ref) | copy-start | bytes 3145732
  35.1 2.7 %collective-permute-start = (f32[8,256,128]{2,1,0:T(8,128)S(1)}, f32[8,256,128]{2,1,0:T(8,128)S(1)}, u32[]{:S(2)}, u32[]{:S(2)}) collective-permute-start(f32[8,256,128]{2,1,0:T(8,128)S(1)} %all-to-all-done.xm_ref), channel_id=1, source_target_pairs={{0,2},{2,0},{1,3},{3,1},{4,6},{6,4},{5,7},{7,5},{8,10},{10,8},{9,1... | collective-permute-start | bytes 3145736 | tf_op jit(solution)/shard_map/ppermute | solution.py:77
  35.4 4.6 %collective-permute-start.1 = (f32[128,128]{1,0:T(8,128)S(1)}, f32[128,128]{1,0:T(8,128)S(1)}, u32[]{:S(2)}, u32[]{:S(2)}) collective-permute-start(f32[128,128]{1,0:T(8,128)S(1)} %fusion.17), channel_id=1, source_target_pairs={{0,1},{1,0},{2,3},{3,2},{4,5},{5,4},{6,7},{7,6},{8,9},{9,8},{10,11... | collective-permute-start | bytes 196616 | tf_op jit(solution)/shard_map/ppermute | solution.py:16
  37.8 1.0 %copy-start.1 = (f32[8,256,128]{2,1,0:T(8,128)}, f32[8,256,128]{2,1,0:T(8,128)S(1)}, u32[]{:S(2)}) copy-start(f32[8,256,128]{2,1,0:T(8,128)S(1)} %collective-permute-done.xo_ref) | copy-start | bytes 3145732
  52.4 11.4 %collective-permute-start.2 = (f32[6,128]{1,0:T(8,128)}, f32[6,128]{1,0:T(8,128)S(1)}, u32[]{:S(2)}, u32[]{:S(2)}) collective-permute-start(f32[6,128]{1,0:T(8,128)} %get-tuple-element.11), channel_id=1, source_target_pairs={{0,1},{1,0},{2,3},{3,2},{4,5},{5,4},{6,7},{7,6},{8,9},{9,8},{10,11... | collective-permute-start | bytes 9224 | tf_op jit(solution)/shard_map/ppermute | solution.py:16

commit v14 on v13

--- a/solution.py
+++ b/solution.py
@@ -101,7 +101,7 @@
 
 
 def sweep_kernel(first, g_ref, o_ref):
-    o_ref[...] = sweep_steps(g_ref[...], first, g_ref.shape[0] - first)
+    o_ref[...] = -sweep_steps(g_ref[...], first, g_ref.shape[0] - first)
 
 
 def sweep_rest(a, first):
@@ -175,7 +175,7 @@
     if other is not None and half % outer == 0:
         core = lax.axis_index("cell_core").astype(jnp.int32).reshape(1)
         partial, mttkrp = fused_half(gram, projected, mine, other, core)
-        neg_inv = sweep_rest(partial, half)
+        inverse = sweep_rest(partial, half)
     else:
         if other is None:
             mttkrp = jnp.sum(projected[:, :, 0] * mine[None], axis=(1, 2))
@@ -185,11 +185,11 @@
             mttkrp = jnp.sum(projected[:, :, 0] * x0[None], axis=(1, 2)) + jnp.sum(
                 projected[:, :, 1] * x1[None], axis=(1, 2)
             )
-        neg_inv = sweep_rest(gram, 0)
+        inverse = sweep_rest(gram, 0)
     totals = exchange_sum(mttkrp, "bin")
     own_cols = rank_cols // lax.axis_size("bin")
-    own = lax.dynamic_slice_in_dim(neg_inv, lax.axis_index("bin") * own_cols, own_cols, 1)
-    return -jnp.sum(totals[:, :, None] * own[None], axis=1)
+    own = lax.dynamic_slice_in_dim(inverse, lax.axis_index("bin") * own_cols, own_cols, 1)
+    return jnp.sum(totals[:, :, None] * own[None], axis=1)
 
 
 def solution(mesh):

time: 65.8 us -> 65.8 us (level)
  no operation moved by 1% of the time
where the time goes in v14:
time: 65.8 us; the launch traced here: 65.3 us
  Pallas kernels  45.1 us (69%)
  starting transfers between devices  10.3 us (16%)
  other arithmetic  3.33 us (5%)
  local copies, waits for them, and re-layouts  3.32 us (5%)
  waiting for transfers between devices  1.95 us (3%)
  matrix products  1.23 us (2%)
    pallas_call x1, Pallas kernels, project(): pl.pallas_call(project_kernel, out_shape=jax.ShapeDtypeStruct((rows, rank...  24.3 us
    pallas_call x1, Pallas kernels, fused_half(): pl.pallas_call(fused_kernel, out_shape=(jax.ShapeDtypeStruct(gram.shape,...  11.8 us
    pallas_call x1, Pallas kernels, sweep_rest(): pl.pallas_call(functools.partial(sweep_kernel, first), out_shape=jax.Shap...  8.96 us
    all_to_all x1, starting transfers between devices, gather_cells(): mine = lax.all_to_all(spread, 'cell_outer', 0, 0, tiled=True)  7.28 us
    ppermute x2, starting transfers between devices, exchange_sum(): value = value + lax.ppermute(value, axis, pairs)  3.04 us
    broadcast_in_dim x1, local copies, waits for them, and re-layouts, gather_cells(): spread = jnp.broadcast_to(cell_factor[None], (outer,) + cell_factor.shape)  2.05 us
  transfers between devices with their start and end apart: 4, of which 3 were waited for; matrix products, arithmetic and copies ran while one was open for 5% of the time, Pallas kernels for 51%

profile of v14, /device:TPU:0, one launch (start us, length us, event | category | flops | bytes accessed | tf_op | source)
XLA Modules:
  0.0 65.3 jit_solution(12365292247755047711)
XLA Ops:
  0.0 0.0 copy-start.2
  0.0 2.1 %broadcast_in_dim.2 = f32[8,256,128]{2,1,0:T(8,128)} broadcast(f32[256,128]{1,0:T(8,128)} %param.4), dimensions={1,2} | broadcast | bytes 1179648 | tf_op jit(solution)/shard_map/broadcast_in_dim | solution.py:72
  2.1 7.3 %all-to-all-start = ((f32[8,256,128]{2,1,0:T(8,128)}), f32[8,256,128]{2,1,0:T(8,128)S(1)}, u32[]{:S(2)}, u32[]{:S(2)}) async-start(f32[8,256,128]{2,1,0:T(8,128)} %broadcast_in_dim.2), calls=%async_computation | async-start | bytes 2097152 | tf_op jit(solution)/shard_map/all_to_all | solution.py:73
  9.3 0.0 copy-done.2
  9.3 0.1 fusion.15
  9.4 0.7 %pad_maximum_fusion.b_ref = bf16[512,256]{1,0:T(8,128)(2,1)} fusion(bf16[512,128]{1,0:T(8,128)(2,1)S(1)} %get-tuple-element.18, bf16[512,128]{1,0:T(8,128)(2,1)S(1)} %get-tuple-element.17), kind=kLoop, calls=%fused_computation.20 | loop fusion | flops 524288 | bytes 524288 | tf_op jit(solution)/shard_map/concatenate | solution.py:52
  10.1 24.3 %shard_map.37 = f32[24576,128]{1,0:T(8,128)} custom-call(f32[24576,512]{1,0:T(8,128)} %bitcast.11, bf16[512,256]{1,0:T(8,128)(2,1)} %pad_maximum_fusion.b_ref), custom_call_target="tpu_custom_call" | custom-call | flops 12884901888 | bytes 62914560 | tf_op jit(solution)/shard_map/pallas_call | solution.py:53
  34.5 0.6 all-to-all-done.xm_ref
  35.1 0.0 copy-start
  35.1 0.0 collective-permute-start
  35.1 0.3 fusion.24
  35.4 1.6 %collective-permute-start.1 = (f32[128,128]{1,0:T(8,128)S(1)}, f32[128,128]{1,0:T(8,128)S(1)}, u32[]{:S(2)}, u32[]{:S(2)}) collective-permute-start(f32[128,128]{1,0:T(8,128)S(1)} %fusion.17), channel_id=1, source_target_pairs={{0,1},{1,0},{2,3},{3,2},{4,5},{5,4},{6,7},{7,6},{8,9},{9,8},{10,11... | collective-permute-start | bytes 196616 | tf_op jit(solution)/shard_map/ppermute | solution.py:16
  37.0 0.2 fusion.1
  37.2 0.5 fusion.6
  37.7 0.0 copy-done
  37.7 0.1 collective-permute-done.xo_ref
  37.8 0.0 copy-start.1
  37.8 0.2 fusion.3
  38.0 0.5 fusion.10
  38.5 0.3 copy-done.1
  38.7 1.2 %collective-permute-done.1 = f32[128,128]{1,0:T(8,128)S(1)} collective-permute-done((f32[128,128]{1,0:T(8,128)S(1)}, f32[128,128]{1,0:T(8,128)S(1)}, u32[]{:S(2)}, u32[]{:S(2)}) %collective-permute-start.1) | collective-permute-done | bytes 65568 | tf_op jit(solution)/shard_map/ppermute | solution.py:16
  40.0 0.7 %fusion.20.g_ref = f32[128,128]{1,0:T(8,128)} fusion(f32[256,256]{1,0:T(8,128)S(1)} %fusion.10, f32[256,256]{1,0:T(8,128)S(1)} %fusion.6, f32[128,128]{1,0:T(8,128)S(1)} %collective-permute-done.1, f32[256,256]{1,0:T(8,128)S(1)} %fusion.24), kind=kLoop, calls=%fused_computation.28 | loop fusion | flops 196608 | bytes 917504 | tf_op jit(solution)/shard_map/mul | solution.py:172
  40.6 11.8 %shard_map.38 = (f32[128,128]{1,0:T(8,128)}, f32[6,128]{1,0:T(8,128)}) custom-call(s32[1]{0:T(128)} %bitcast.core_ref, f32[128,128]{1,0:T(8,128)} %fusion.20.g_ref, f32[6,8,2,256,128]{4,3,2,1,0:T(8,128)} %bitcast.9, f32[6,8,2,256,128]{4,3,2,1,0:T(8,128)} %bitcast.10, f32[8,256,128]{2,1,0:T(8,128)} %copy-done, f32[8,256,128]{2,1,0:T(8,128)} %copy-done.1), custom_call_target="tpu_custom_call" | custom-call | tf_op jit(solution)/shard_map/pallas_call | solution.py:150
  52.4 1.5 %collective-permute-start.2 = (f32[6,128]{1,0:T(8,128)}, f32[6,128]{1,0:T(8,128)S(1)}, u32[]{:S(2)}, u32[]{:S(2)}) collective-permute-start(f32[6,128]{1,0:T(8,128)} %get-tuple-element.11), channel_id=1, source_target_pairs={{0,1},{1,0},{2,3},{3,2},{4,5},{5,4},{6,7},{7,6},{8,9},{9,8},{10,11... | collective-permute-start | bytes 9224 | tf_op jit(solution)/shard_map/ppermute | solution.py:16
  53.9 9.0 %shard_map.39 = f32[128,128]{1,0:T(8,128)} custom-call(f32[128,128]{1,0:T(8,128)} %get-tuple-element.12.g_ref), custom_call_target="tpu_custom_call" | custom-call | tf_op jit(solution)/shard_map/pallas_call | solution.py:108
  62.8 0.9 %constant_dynamic-slice_fusion = f32[128,64]{1,0:T(8,128)S(1)} fusion(f32[128,128]{1,0:T(8,128)} %shard_map.39, s32[]{:T(128)S(6)} %select_n.3), kind=kLoop, calls=%fused_computation.33 | loop fusion | bytes 65540 | tf_op jit(solution)/shard_map/dynamic_slice | solution.py:191
  63.8 0.1 copy.4
  63.8 0.0 collective-permute-done.2
  63.9 0.7 %add.50 = f32[6,128]{1,0:T(8,128)S(1)} add(f32[6,128]{1,0:T(8,128)} %get-tuple-element.11, f32[6,128]{1,0:T(8,128)S(1)} %collective-permute-done.2) | non-fusion elementwise | flops 768 | bytes 9216 | tf_op jit(solution)/shard_map/add | solution.py:16
  64.6 0.7 %multiply_reduce_fusion = f32[6,64]{1,0:T(8,128)} fusion(f32[128,64]{0,1:T(8,128)S(1)} %copy.4, f32[6,128]{1,0:T(8,128)S(1)} %add.50), kind=kLoop, calls=%fused_computation.21 | loop fusion | flops 97920 | bytes 37376 | tf_op jit(solution)/shard_map/reduce_sum | solution.py:192
  (1 shorter events, 0.0 us)
Async XLA Ops:
  0.0 9.3 %copy-start.2 = (f32[512,128]{1,0:T(8,128)S(1)}, f32[512,128]{1,0:T(8,128)}, u32[]{:S(2)}) copy-start(f32[512,128]{1,0:T(8,128)} %param.5) | copy-start | bytes 786436
  2.1 33.0 %all-to-all-start = ((f32[8,256,128]{2,1,0:T(8,128)}), f32[8,256,128]{2,1,0:T(8,128)S(1)}, u32[]{:S(2)}, u32[]{:S(2)}) async-start(f32[8,256,128]{2,1,0:T(8,128)} %broadcast_in_dim.2), calls=%async_computation | async-start | bytes 2097152 | tf_op jit(solution)/shard_map/all_to_all | solution.py:73
  35.1 2.6 %copy-start = (f32[8,256,128]{2,1,0:T(8,128)}, f32[8,256,128]{2,1,0:T(8,128)S(1)}, u32[]{:S(2)}) copy-start(f32[8,256,128]{2,1,0:T(8,128)S(1)} %all-to-all-done.xm_ref) | copy-start | bytes 3145732
  35.1 2.7 %collective-permute-start = (f32[8,256,128]{2,1,0:T(8,128)S(1)}, f32[8,256,128]{2,1,0:T(8,128)S(1)}, u32[]{:S(2)}, u32[]{:S(2)}) collective-permute-start(f32[8,256,128]{2,1,0:T(8,128)S(1)} %all-to-all-done.xm_ref), channel_id=1, source_target_pairs={{0,2},{2,0},{1,3},{3,1},{4,6},{6,4},{5,7},{7,5},{8,10},{10,8},{9,1... | collective-permute-start | bytes 3145736 | tf_op jit(solution)/shard_map/ppermute | solution.py:77
  35.4 4.6 %collective-permute-start.1 = (f32[128,128]{1,0:T(8,128)S(1)}, f32[128,128]{1,0:T(8,128)S(1)}, u32[]{:S(2)}, u32[]{:S(2)}) collective-permute-start(f32[128,128]{1,0:T(8,128)S(1)} %fusion.17), channel_id=1, source_target_pairs={{0,1},{1,0},{2,3},{3,2},{4,5},{5,4},{6,7},{7,6},{8,9},{9,8},{10,11... | collective-permute-start | bytes 196616 | tf_op jit(solution)/shard_map/ppermute | solution.py:16
  37.8 1.0 %copy-start.1 = (f32[8,256,128]{2,1,0:T(8,128)}, f32[8,256,128]{2,1,0:T(8,128)S(1)}, u32[]{:S(2)}) copy-start(f32[8,256,128]{2,1,0:T(8,128)S(1)} %collective-permute-done.xo_ref) | copy-start | bytes 3145732
  52.4 11.5 %collective-permute-start.2 = (f32[6,128]{1,0:T(8,128)}, f32[6,128]{1,0:T(8,128)S(1)}, u32[]{:S(2)}, u32[]{:S(2)}) collective-permute-start(f32[6,128]{1,0:T(8,128)} %get-tuple-element.11), channel_id=1, source_target_pairs={{0,1},{1,0},{2,3},{3,2},{4,5},{5,4},{6,7},{7,6},{8,9},{9,8},{10,11... | collective-permute-start | bytes 9224 | tf_op jit(solution)/shard_map/ppermute | solution.py:16

commit v15 on v12

--- a/solution.py
+++ b/solution.py
@@ -113,7 +113,7 @@
 
 def fused_kernel(core_ref, g_ref, pm_ref, po_ref, xm_ref, xo_ref, o_ref, m_ref, a_ref):
     o = pl.program_id(0)
-    share = g_ref.shape[0] // (2 * pl.num_programs(0))
+    share = (3 * g_ref.shape[0] // 4) // pl.num_programs(0)
 
     @pl.when(o == 0)
     def _():
@@ -170,7 +170,7 @@
     blocks = [mine] if other is None else [mine, other]
     gram_cell = sum(gram_of(b.reshape(-1, rank_cols)) for b in blocks)
     gram = gram_cell * gram_bin
-    half = rank_cols // 2
+    half = 3 * rank_cols // 4
     projected = projected.reshape(image_rows, outer, len(blocks), block_rows, rank_cols)
     if other is not None and half % outer == 0:
         core = lax.axis_index("cell_core").astype(jnp.int32).reshape(1)

time: 65 us -> 64.5 us (level)
    pallas_call x1, Pallas kernels: 8.95 us -> 5.21 us  [sweep_rest(): pl.pallas_call(functools.partial(sweep_kernel, first), out_shape=jax.Shap...]
    pallas_call x1, Pallas kernels: 11.8 us -> 15.1 us  [fused_half(): pl.pallas_call(fused_kernel, out_shape=(jax.ShapeDtypeStruct(gram.shape,...]
  transfers between devices with their start and end apart: 4 -> 4, of which waited for: 3 -> 3; matrix products, arithmetic and copies ran while one was open for 4% -> 4% of each run, Pallas kernels for 52% -> 46%
where the time goes in v15:
time: 64.5 us; the launch traced here: 64.1 us
  Pallas kernels  44.6 us (69%)
  starting transfers between devices  10.3 us (16%)
  matrix products  2.91 us (5%)
  local copies, waits for them, and re-layouts  2.34 us (4%)
  waiting for transfers between devices  1.97 us (3%)
  other arithmetic  1.88 us (3%)
    pallas_call x1, Pallas kernels, project(): pl.pallas_call(project_kernel, out_shape=jax.ShapeDtypeStruct((rows, rank...  24.3 us
    pallas_call x1, Pallas kernels, fused_half(): pl.pallas_call(fused_kernel, out_shape=(jax.ShapeDtypeStruct(gram.shape,...  15.1 us
    all_to_all x1, starting transfers between devices, gather_cells(): mine = lax.all_to_all(spread, 'cell_outer', 0, 0, tiled=True)  7.28 us
    pallas_call x1, Pallas kernels, sweep_rest(): pl.pallas_call(functools.partial(sweep_kernel, first), out_shape=jax.Shap...  5.21 us
    ppermute x2, starting transfers between devices, exchange_sum(): value = value + lax.ppermute(value, axis, pairs)  3.04 us
    broadcast_in_dim x1, local copies, waits for them, and re-layouts, gather_cells(): spread = jnp.broadcast_to(cell_factor[None], (outer,) + cell_factor.shape)  2.06 us
    dot_general x1, matrix products, body(): return -jnp.dot(totals, own, precision=lax.Precision.HIGHEST)  1.68 us
  transfers between devices with their start and end apart: 4, of which 3 were waited for; matrix products, arithmetic and copies ran while one was open for 4% of the time, Pallas kernels for 46%

profile of v15, /device:TPU:0, one launch (start us, length us, event | category | flops | bytes accessed | tf_op | source)
XLA Modules:
  0.0 64.1 jit_solution(13236694574939129281)
XLA Ops:
  0.0 0.0 copy-start.2
  0.0 2.1 %broadcast_in_dim.2 = f32[8,256,128]{2,1,0:T(8,128)} broadcast(f32[256,128]{1,0:T(8,128)} %param.4), dimensions={1,2} | broadcast | bytes 1179648 | tf_op jit(solution)/shard_map/broadcast_in_dim | solution.py:72
  2.1 7.3 %all-to-all-start = ((f32[8,256,128]{2,1,0:T(8,128)}), f32[8,256,128]{2,1,0:T(8,128)S(1)}, u32[]{:S(2)}, u32[]{:S(2)}) async-start(f32[8,256,128]{2,1,0:T(8,128)} %broadcast_in_dim.2), calls=%async_computation | async-start | bytes 2097152 | tf_op jit(solution)/shard_map/all_to_all | solution.py:73
  9.3 0.0 copy-done.2
  9.4 0.1 fusion.15
  9.4 0.7 %pad_maximum_fusion.b_ref = bf16[512,256]{1,0:T(8,128)(2,1)} fusion(bf16[512,128]{1,0:T(8,128)(2,1)S(1)} %get-tuple-element.18, bf16[512,128]{1,0:T(8,128)(2,1)S(1)} %get-tuple-element.17), kind=kLoop, calls=%fused_computation.21 | loop fusion | flops 524288 | bytes 524288 | tf_op jit(solution)/shard_map/concatenate | solution.py:52
  10.1 24.3 %shard_map.37 = f32[24576,128]{1,0:T(8,128)} custom-call(f32[24576,512]{1,0:T(8,128)} %bitcast.11, bf16[512,256]{1,0:T(8,128)(2,1)} %pad_maximum_fusion.b_ref), custom_call_target="tpu_custom_call" | custom-call | flops 12884901888 | bytes 62914560 | tf_op jit(solution)/shard_map/pallas_call | solution.py:53
  34.5 0.6 all-to-all-done.xm_ref
  35.1 0.0 copy-start
  35.1 0.0 collective-permute-start
  35.1 0.3 fusion.27
  35.4 1.6 %collective-permute-start.1 = (f32[128,128]{1,0:T(8,128)S(1)}, f32[128,128]{1,0:T(8,128)S(1)}, u32[]{:S(2)}, u32[]{:S(2)}) collective-permute-start(f32[128,128]{1,0:T(8,128)S(1)} %fusion.17), channel_id=1, source_target_pairs={{0,1},{1,0},{2,3},{3,2},{4,5},{5,4},{6,7},{7,6},{8,9},{9,8},{10,11... | collective-permute-start | bytes 196616 | tf_op jit(solution)/shard_map/ppermute | solution.py:16
  37.0 0.2 fusion.1
  37.2 0.5 fusion.6
  37.7 0.0 copy-done
  37.7 0.1 collective-permute-done.xo_ref
  37.8 0.0 copy-start.1
  37.8 0.2 fusion.3
  38.0 0.5 fusion.10
  38.5 0.3 copy-done.1
  38.8 1.2 %collective-permute-done.1 = f32[128,128]{1,0:T(8,128)S(1)} collective-permute-done((f32[128,128]{1,0:T(8,128)S(1)}, f32[128,128]{1,0:T(8,128)S(1)}, u32[]{:S(2)}, u32[]{:S(2)}) %collective-permute-start.1) | collective-permute-done | bytes 65568 | tf_op jit(solution)/shard_map/ppermute | solution.py:16
  40.0 0.7 %fusion.20.g_ref = f32[128,128]{1,0:T(8,128)} fusion(f32[256,256]{1,0:T(8,128)S(1)} %fusion.10, f32[256,256]{1,0:T(8,128)S(1)} %fusion.6, f32[128,128]{1,0:T(8,128)S(1)} %collective-permute-done.1, f32[256,256]{1,0:T(8,128)S(1)} %fusion.27), kind=kLoop, calls=%fused_computation.28 | loop fusion | flops 196608 | bytes 917504 | tf_op jit(solution)/shard_map/mul | solution.py:172
  40.6 15.1 %shard_map.38 = (f32[128,128]{1,0:T(8,128)}, f32[6,128]{1,0:T(8,128)}) custom-call(s32[1]{0:T(128)} %bitcast.core_ref, f32[128,128]{1,0:T(8,128)} %fusion.20.g_ref, f32[6,8,2,256,128]{4,3,2,1,0:T(8,128)} %bitcast.9, f32[6,8,2,256,128]{4,3,2,1,0:T(8,128)} %bitcast.10, f32[8,256,128]{2,1,0:T(8,128)} %copy-done, f32[8,256,128]{2,1,0:T(8,128)} %copy-done.1), custom_call_target="tpu_custom_call" | custom-call | tf_op jit(solution)/shard_map/pallas_call | solution.py:150
  55.7 1.5 %collective-permute-start.2 = (f32[6,128]{1,0:T(8,128)}, f32[6,128]{1,0:T(8,128)S(1)}, u32[]{:S(2)}, u32[]{:S(2)}) collective-permute-start(f32[6,128]{1,0:T(8,128)} %get-tuple-element.11), channel_id=1, source_target_pairs={{0,1},{1,0},{2,3},{3,2},{4,5},{5,4},{6,7},{7,6},{8,9},{9,8},{10,11... | collective-permute-start | bytes 9224 | tf_op jit(solution)/shard_map/ppermute | solution.py:16
  57.2 5.2 %shard_map.39 = f32[128,128]{1,0:T(8,128)} custom-call(f32[128,128]{1,0:T(8,128)} %get-tuple-element.12.g_ref), custom_call_target="tpu_custom_call" | custom-call | tf_op jit(solution)/shard_map/pallas_call | solution.py:108
  62.4 0.0 collective-permute-done.2
  62.4 1.7 %convolution_negate_fusion = f32[6,64]{1,0:T(8,128)} fusion(f32[128,128]{1,0:T(8,128)} %shard_map.39, s32[]{:T(128)S(6)} %select_n.3, f32[6,128]{1,0:T(8,128)} %get-tuple-element.11, f32[6,128]{1,0:T(8,128)S(1)} %collective-permute-done.2), kind=kOutput, calls=%fused_computation.6 | convolution fusion | flops 590976 | bytes 73220 | tf_op jit(solution)/shard_map/dot_general | solution.py:192
  (1 shorter events, 0.0 us)
Async XLA Ops:
  0.0 9.4 %copy-start.2 = (f32[512,128]{1,0:T(8,128)S(1)}, f32[512,128]{1,0:T(8,128)}, u32[]{:S(2)}) copy-start(f32[512,128]{1,0:T(8,128)} %param.5) | copy-start | bytes 786436
  2.1 33.0 %all-to-all-start = ((f32[8,256,128]{2,1,0:T(8,128)}), f32[8,256,128]{2,1,0:T(8,128)S(1)}, u32[]{:S(2)}, u32[]{:S(2)}) async-start(f32[8,256,128]{2,1,0:T(8,128)} %broadcast_in_dim.2), calls=%async_computation | async-start | bytes 2097152 | tf_op jit(solution)/shard_map/all_to_all | solution.py:73
  35.1 2.6 %copy-start = (f32[8,256,128]{2,1,0:T(8,128)}, f32[8,256,128]{2,1,0:T(8,128)S(1)}, u32[]{:S(2)}) copy-start(f32[8,256,128]{2,1,0:T(8,128)S(1)} %all-to-all-done.xm_ref) | copy-start | bytes 3145732
  35.1 2.7 %collective-permute-start = (f32[8,256,128]{2,1,0:T(8,128)S(1)}, f32[8,256,128]{2,1,0:T(8,128)S(1)}, u32[]{:S(2)}, u32[]{:S(2)}) collective-permute-start(f32[8,256,128]{2,1,0:T(8,128)S(1)} %all-to-all-done.xm_ref), channel_id=1, source_target_pairs={{0,2},{2,0},{1,3},{3,1},{4,6},{6,4},{5,7},{7,5},{8,10},{10,8},{9,1... | collective-permute-start | bytes 3145736 | tf_op jit(solution)/shard_map/ppermute | solution.py:77
  35.4 4.6 %collective-permute-start.1 = (f32[128,128]{1,0:T(8,128)S(1)}, f32[128,128]{1,0:T(8,128)S(1)}, u32[]{:S(2)}, u32[]{:S(2)}) collective-permute-start(f32[128,128]{1,0:T(8,128)S(1)} %fusion.17), channel_id=1, source_target_pairs={{0,1},{1,0},{2,3},{3,2},{4,5},{5,4},{6,7},{7,6},{8,9},{9,8},{10,11... | collective-permute-start | bytes 196616 | tf_op jit(solution)/shard_map/ppermute | solution.py:16
  37.8 1.0 %copy-start.1 = (f32[8,256,128]{2,1,0:T(8,128)}, f32[8,256,128]{2,1,0:T(8,128)S(1)}, u32[]{:S(2)}) copy-start(f32[8,256,128]{2,1,0:T(8,128)S(1)} %collective-permute-done.xo_ref) | copy-start | bytes 3145732
  55.7 6.7 %collective-permute-start.2 = (f32[6,128]{1,0:T(8,128)}, f32[6,128]{1,0:T(8,128)S(1)}, u32[]{:S(2)}, u32[]{:S(2)}) collective-permute-start(f32[6,128]{1,0:T(8,128)} %get-tuple-element.11), channel_id=1, source_target_pairs={{0,1},{1,0},{2,3},{3,2},{4,5},{5,4},{6,7},{7,6},{8,9},{9,8},{10,11... | collective-permute-start | bytes 9224 | tf_op jit(solution)/shard_map/ppermute | solution.py:16

commit v16 on v15

--- a/solution.py
+++ b/solution.py
@@ -113,7 +113,7 @@
 
 def fused_kernel(core_ref, g_ref, pm_ref, po_ref, xm_ref, xo_ref, o_ref, m_ref, a_ref):
     o = pl.program_id(0)
-    share = (3 * g_ref.shape[0] // 4) // pl.num_programs(0)
+    share = (7 * g_ref.shape[0] // 8) // pl.num_programs(0)
 
     @pl.when(o == 0)
     def _():
@@ -170,7 +170,7 @@
     blocks = [mine] if other is None else [mine, other]
     gram_cell = sum(gram_of(b.reshape(-1, rank_cols)) for b in blocks)
     gram = gram_cell * gram_bin
-    half = 3 * rank_cols // 4
+    half = 7 * rank_cols // 8
     projected = projected.reshape(image_rows, outer, len(blocks), block_rows, rank_cols)
     if other is not None and half % outer == 0:
         core = lax.axis_index("cell_core").astype(jnp.int32).reshape(1)

time: 64.5 us -> 64.6 us (level)
    pallas_call x1, Pallas kernels: 15.1 us -> 17.1 us  [fused_half(): pl.pallas_call(fused_kernel, out_shape=(jax.ShapeDtypeStruct(gram.shape,...]
    pallas_call x1, Pallas kernels: 5.21 us -> 3.33 us  [sweep_rest(): pl.pallas_call(functools.partial(sweep_kernel, first), out_shape=jax.Shap...]
  transfers between devices with their start and end apart: 4 -> 4, of which waited for: 3 -> 3; matrix products, arithmetic and copies ran while one was open for 4% -> 4% of each run, Pallas kernels for 46% -> 43%
where the time goes in v16:
time: 64.6 us; the launch traced here: 64.2 us
  Pallas kernels  44.7 us (69%)
  starting transfers between devices  10.3 us (16%)
  matrix products  2.91 us (5%)
  local copies, waits for them, and re-layouts  2.34 us (4%)
  waiting for transfers between devices  1.97 us (3%)
  other arithmetic  1.88 us (3%)
    pallas_call x1, Pallas kernels, project(): pl.pallas_call(project_kernel, out_shape=jax.ShapeDtypeStruct((rows, rank...  24.3 us
    pallas_call x1, Pallas kernels, fused_half(): pl.pallas_call(fused_kernel, out_shape=(jax.ShapeDtypeStruct(gram.shape,...  17.1 us
    all_to_all x1, starting transfers between devices, gather_cells(): mine = lax.all_to_all(spread, 'cell_outer', 0, 0, tiled=True)  7.28 us
    pallas_call x1, Pallas kernels, sweep_rest(): pl.pallas_call(functools.partial(sweep_kernel, first), out_shape=jax.Shap...  3.33 us
    ppermute x2, starting transfers between devices, exchange_sum(): value = value + lax.ppermute(value, axis, pairs)  3.04 us
    broadcast_in_dim x1, local copies, waits for them, and re-layouts, gather_cells(): spread = jnp.broadcast_to(cell_factor[None], (outer,) + cell_factor.shape)  2.06 us
    dot_general x1, matrix products, body(): return -jnp.dot(totals, own, precision=lax.Precision.HIGHEST)  1.68 us
  transfers between devices with their start and end apart: 4, of which 3 were waited for; matrix products, arithmetic and copies ran while one was open for 4% of the time, Pallas kernels for 43%

profile of v16, /device:TPU:0, one launch (start us, length us, event | category | flops | bytes accessed | tf_op | source)
XLA Modules:
  0.0 64.2 jit_solution(2846825741890250590)
XLA Ops:
  0.0 0.0 copy-start.2
  0.0 2.1 %broadcast_in_dim.2 = f32[8,256,128]{2,1,0:T(8,128)} broadcast(f32[256,128]{1,0:T(8,128)} %param.4), dimensions={1,2} | broadcast | bytes 1179648 | tf_op jit(solution)/shard_map/broadcast_in_dim | solution.py:72
  2.1 7.3 %all-to-all-start = ((f32[8,256,128]{2,1,0:T(8,128)}), f32[8,256,128]{2,1,0:T(8,128)S(1)}, u32[]{:S(2)}, u32[]{:S(2)}) async-start(f32[8,256,128]{2,1,0:T(8,128)} %broadcast_in_dim.2), calls=%async_computation | async-start | bytes 2097152 | tf_op jit(solution)/shard_map/all_to_all | solution.py:73
  9.3 0.0 copy-done.2
  9.4 0.1 fusion.15
  9.4 0.7 %pad_maximum_fusion.b_ref = bf16[512,256]{1,0:T(8,128)(2,1)} fusion(bf16[512,128]{1,0:T(8,128)(2,1)S(1)} %get-tuple-element.18, bf16[512,128]{1,0:T(8,128)(2,1)S(1)} %get-tuple-element.17), kind=kLoop, calls=%fused_computation.21 | loop fusion | flops 524288 | bytes 524288 | tf_op jit(solution)/shard_map/concatenate | solution.py:52
  10.1 24.3 %shard_map.37 = f32[24576,128]{1,0:T(8,128)} custom-call(f32[24576,512]{1,0:T(8,128)} %bitcast.11, bf16[512,256]{1,0:T(8,128)(2,1)} %pad_maximum_fusion.b_ref), custom_call_target="tpu_custom_call" | custom-call | flops 12884901888 | bytes 62914560 | tf_op jit(solution)/shard_map/pallas_call | solution.py:53
  34.5 0.6 all-to-all-done.xm_ref
  35.1 0.0 copy-start
  35.1 0.0 collective-permute-start
  35.1 0.3 fusion.27
  35.4 1.6 %collective-permute-start.1 = (f32[128,128]{1,0:T(8,128)S(1)}, f32[128,128]{1,0:T(8,128)S(1)}, u32[]{:S(2)}, u32[]{:S(2)}) collective-permute-start(f32[128,128]{1,0:T(8,128)S(1)} %fusion.17), channel_id=1, source_target_pairs={{0,1},{1,0},{2,3},{3,2},{4,5},{5,4},{6,7},{7,6},{8,9},{9,8},{10,11... | collective-permute-start | bytes 196616 | tf_op jit(solution)/shard_map/ppermute | solution.py:16
  37.0 0.2 fusion.1
  37.2 0.5 fusion.6
  37.7 0.0 copy-done
  37.7 0.1 collective-permute-done.xo_ref
  37.8 0.0 copy-start.1
  37.8 0.2 fusion.3
  38.0 0.5 fusion.10
  38.5 0.3 copy-done.1
  38.8 1.2 %collective-permute-done.1 = f32[128,128]{1,0:T(8,128)S(1)} collective-permute-done((f32[128,128]{1,0:T(8,128)S(1)}, f32[128,128]{1,0:T(8,128)S(1)}, u32[]{:S(2)}, u32[]{:S(2)}) %collective-permute-start.1) | collective-permute-done | bytes 65568 | tf_op jit(solution)/shard_map/ppermute | solution.py:16
  40.0 0.7 %fusion.20.g_ref = f32[128,128]{1,0:T(8,128)} fusion(f32[256,256]{1,0:T(8,128)S(1)} %fusion.10, f32[256,256]{1,0:T(8,128)S(1)} %fusion.6, f32[128,128]{1,0:T(8,128)S(1)} %collective-permute-done.1, f32[256,256]{1,0:T(8,128)S(1)} %fusion.27), kind=kLoop, calls=%fused_computation.28 | loop fusion | flops 196608 | bytes 917504 | tf_op jit(solution)/shard_map/mul | solution.py:172
  40.6 17.1 %shard_map.38 = (f32[128,128]{1,0:T(8,128)}, f32[6,128]{1,0:T(8,128)}) custom-call(s32[1]{0:T(128)} %bitcast.core_ref, f32[128,128]{1,0:T(8,128)} %fusion.20.g_ref, f32[6,8,2,256,128]{4,3,2,1,0:T(8,128)} %bitcast.9, f32[6,8,2,256,128]{4,3,2,1,0:T(8,128)} %bitcast.10, f32[8,256,128]{2,1,0:T(8,128)} %copy-done, f32[8,256,128]{2,1,0:T(8,128)} %copy-done.1), custom_call_target="tpu_custom_call" | custom-call | tf_op jit(solution)/shard_map/pallas_call | solution.py:150
  57.7 1.5 %collective-permute-start.2 = (f32[6,128]{1,0:T(8,128)}, f32[6,128]{1,0:T(8,128)S(1)}, u32[]{:S(2)}, u32[]{:S(2)}) collective-permute-start(f32[6,128]{1,0:T(8,128)} %get-tuple-element.11), channel_id=1, source_target_pairs={{0,1},{1,0},{2,3},{3,2},{4,5},{5,4},{6,7},{7,6},{8,9},{9,8},{10,11... | collective-permute-start | bytes 9224 | tf_op jit(solution)/shard_map/ppermute | solution.py:16
  59.2 3.3 %shard_map.39 = f32[128,128]{1,0:T(8,128)} custom-call(f32[128,128]{1,0:T(8,128)} %get-tuple-element.12.g_ref), custom_call_target="tpu_custom_call" | custom-call | tf_op jit(solution)/shard_map/pallas_call | solution.py:108
  62.5 0.0 collective-permute-done.2
  62.5 1.7 %convolution_negate_fusion = f32[6,64]{1,0:T(8,128)} fusion(f32[128,128]{1,0:T(8,128)} %shard_map.39, s32[]{:T(128)S(6)} %select_n.3, f32[6,128]{1,0:T(8,128)} %get-tuple-element.11, f32[6,128]{1,0:T(8,128)S(1)} %collective-permute-done.2), kind=kOutput, calls=%fused_computation.6 | convolution fusion | flops 590976 | bytes 73220 | tf_op jit(solution)/shard_map/dot_general | solution.py:192
  (1 shorter events, 0.0 us)
Async XLA Ops:
  0.0 9.4 %copy-start.2 = (f32[512,128]{1,0:T(8,128)S(1)}, f32[512,128]{1,0:T(8,128)}, u32[]{:S(2)}) copy-start(f32[512,128]{1,0:T(8,128)} %param.5) | copy-start | bytes 786436
  2.1 33.0 %all-to-all-start = ((f32[8,256,128]{2,1,0:T(8,128)}), f32[8,256,128]{2,1,0:T(8,128)S(1)}, u32[]{:S(2)}, u32[]{:S(2)}) async-start(f32[8,256,128]{2,1,0:T(8,128)} %broadcast_in_dim.2), calls=%async_computation | async-start | bytes 2097152 | tf_op jit(solution)/shard_map/all_to_all | solution.py:73
  35.1 2.6 %copy-start = (f32[8,256,128]{2,1,0:T(8,128)}, f32[8,256,128]{2,1,0:T(8,128)S(1)}, u32[]{:S(2)}) copy-start(f32[8,256,128]{2,1,0:T(8,128)S(1)} %all-to-all-done.xm_ref) | copy-start | bytes 3145732
  35.1 2.7 %collective-permute-start = (f32[8,256,128]{2,1,0:T(8,128)S(1)}, f32[8,256,128]{2,1,0:T(8,128)S(1)}, u32[]{:S(2)}, u32[]{:S(2)}) collective-permute-start(f32[8,256,128]{2,1,0:T(8,128)S(1)} %all-to-all-done.xm_ref), channel_id=1, source_target_pairs={{0,2},{2,0},{1,3},{3,1},{4,6},{6,4},{5,7},{7,5},{8,10},{10,8},{9,1... | collective-permute-start | bytes 3145736 | tf_op jit(solution)/shard_map/ppermute | solution.py:77
  35.4 4.6 %collective-permute-start.1 = (f32[128,128]{1,0:T(8,128)S(1)}, f32[128,128]{1,0:T(8,128)S(1)}, u32[]{:S(2)}, u32[]{:S(2)}) collective-permute-start(f32[128,128]{1,0:T(8,128)S(1)} %fusion.17), channel_id=1, source_target_pairs={{0,1},{1,0},{2,3},{3,2},{4,5},{5,4},{6,7},{7,6},{8,9},{9,8},{10,11... | collective-permute-start | bytes 196616 | tf_op jit(solution)/shard_map/ppermute | solution.py:16
  37.8 1.0 %copy-start.1 = (f32[8,256,128]{2,1,0:T(8,128)}, f32[8,256,128]{2,1,0:T(8,128)S(1)}, u32[]{:S(2)}) copy-start(f32[8,256,128]{2,1,0:T(8,128)S(1)} %collective-permute-done.xo_ref) | copy-start | bytes 3145732
  57.7 4.8 %collective-permute-start.2 = (f32[6,128]{1,0:T(8,128)}, f32[6,128]{1,0:T(8,128)S(1)}, u32[]{:S(2)}, u32[]{:S(2)}) collective-permute-start(f32[6,128]{1,0:T(8,128)} %get-tuple-element.11), channel_id=1, source_target_pairs={{0,1},{1,0},{2,3},{3,2},{4,5},{5,4},{6,7},{7,6},{8,9},{9,8},{10,11... | collective-permute-start | bytes 9224 | tf_op jit(solution)/shard_map/ppermute | solution.py:16

commit v17 on v15

--- a/solution.py
+++ b/solution.py
@@ -111,13 +111,13 @@
     )(a)
 
 
-def fused_kernel(core_ref, g_ref, pm_ref, po_ref, xm_ref, xo_ref, o_ref, m_ref, a_ref):
+def fused_kernel(core_ref, gc_ref, gb_ref, pm_ref, po_ref, xm_ref, xo_ref, o_ref, m_ref, a_ref):
     o = pl.program_id(0)
-    share = (3 * g_ref.shape[0] // 4) // pl.num_programs(0)
+    share = (3 * gc_ref.shape[0] // 4) // pl.num_programs(0)
 
     @pl.when(o == 0)
     def _():
-        a_ref[...] = g_ref[...]
+        a_ref[...] = gc_ref[...] * gb_ref[...]
         m_ref[...] = jnp.zeros_like(m_ref)
 
     a_ref[...] = sweep_steps(a_ref[...], o * share, share)
@@ -127,14 +127,15 @@
     o_ref[...] = a_ref[...]
 
 
-def fused_half(gram, projected, mine, other, core):
+def fused_half(gram_cell, gram_bin, projected, mine, other, core):
     images, outer, _, rows, rank = projected.shape
-    n = gram.shape[0]
+    n = gram_cell.shape[0]
     p_block = (images, 1, 1, rows, rank)
     grid_spec = pltpu.PrefetchScalarGridSpec(
         num_scalar_prefetch=1,
         grid=(outer,),
         in_specs=[
+            pl.BlockSpec((n, n), lambda o, c: (0, 0)),
             pl.BlockSpec((n, n), lambda o, c: (0, 0)),
             pl.BlockSpec(p_block, lambda o, c: (0, o, c[0], 0, 0)),
             pl.BlockSpec(p_block, lambda o, c: (0, o, 1 - c[0], 0, 0)),
@@ -150,11 +151,11 @@
     return pl.pallas_call(
         fused_kernel,
         out_shape=(
-            jax.ShapeDtypeStruct(gram.shape, jnp.float32),
+            jax.ShapeDtypeStruct(gram_cell.shape, jnp.float32),
             jax.ShapeDtypeStruct((images, rank), jnp.float32),
         ),
         grid_spec=grid_spec,
-    )(core, gram, projected, projected, mine, other)
+    )(core, gram_cell, gram_bin, projected, projected, mine, other)
 
 
 def body(tensor, cell_factor, bin_factor):
@@ -169,12 +170,11 @@
     outer, block_rows = mine.shape[:2]
     blocks = [mine] if other is None else [mine, other]
     gram_cell = sum(gram_of(b.reshape(-1, rank_cols)) for b in blocks)
-    gram = gram_cell * gram_bin
     half = 3 * rank_cols // 4
     projected = projected.reshape(image_rows, outer, len(blocks), block_rows, rank_cols)
     if other is not None and half % outer == 0:
         core = lax.axis_index("cell_core").astype(jnp.int32).reshape(1)
-        partial, mttkrp = fused_half(gram, projected, mine, other, core)
+        partial, mttkrp = fused_half(gram_cell, gram_bin, projected, mine, other, core)
         neg_inv = sweep_rest(partial, half)
     else:
         if other is None:
@@ -185,7 +185,7 @@
             mttkrp = jnp.sum(projected[:, :, 0] * x0[None], axis=(1, 2)) + jnp.sum(
                 projected[:, :, 1] * x1[None], axis=(1, 2)
             )
-        neg_inv = sweep_rest(gram, 0)
+        neg_inv = sweep_rest(gram_cell * gram_bin, 0)
     totals = exchange_sum(mttkrp, "bin")
     own_cols = rank_cols // lax.axis_size("bin")
     own = lax.dynamic_slice_in_dim(neg_inv, lax.axis_index("bin") * own_cols, own_cols, 1)

time: 64.5 us -> 66.5 us (1.031)
  waiting for transfers between devices: 1.97 us -> 3.39 us
    ppermute x2, waiting for transfers between devices: 1.23 us -> 3.02 us  [exchange_sum(): value = value + lax.ppermute(value, axis, pairs)]
    add x0 -> x2, other arithmetic: none -> 1.28 us  [the longest x1 0.64 us: body(): gram_cell = sum((gram_of(b.reshape(-1, rank_cols)) for b in blocks))]
  transfers between devices with their start and end apart: 4 -> 4, of which waited for: 3 -> 2; matrix products, arithmetic and copies ran while one was open for 4% -> 4% of each run, Pallas kernels for 46% -> 45%
where the time goes in v17:
time: 66.5 us; the launch traced here: 66.2 us
  Pallas kernels  44.6 us (67%)
  starting transfers between devices  10.3 us (15%)
  waiting for transfers between devices  3.39 us (5%)
  matrix products  2.91 us (4%)
  other arithmetic  2.5 us (4%)
  local copies, waits for them, and re-layouts  2.33 us (4%)
    pallas_call x1, Pallas kernels, project(): pl.pallas_call(project_kernel, out_shape=jax.ShapeDtypeStruct((rows, rank...  24.3 us
    pallas_call x1, Pallas kernels, fused_half(): pl.pallas_call(fused_kernel, out_shape=(jax.ShapeDtypeStruct(gram_cell.sh...  15.1 us
    all_to_all x1, starting transfers between devices, gather_cells(): mine = lax.all_to_all(spread, 'cell_outer', 0, 0, tiled=True)  7.28 us
    pallas_call x1, Pallas kernels, sweep_rest(): pl.pallas_call(functools.partial(sweep_kernel, first), out_shape=jax.Shap...  5.21 us
    ppermute x2, starting transfers between devices, exchange_sum(): value = value + lax.ppermute(value, axis, pairs)  3.05 us
    ppermute x2, waiting for transfers between devices, exchange_sum(): value = value + lax.ppermute(value, axis, pairs)  3.02 us
    broadcast_in_dim x1, local copies, waits for them, and re-layouts, gather_cells(): spread = jnp.broadcast_to(cell_factor[None], (outer,) + cell_factor.shape)  2.06 us
    dot_general x1, matrix products, body(): return -jnp.dot(totals, own, precision=lax.Precision.HIGHEST)  1.68 us
  transfers between devices with their start and end apart: 4, of which 2 were waited for; matrix products, arithmetic and copies ran while one was open for 4% of the time, Pallas kernels for 45%

profile of v17, /device:TPU:0, one launch (start us, length us, event | category | flops | bytes accessed | tf_op | source)
XLA Modules:
  0.0 66.2 jit_solution(12030457494651790026)
XLA Ops:
  0.0 0.0 copy-start.2
  0.0 2.1 %broadcast_in_dim.2 = f32[8,256,128]{2,1,0:T(8,128)} broadcast(f32[256,128]{1,0:T(8,128)} %param.4), dimensions={1,2} | broadcast | bytes 1179648 | tf_op jit(solution)/shard_map/broadcast_in_dim | solution.py:72
  2.1 7.3 %all-to-all-start = ((f32[8,256,128]{2,1,0:T(8,128)}), f32[8,256,128]{2,1,0:T(8,128)S(1)}, u32[]{:S(2)}, u32[]{:S(2)}) async-start(f32[8,256,128]{2,1,0:T(8,128)} %broadcast_in_dim.2), calls=%async_computation | async-start | bytes 2097152 | tf_op jit(solution)/shard_map/all_to_all | solution.py:73
  9.3 0.0 copy-done.2
  9.4 0.1 fusion.15
  9.4 0.3 fusion.26
  9.7 0.7 %pad_maximum_fusion.b_ref = bf16[512,256]{1,0:T(8,128)(2,1)} fusion(bf16[512,128]{1,0:T(8,128)(2,1)S(1)} %get-tuple-element.18, bf16[512,128]{1,0:T(8,128)(2,1)S(1)} %get-tuple-element.17), kind=kLoop, calls=%fused_computation.21 | loop fusion | flops 524288 | bytes 524288 | tf_op jit(solution)/shard_map/concatenate | solution.py:52
  10.4 24.3 %shard_map.37 = f32[24576,128]{1,0:T(8,128)} custom-call(f32[24576,512]{1,0:T(8,128)} %bitcast.11, bf16[512,256]{1,0:T(8,128)(2,1)} %pad_maximum_fusion.b_ref), custom_call_target="tpu_custom_call" | custom-call | flops 12884901888 | bytes 62914560 | tf_op jit(solution)/shard_map/pallas_call | solution.py:53
  34.7 0.4 all-to-all-done.xm_ref
  35.1 0.0 copy-start
  35.1 0.0 collective-permute-start
  35.1 1.6 %collective-permute-start.1 = (f32[128,128]{1,0:T(8,128)S(1)}, f32[128,128]{1,0:T(8,128)S(1)}, u32[]{:S(2)}, u32[]{:S(2)}) collective-permute-start(f32[128,128]{1,0:T(8,128)S(1)} %fusion.17), channel_id=1, source_target_pairs={{0,1},{1,0},{2,3},{3,2},{4,5},{5,4},{6,7},{7,6},{8,9},{9,8},{10,11... | collective-permute-start | bytes 196616 | tf_op jit(solution)/shard_map/ppermute | solution.py:16
  36.7 3.0 %collective-permute-done.1 = f32[128,128]{1,0:T(8,128)S(1)} collective-permute-done((f32[128,128]{1,0:T(8,128)S(1)}, f32[128,128]{1,0:T(8,128)S(1)}, u32[]{:S(2)}, u32[]{:S(2)}) %collective-permute-start.1) | collective-permute-done | bytes 65568 | tf_op jit(solution)/shard_map/ppermute | solution.py:16
  39.7 0.6 fusion.27.gb_ref
  40.3 0.2 fusion.1
  40.6 0.5 fusion.6
  41.1 0.0 copy-done
  41.1 0.0 collective-permute-done.xo_ref
  41.1 0.0 copy-start.1
  41.1 0.2 fusion.3
  41.3 0.5 fusion.10
  41.8 0.3 copy-done.1
  42.1 0.6 fusion.19.gc_ref
  42.7 15.1 %shard_map.38 = (f32[128,128]{1,0:T(8,128)}, f32[6,128]{1,0:T(8,128)}) custom-call(s32[1]{0:T(128)} %bitcast.core_ref, f32[128,128]{1,0:T(8,128)} %fusion.19.gc_ref, f32[128,128]{1,0:T(8,128)} %fusion.27.gb_ref, f32[6,8,2,256,128]{4,3,2,1,0:T(8,128)} %bitcast.9, f32[6,8,2,256,128]{4,3,2,1,0:T(8,128)} %bitcast.10, f32[8,256,128]{2,1,0:T(8,128)} %copy-done, ...), custom_call_target="tpu_custom_call" | custom-call | tf_op jit(solution)/shard_map/pallas_call | solution.py:151
  57.8 1.5 %collective-permute-start.2 = (f32[6,128]{1,0:T(8,128)}, f32[6,128]{1,0:T(8,128)S(1)}, u32[]{:S(2)}, u32[]{:S(2)}) collective-permute-start(f32[6,128]{1,0:T(8,128)} %get-tuple-element.11), channel_id=1, source_target_pairs={{0,1},{1,0},{2,3},{3,2},{4,5},{5,4},{6,7},{7,6},{8,9},{9,8},{10,11... | collective-permute-start | bytes 9224 | tf_op jit(solution)/shard_map/ppermute | solution.py:16
  59.3 5.2 %shard_map.39 = f32[128,128]{1,0:T(8,128)} custom-call(f32[128,128]{1,0:T(8,128)} %get-tuple-element.12.g_ref), custom_call_target="tpu_custom_call" | custom-call | tf_op jit(solution)/shard_map/pallas_call | solution.py:108
  64.5 0.0 collective-permute-done.2
  64.5 1.7 %convolution_negate_fusion = f32[6,64]{1,0:T(8,128)} fusion(f32[128,128]{1,0:T(8,128)} %shard_map.39, s32[]{:T(128)S(6)} %select_n.3, f32[6,128]{1,0:T(8,128)} %get-tuple-element.11, f32[6,128]{1,0:T(8,128)S(1)} %collective-permute-done.2), kind=kOutput, calls=%fused_computation.6 | convolution fusion | flops 590976 | bytes 73220 | tf_op jit(solution)/shard_map/dot_general | solution.py:192
  (1 shorter events, 0.0 us)
Async XLA Ops:
  0.0 9.4 %copy-start.2 = (f32[512,128]{1,0:T(8,128)S(1)}, f32[512,128]{1,0:T(8,128)}, u32[]{:S(2)}) copy-start(f32[512,128]{1,0:T(8,128)} %param.5) | copy-start | bytes 786436
  2.1 33.0 %all-to-all-start = ((f32[8,256,128]{2,1,0:T(8,128)}), f32[8,256,128]{2,1,0:T(8,128)S(1)}, u32[]{:S(2)}, u32[]{:S(2)}) async-start(f32[8,256,128]{2,1,0:T(8,128)} %broadcast_in_dim.2), calls=%async_computation | async-start | bytes 2097152 | tf_op jit(solution)/shard_map/all_to_all | solution.py:73
  35.1 5.9 %copy-start = (f32[8,256,128]{2,1,0:T(8,128)}, f32[8,256,128]{2,1,0:T(8,128)S(1)}, u32[]{:S(2)}) copy-start(f32[8,256,128]{2,1,0:T(8,128)S(1)} %all-to-all-done.xm_ref) | copy-start | bytes 3145732
  35.1 5.9 %collective-permute-start = (f32[8,256,128]{2,1,0:T(8,128)S(1)}, f32[8,256,128]{2,1,0:T(8,128)S(1)}, u32[]{:S(2)}, u32[]{:S(2)}) collective-permute-start(f32[8,256,128]{2,1,0:T(8,128)S(1)} %all-to-all-done.xm_ref), channel_id=1, source_target_pairs={{0,2},{2,0},{1,3},{3,1},{4,6},{6,4},{5,7},{7,5},{8,10},{10,8},{9,1... | collective-permute-start | bytes 3145736 | tf_op jit(solution)/shard_map/ppermute | solution.py:77
  35.1 4.6 %collective-permute-start.1 = (f32[128,128]{1,0:T(8,128)S(1)}, f32[128,128]{1,0:T(8,128)S(1)}, u32[]{:S(2)}, u32[]{:S(2)}) collective-permute-start(f32[128,128]{1,0:T(8,128)S(1)} %fusion.17), channel_id=1, source_target_pairs={{0,1},{1,0},{2,3},{3,2},{4,5},{5,4},{6,7},{7,6},{8,9},{9,8},{10,11... | collective-permute-start | bytes 196616 | tf_op jit(solution)/shard_map/ppermute | solution.py:16
  41.1 1.0 %copy-start.1 = (f32[8,256,128]{2,1,0:T(8,128)}, f32[8,256,128]{2,1,0:T(8,128)S(1)}, u32[]{:S(2)}) copy-start(f32[8,256,128]{2,1,0:T(8,128)S(1)} %collective-permute-done.xo_ref) | copy-start | bytes 3145732
  57.8 6.7 %collective-permute-start.2 = (f32[6,128]{1,0:T(8,128)}, f32[6,128]{1,0:T(8,128)S(1)}, u32[]{:S(2)}, u32[]{:S(2)}) collective-permute-start(f32[6,128]{1,0:T(8,128)} %get-tuple-element.11), channel_id=1, source_target_pairs={{0,1},{1,0},{2,3},{3,2},{4,5},{5,4},{6,7},{7,6},{8,9},{9,8},{10,11... | collective-permute-start | bytes 9224 | tf_op jit(solution)/shard_map/ppermute | solution.py:16

commit v18 on v15

--- a/solution.py
+++ b/solution.py
@@ -78,7 +78,7 @@
     return mine, other, early
 
 
-def sweep_steps(a, first, count):
+def sweep_steps(a, first, count, unroll=8):
     n = a.shape[0]
     sub = lax.broadcasted_iota(jnp.int32, (n, n), 0)
     lane = lax.broadcasted_iota(jnp.int32, (n, n), 1)
@@ -97,7 +97,7 @@
         upd = jnp.where(on_row, scaled_row, upd)
         return jnp.where(on_row & on_col, -inv, upd)
 
-    return lax.fori_loop(0, count, step, a, unroll=8)
+    return lax.fori_loop(0, count, step, a, unroll=unroll)
 
 
 def sweep_kernel(first, g_ref, o_ref):
@@ -120,7 +120,7 @@
         a_ref[...] = g_ref[...]
         m_ref[...] = jnp.zeros_like(m_ref)
 
-    a_ref[...] = sweep_steps(a_ref[...], o * share, share)
+    a_ref[...] = sweep_steps(a_ref[...], o * share, share, unroll=share)
     m_ref[...] += jnp.sum(pm_ref[:, 0, 0] * xm_ref[...], axis=1) + jnp.sum(
         po_ref[:, 0, 0] * xo_ref[...], axis=1
     )

time: 64.5 us -> 63.7 us (0.988)
  Pallas kernels: 44.6 us -> 43.9 us
    pallas_call x1, Pallas kernels: 15.1 us -> 14.3 us  [fused_half(): pl.pallas_call(fused_kernel, out_shape=(jax.ShapeDtypeStruct(gram.shape,...]
  transfers between devices with their start and end apart: 4 -> 4, of which waited for: 3 -> 3; matrix products, arithmetic and copies ran while one was open for 4% -> 4% of each run, Pallas kernels for 46% -> 47%
where the time goes in v18:
time: 63.7 us; the launch traced here: 63.4 us
  Pallas kernels  43.9 us (69%)
  starting transfers between devices  10.3 us (16%)
  matrix products  2.91 us (5%)
  local copies, waits for them, and re-layouts  2.34 us (4%)
  waiting for transfers between devices  1.97 us (3%)
  other arithmetic  1.88 us (3%)
    pallas_call x1, Pallas kernels, project(): pl.pallas_call(project_kernel, out_shape=jax.ShapeDtypeStruct((rows, rank...  24.3 us
    pallas_call x1, Pallas kernels, fused_half(): pl.pallas_call(fused_kernel, out_shape=(jax.ShapeDtypeStruct(gram.shape,...  14.3 us
    all_to_all x1, starting transfers between devices, gather_cells(): mine = lax.all_to_all(spread, 'cell_outer', 0, 0, tiled=True)  7.28 us
    pallas_call x1, Pallas kernels, sweep_rest(): pl.pallas_call(functools.partial(sweep_kernel, first), out_shape=jax.Shap...  5.21 us
    ppermute x2, starting transfers between devices, exchange_sum(): value = value + lax.ppermute(value, axis, pairs)  3.04 us
    broadcast_in_dim x1, local copies, waits for them, and re-layouts, gather_cells(): spread = jnp.broadcast_to(cell_factor[None], (outer,) + cell_factor.shape)  2.06 us
    dot_general x1, matrix products, body(): return -jnp.dot(totals, own, precision=lax.Precision.HIGHEST)  1.68 us
  transfers between devices with their start and end apart: 4, of which 3 were waited for; matrix products, arithmetic and copies ran while one was open for 4% of the time, Pallas kernels for 47%

profile of v18, /device:TPU:0, one launch (start us, length us, event | category | flops | bytes accessed | tf_op | source)
XLA Modules:
  0.0 63.4 jit_solution(3067324028714566659)
XLA Ops:
  0.0 0.0 copy-start.2
  0.0 2.1 %broadcast_in_dim.2 = f32[8,256,128]{2,1,0:T(8,128)} broadcast(f32[256,128]{1,0:T(8,128)} %param.4), dimensions={1,2} | broadcast | bytes 1179648 | tf_op jit(solution)/shard_map/broadcast_in_dim | solution.py:72
  2.1 7.3 %all-to-all-start = ((f32[8,256,128]{2,1,0:T(8,128)}), f32[8,256,128]{2,1,0:T(8,128)S(1)}, u32[]{:S(2)}, u32[]{:S(2)}) async-start(f32[8,256,128]{2,1,0:T(8,128)} %broadcast_in_dim.2), calls=%async_computation | async-start | bytes 2097152 | tf_op jit(solution)/shard_map/all_to_all | solution.py:73
  9.3 0.0 copy-done.2
  9.4 0.1 fusion.15
  9.4 0.7 %pad_maximum_fusion.b_ref = bf16[512,256]{1,0:T(8,128)(2,1)} fusion(bf16[512,128]{1,0:T(8,128)(2,1)S(1)} %get-tuple-element.18, bf16[512,128]{1,0:T(8,128)(2,1)S(1)} %get-tuple-element.17), kind=kLoop, calls=%fused_computation.21 | loop fusion | flops 524288 | bytes 524288 | tf_op jit(solution)/shard_map/concatenate | solution.py:52
  10.1 24.3 %shard_map.37 = f32[24576,128]{1,0:T(8,128)} custom-call(f32[24576,512]{1,0:T(8,128)} %bitcast.11, bf16[512,256]{1,0:T(8,128)(2,1)} %pad_maximum_fusion.b_ref), custom_call_target="tpu_custom_call" | custom-call | flops 12884901888 | bytes 62914560 | tf_op jit(solution)/shard_map/pallas_call | solution.py:53
  34.5 0.6 %all-to-all-done.xm_ref = f32[8,256,128]{2,1,0:T(8,128)S(1)} async-done(((f32[8,256,128]{2,1,0:T(8,128)}), f32[8,256,128]{2,1,0:T(8,128)S(1)}, u32[]{:S(2)}, u32[]{:S(2)}) %all-to-all-start) | async-done | bytes 1048608 | tf_op jit(solution)/shard_map/all_to_all | solution.py:73
  35.1 0.0 copy-start
  35.1 0.0 collective-permute-start
  35.1 0.3 fusion.27
  35.4 1.6 %collective-permute-start.1 = (f32[128,128]{1,0:T(8,128)S(1)}, f32[128,128]{1,0:T(8,128)S(1)}, u32[]{:S(2)}, u32[]{:S(2)}) collective-permute-start(f32[128,128]{1,0:T(8,128)S(1)} %fusion.17), channel_id=1, source_target_pairs={{0,1},{1,0},{2,3},{3,2},{4,5},{5,4},{6,7},{7,6},{8,9},{9,8},{10,11... | collective-permute-start | bytes 196616 | tf_op jit(solution)/shard_map/ppermute | solution.py:16
  37.0 0.2 fusion.1
  37.2 0.5 fusion.6
  37.7 0.0 copy-done
  37.7 0.1 collective-permute-done.xo_ref
  37.8 0.0 copy-start.1
  37.8 0.2 fusion.3
  38.0 0.5 fusion.10
  38.5 0.3 copy-done.1
  38.8 1.2 %collective-permute-done.1 = f32[128,128]{1,0:T(8,128)S(1)} collective-permute-done((f32[128,128]{1,0:T(8,128)S(1)}, f32[128,128]{1,0:T(8,128)S(1)}, u32[]{:S(2)}, u32[]{:S(2)}) %collective-permute-start.1) | collective-permute-done | bytes 65568 | tf_op jit(solution)/shard_map/ppermute | solution.py:16
  40.0 0.7 %fusion.20.g_ref = f32[128,128]{1,0:T(8,128)} fusion(f32[256,256]{1,0:T(8,128)S(1)} %fusion.10, f32[256,256]{1,0:T(8,128)S(1)} %fusion.6, f32[128,128]{1,0:T(8,128)S(1)} %collective-permute-done.1, f32[256,256]{1,0:T(8,128)S(1)} %fusion.27), kind=kLoop, calls=%fused_computation.28 | loop fusion | flops 196608 | bytes 917504 | tf_op jit(solution)/shard_map/mul | solution.py:172
  40.6 14.3 %shard_map.38 = (f32[128,128]{1,0:T(8,128)}, f32[6,128]{1,0:T(8,128)}) custom-call(s32[1]{0:T(128)} %bitcast.core_ref, f32[128,128]{1,0:T(8,128)} %fusion.20.g_ref, f32[6,8,2,256,128]{4,3,2,1,0:T(8,128)} %bitcast.9, f32[6,8,2,256,128]{4,3,2,1,0:T(8,128)} %bitcast.10, f32[8,256,128]{2,1,0:T(8,128)} %copy-done, f32[8,256,128]{2,1,0:T(8,128)} %copy-done.1), custom_call_target="tpu_custom_call" | custom-call | tf_op jit(solution)/shard_map/pallas_call | solution.py:150
  55.0 1.5 %collective-permute-start.2 = (f32[6,128]{1,0:T(8,128)}, f32[6,128]{1,0:T(8,128)S(1)}, u32[]{:S(2)}, u32[]{:S(2)}) collective-permute-start(f32[6,128]{1,0:T(8,128)} %get-tuple-element.11), channel_id=1, source_target_pairs={{0,1},{1,0},{2,3},{3,2},{4,5},{5,4},{6,7},{7,6},{8,9},{9,8},{10,11... | collective-permute-start | bytes 9224 | tf_op jit(solution)/shard_map/ppermute | solution.py:16
  56.5 5.2 %shard_map.39 = f32[128,128]{1,0:T(8,128)} custom-call(f32[128,128]{1,0:T(8,128)} %get-tuple-element.12.g_ref), custom_call_target="tpu_custom_call" | custom-call | tf_op jit(solution)/shard_map/pallas_call | solution.py:108
  61.7 0.0 collective-permute-done.2
  61.7 1.7 %convolution_negate_fusion = f32[6,64]{1,0:T(8,128)} fusion(f32[128,128]{1,0:T(8,128)} %shard_map.39, s32[]{:T(128)S(6)} %select_n.3, f32[6,128]{1,0:T(8,128)} %get-tuple-element.11, f32[6,128]{1,0:T(8,128)S(1)} %collective-permute-done.2), kind=kOutput, calls=%fused_computation.6 | convolution fusion | flops 590976 | bytes 73220 | tf_op jit(solution)/shard_map/dot_general | solution.py:192
  (1 shorter events, 0.0 us)
Async XLA Ops:
  0.0 9.4 %copy-start.2 = (f32[512,128]{1,0:T(8,128)S(1)}, f32[512,128]{1,0:T(8,128)}, u32[]{:S(2)}) copy-start(f32[512,128]{1,0:T(8,128)} %param.5) | copy-start | bytes 786436
  2.1 33.0 %all-to-all-start = ((f32[8,256,128]{2,1,0:T(8,128)}), f32[8,256,128]{2,1,0:T(8,128)S(1)}, u32[]{:S(2)}, u32[]{:S(2)}) async-start(f32[8,256,128]{2,1,0:T(8,128)} %broadcast_in_dim.2), calls=%async_computation | async-start | bytes 2097152 | tf_op jit(solution)/shard_map/all_to_all | solution.py:73
  35.1 2.6 %copy-start = (f32[8,256,128]{2,1,0:T(8,128)}, f32[8,256,128]{2,1,0:T(8,128)S(1)}, u32[]{:S(2)}) copy-start(f32[8,256,128]{2,1,0:T(8,128)S(1)} %all-to-all-done.xm_ref) | copy-start | bytes 3145732
  35.1 2.7 %collective-permute-start = (f32[8,256,128]{2,1,0:T(8,128)S(1)}, f32[8,256,128]{2,1,0:T(8,128)S(1)}, u32[]{:S(2)}, u32[]{:S(2)}) collective-permute-start(f32[8,256,128]{2,1,0:T(8,128)S(1)} %all-to-all-done.xm_ref), channel_id=1, source_target_pairs={{0,2},{2,0},{1,3},{3,1},{4,6},{6,4},{5,7},{7,5},{8,10},{10,8},{9,1... | collective-permute-start | bytes 3145736 | tf_op jit(solution)/shard_map/ppermute | solution.py:77
  35.4 4.6 %collective-permute-start.1 = (f32[128,128]{1,0:T(8,128)S(1)}, f32[128,128]{1,0:T(8,128)S(1)}, u32[]{:S(2)}, u32[]{:S(2)}) collective-permute-start(f32[128,128]{1,0:T(8,128)S(1)} %fusion.17), channel_id=1, source_target_pairs={{0,1},{1,0},{2,3},{3,2},{4,5},{5,4},{6,7},{7,6},{8,9},{9,8},{10,11... | collective-permute-start | bytes 196616 | tf_op jit(solution)/shard_map/ppermute | solution.py:16
  37.8 1.0 %copy-start.1 = (f32[8,256,128]{2,1,0:T(8,128)}, f32[8,256,128]{2,1,0:T(8,128)S(1)}, u32[]{:S(2)}) copy-start(f32[8,256,128]{2,1,0:T(8,128)S(1)} %collective-permute-done.xo_ref) | copy-start | bytes 3145732
  55.0 6.7 %collective-permute-start.2 = (f32[6,128]{1,0:T(8,128)}, f32[6,128]{1,0:T(8,128)S(1)}, u32[]{:S(2)}, u32[]{:S(2)}) collective-permute-start(f32[6,128]{1,0:T(8,128)} %get-tuple-element.11), channel_id=1, source_target_pairs={{0,1},{1,0},{2,3},{3,2},{4,5},{5,4},{6,7},{7,6},{8,9},{9,8},{10,11... | collective-permute-start | bytes 9224 | tf_op jit(solution)/shard_map/ppermute | solution.py:16

commit v19 on v18

--- a/solution.py
+++ b/solution.py
@@ -101,7 +101,8 @@
 
 
 def sweep_kernel(first, g_ref, o_ref):
-    o_ref[...] = sweep_steps(g_ref[...], first, g_ref.shape[0] - first)
+    count = g_ref.shape[0] - first
+    o_ref[...] = sweep_steps(g_ref[...], first, count, unroll=min(count, 32))
 
 
 def sweep_rest(a, first):

time: 63.7 us -> 63.3 us (level)
  transfers between devices with their start and end apart: 4 -> 4, of which waited for: 3 -> 3; matrix products, arithmetic and copies ran while one was open for 4% -> 4% of each run, Pallas kernels for 47% -> 46%
where the time goes in v19:
time: 63.3 us; the launch traced here: 62.9 us
  Pallas kernels  43.4 us (69%)
  starting transfers between devices  10.3 us (16%)
  matrix products  2.91 us (5%)
  local copies, waits for them, and re-layouts  2.34 us (4%)
  waiting for transfers between devices  1.97 us (3%)
  other arithmetic  1.88 us (3%)
    pallas_call x1, Pallas kernels, project(): pl.pallas_call(project_kernel, out_shape=jax.ShapeDtypeStruct((rows, rank...  24.3 us
    pallas_call x1, Pallas kernels, fused_half(): pl.pallas_call(fused_kernel, out_shape=(jax.ShapeDtypeStruct(gram.shape,...  14.3 us
    all_to_all x1, starting transfers between devices, gather_cells(): mine = lax.all_to_all(spread, 'cell_outer', 0, 0, tiled=True)  7.28 us
    pallas_call x1, Pallas kernels, sweep_rest(): pl.pallas_call(functools.partial(sweep_kernel, first), out_shape=jax.Shap...  4.77 us
    ppermute x2, starting transfers between devices, exchange_sum(): value = value + lax.ppermute(value, axis, pairs)  3.04 us
    broadcast_in_dim x1, local copies, waits for them, and re-layouts, gather_cells(): spread = jnp.broadcast_to(cell_factor[None], (outer,) + cell_factor.shape)  2.06 us
    dot_general x1, matrix products, body(): return -jnp.dot(totals, own, precision=lax.Precision.HIGHEST)  1.68 us
  transfers between devices with their start and end apart: 4, of which 3 were waited for; matrix products, arithmetic and copies ran while one was open for 4% of the time, Pallas kernels for 46%

profile of v19, /device:TPU:0, one launch (start us, length us, event | category | flops | bytes accessed | tf_op | source)
XLA Modules:
  0.0 62.9 jit_solution(8194508334297119322)
XLA Ops:
  0.0 0.0 copy-start.2
  0.0 2.1 %broadcast_in_dim.2 = f32[8,256,128]{2,1,0:T(8,128)} broadcast(f32[256,128]{1,0:T(8,128)} %param.4), dimensions={1,2} | broadcast | bytes 1179648 | tf_op jit(solution)/shard_map/broadcast_in_dim | solution.py:72
  2.1 7.3 %all-to-all-start = ((f32[8,256,128]{2,1,0:T(8,128)}), f32[8,256,128]{2,1,0:T(8,128)S(1)}, u32[]{:S(2)}, u32[]{:S(2)}) async-start(f32[8,256,128]{2,1,0:T(8,128)} %broadcast_in_dim.2), calls=%async_computation | async-start | bytes 2097152 | tf_op jit(solution)/shard_map/all_to_all | solution.py:73
  9.3 0.0 copy-done.2
  9.4 0.1 fusion.15
  9.4 0.7 %pad_maximum_fusion.b_ref = bf16[512,256]{1,0:T(8,128)(2,1)} fusion(bf16[512,128]{1,0:T(8,128)(2,1)S(1)} %get-tuple-element.18, bf16[512,128]{1,0:T(8,128)(2,1)S(1)} %get-tuple-element.17), kind=kLoop, calls=%fused_computation.21 | loop fusion | flops 524288 | bytes 524288 | tf_op jit(solution)/shard_map/concatenate | solution.py:52
  10.1 24.3 %shard_map.37 = f32[24576,128]{1,0:T(8,128)} custom-call(f32[24576,512]{1,0:T(8,128)} %bitcast.11, bf16[512,256]{1,0:T(8,128)(2,1)} %pad_maximum_fusion.b_ref), custom_call_target="tpu_custom_call" | custom-call | flops 12884901888 | bytes 62914560 | tf_op jit(solution)/shard_map/pallas_call | solution.py:53
  34.5 0.6 %all-to-all-done.xm_ref = f32[8,256,128]{2,1,0:T(8,128)S(1)} async-done(((f32[8,256,128]{2,1,0:T(8,128)}), f32[8,256,128]{2,1,0:T(8,128)S(1)}, u32[]{:S(2)}, u32[]{:S(2)}) %all-to-all-start) | async-done | bytes 1048608 | tf_op jit(solution)/shard_map/all_to_all | solution.py:73
  35.1 0.0 copy-start
  35.1 0.0 collective-permute-start
  35.1 0.3 fusion.27
  35.4 1.6 %collective-permute-start.1 = (f32[128,128]{1,0:T(8,128)S(1)}, f32[128,128]{1,0:T(8,128)S(1)}, u32[]{:S(2)}, u32[]{:S(2)}) collective-permute-start(f32[128,128]{1,0:T(8,128)S(1)} %fusion.17), channel_id=1, source_target_pairs={{0,1},{1,0},{2,3},{3,2},{4,5},{5,4},{6,7},{7,6},{8,9},{9,8},{10,11... | collective-permute-start | bytes 196616 | tf_op jit(solution)/shard_map/ppermute | solution.py:16
  37.0 0.2 fusion.1
  37.2 0.5 fusion.6
  37.7 0.0 copy-done
  37.7 0.1 collective-permute-done.xo_ref
  37.8 0.0 copy-start.1
  37.8 0.2 fusion.3
  38.0 0.5 fusion.10
  38.5 0.3 copy-done.1
  38.8 1.2 %collective-permute-done.1 = f32[128,128]{1,0:T(8,128)S(1)} collective-permute-done((f32[128,128]{1,0:T(8,128)S(1)}, f32[128,128]{1,0:T(8,128)S(1)}, u32[]{:S(2)}, u32[]{:S(2)}) %collective-permute-start.1) | collective-permute-done | bytes 65568 | tf_op jit(solution)/shard_map/ppermute | solution.py:16
  40.0 0.7 %fusion.20.g_ref = f32[128,128]{1,0:T(8,128)} fusion(f32[256,256]{1,0:T(8,128)S(1)} %fusion.10, f32[256,256]{1,0:T(8,128)S(1)} %fusion.6, f32[128,128]{1,0:T(8,128)S(1)} %collective-permute-done.1, f32[256,256]{1,0:T(8,128)S(1)} %fusion.27), kind=kLoop, calls=%fused_computation.28 | loop fusion | flops 196608 | bytes 917504 | tf_op jit(solution)/shard_map/mul | solution.py:173
  40.6 14.3 %shard_map.38 = (f32[128,128]{1,0:T(8,128)}, f32[6,128]{1,0:T(8,128)}) custom-call(s32[1]{0:T(128)} %bitcast.core_ref, f32[128,128]{1,0:T(8,128)} %fusion.20.g_ref, f32[6,8,2,256,128]{4,3,2,1,0:T(8,128)} %bitcast.9, f32[6,8,2,256,128]{4,3,2,1,0:T(8,128)} %bitcast.10, f32[8,256,128]{2,1,0:T(8,128)} %copy-done, f32[8,256,128]{2,1,0:T(8,128)} %copy-done.1), custom_call_target="tpu_custom_call" | custom-call | tf_op jit(solution)/shard_map/pallas_call | solution.py:151
  55.0 1.5 %collective-permute-start.2 = (f32[6,128]{1,0:T(8,128)}, f32[6,128]{1,0:T(8,128)S(1)}, u32[]{:S(2)}, u32[]{:S(2)}) collective-permute-start(f32[6,128]{1,0:T(8,128)} %get-tuple-element.11), channel_id=1, source_target_pairs={{0,1},{1,0},{2,3},{3,2},{4,5},{5,4},{6,7},{7,6},{8,9},{9,8},{10,11... | collective-permute-start | bytes 9224 | tf_op jit(solution)/shard_map/ppermute | solution.py:16
  56.5 4.8 %shard_map.39 = f32[128,128]{1,0:T(8,128)} custom-call(f32[128,128]{1,0:T(8,128)} %get-tuple-element.12.g_ref), custom_call_target="tpu_custom_call" | custom-call | tf_op jit(solution)/shard_map/pallas_call | solution.py:109
  61.3 0.0 collective-permute-done.2
  61.3 1.7 %convolution_negate_fusion = f32[6,64]{1,0:T(8,128)} fusion(f32[128,128]{1,0:T(8,128)} %shard_map.39, s32[]{:T(128)S(6)} %select_n.3, f32[6,128]{1,0:T(8,128)} %get-tuple-element.11, f32[6,128]{1,0:T(8,128)S(1)} %collective-permute-done.2), kind=kOutput, calls=%fused_computation.6 | convolution fusion | flops 590976 | bytes 73220 | tf_op jit(solution)/shard_map/dot_general | solution.py:193
  (1 shorter events, 0.0 us)
Async XLA Ops:
  0.0 9.4 %copy-start.2 = (f32[512,128]{1,0:T(8,128)S(1)}, f32[512,128]{1,0:T(8,128)}, u32[]{:S(2)}) copy-start(f32[512,128]{1,0:T(8,128)} %param.5) | copy-start | bytes 786436
  2.1 33.0 %all-to-all-start = ((f32[8,256,128]{2,1,0:T(8,128)}), f32[8,256,128]{2,1,0:T(8,128)S(1)}, u32[]{:S(2)}, u32[]{:S(2)}) async-start(f32[8,256,128]{2,1,0:T(8,128)} %broadcast_in_dim.2), calls=%async_computation | async-start | bytes 2097152 | tf_op jit(solution)/shard_map/all_to_all | solution.py:73
  35.1 2.6 %copy-start = (f32[8,256,128]{2,1,0:T(8,128)}, f32[8,256,128]{2,1,0:T(8,128)S(1)}, u32[]{:S(2)}) copy-start(f32[8,256,128]{2,1,0:T(8,128)S(1)} %all-to-all-done.xm_ref) | copy-start | bytes 3145732
  35.1 2.7 %collective-permute-start = (f32[8,256,128]{2,1,0:T(8,128)S(1)}, f32[8,256,128]{2,1,0:T(8,128)S(1)}, u32[]{:S(2)}, u32[]{:S(2)}) collective-permute-start(f32[8,256,128]{2,1,0:T(8,128)S(1)} %all-to-all-done.xm_ref), channel_id=1, source_target_pairs={{0,2},{2,0},{1,3},{3,1},{4,6},{6,4},{5,7},{7,5},{8,10},{10,8},{9,1... | collective-permute-start | bytes 3145736 | tf_op jit(solution)/shard_map/ppermute | solution.py:77
  35.4 4.6 %collective-permute-start.1 = (f32[128,128]{1,0:T(8,128)S(1)}, f32[128,128]{1,0:T(8,128)S(1)}, u32[]{:S(2)}, u32[]{:S(2)}) collective-permute-start(f32[128,128]{1,0:T(8,128)S(1)} %fusion.17), channel_id=1, source_target_pairs={{0,1},{1,0},{2,3},{3,2},{4,5},{5,4},{6,7},{7,6},{8,9},{9,8},{10,11... | collective-permute-start | bytes 196616 | tf_op jit(solution)/shard_map/ppermute | solution.py:16
  37.8 1.0 %copy-start.1 = (f32[8,256,128]{2,1,0:T(8,128)}, f32[8,256,128]{2,1,0:T(8,128)S(1)}, u32[]{:S(2)}) copy-start(f32[8,256,128]{2,1,0:T(8,128)S(1)} %collective-permute-done.xo_ref) | copy-start | bytes 3145732
  55.0 6.3 %collective-permute-start.2 = (f32[6,128]{1,0:T(8,128)}, f32[6,128]{1,0:T(8,128)S(1)}, u32[]{:S(2)}, u32[]{:S(2)}) collective-permute-start(f32[6,128]{1,0:T(8,128)} %get-tuple-element.11), channel_id=1, source_target_pairs={{0,1},{1,0},{2,3},{3,2},{4,5},{5,4},{6,7},{7,6},{8,9},{9,8},{10,11... | collective-permute-start | bytes 9224 | tf_op jit(solution)/shard_map/ppermute | solution.py:16
